TPU v7x, 256 devices: a whole 4x4x8 slice. The times are simulated.
256 devices in a mesh: seq: 32 (over z, y_lo, core), head: 8 (over x, y_hi).
Axes of the slice: x: 4, y: 4 (y_hi: 2, y_lo: 2; y = y_hi * 2 + y_lo), z: 8, core: 2. Of those that a mesh axis runs over, the one named last changes fastest.
Arguments:
- queries: bfloat16 [32768, 1024], P('seq', 'head'), may hold values from -6 to 6
- keys: bfloat16 [32768, 1024], P('seq', 'head'), may hold values from -6 to 6
- values: bfloat16 [32768, 1024], P('seq', 'head'), may hold values from -6 to 6
- gates: bfloat16 [32768, 1024], P('seq', 'head'), may hold values from -6 to 6
- sessions: int32 [32768], P('seq'), may hold values from 0 to 15, never falling along the last dimension, each value on 1 to 3072 neighbouring positions
- score_bias: float32 [8], P('head'), may hold values from -1 to 1
- grad_out: bfloat16 [32768, 1024], P('seq', 'head'), may hold values from -6 to 6
- w_out: bfloat16 [1024, 1024], P('head'), may hold values from -0.1875 to 0.1875
Outputs:
- grad_queries: float32 [32768, 1024], P('seq', 'head')
- grad_keys: float32 [32768, 1024], P('seq', 'head')
- grad_values: float32 [32768, 1024], P('seq', 'head')
- grad_gates: float32 [32768, 1024], P('seq', 'head')
- grad_w_out: float32 [1024, 1024], P('head', 'seq')
Inputs may be any that keep to these rules, and one draw needn't show every extreme that they name: `sessions`: session numbers never fall from one event to the next; every session number is used, each session has 1 to 3072 events and one has exactly 3072.
All inputs are finite; a program needn't handle non-finite values.
Results may differ from a plain program's by a relative error of at most 0.0042.
Values may be sent and summed in bfloat16 or wider, within the bound.
No kernel may reach another device: no remote copies, remote signals or barrier semaphores. Data moves between devices by JAX's collectives and lax.ppermute only.
A program may use at most 128 MiB of HBM per device.

v0:
```python
import math

import jax
import jax.numpy as jnp
from jax import lax
from jax.sharding import PartitionSpec as P

DH = 128


back_steps = (1, 2, 3)
norm_eps = 1e-05


def shifted(block, axis, distance):
    devices = range(lax.axis_size(axis))
    route = [(i - distance, i) for i in devices if i - distance in devices]
    return lax.ppermute(block, axis, route)


def silu_parts(scores):
    sigma = jax.nn.sigmoid(scores)
    return (scores * sigma, sigma * (1.0 + scores * (1.0 - sigma)))


def per_device(queries, keys, values, gates, sessions, score_bias, grad_out, w_out):
    row_count = queries.shape[0]
    feature_count = queries.shape[1]
    head_count = feature_count // DH
    scale = 1.0 / math.sqrt(DH)
    my_index = lax.axis_index("seq")
    q_heads = queries.reshape(row_count, head_count, DH)
    bias_col = score_bias.reshape(head_count, 1, 1)
    offsets = jnp.arange(row_count, dtype=jnp.int32)
    packed = jnp.stack([keys, values])
    windows = [(packed, sessions)]
    for distance in back_steps:
        windows.append(shifted((packed, sessions), "seq", distance))
    prepared = []
    for distance in range(4):
        key_pack, key_sessions = windows[distance]
        allowed = (sessions[:, None] == key_sessions[None, :]) & (my_index >= distance)
        if distance == 0:
            allowed = allowed & (offsets[None, :] <= offsets[:, None])
        k_heads = key_pack[0].reshape(row_count, head_count, DH)
        v_heads = key_pack[1].reshape(row_count, head_count, DH)
        prepared.append((k_heads, v_heads, allowed))

    def pair_scores(query_heads, k_heads):
        raw = jnp.einsum("ihd,jhd->hij", query_heads, k_heads, preferred_element_type=jnp.float32)
        return raw * scale + bias_col

    attended = jnp.zeros((row_count, head_count, DH), jnp.float32)
    for k_heads, v_heads, allowed in prepared:
        act, deriv = silu_parts(pair_scores(q_heads, k_heads))
        weights = jnp.where(allowed[None], act, 0.0).astype(jnp.bfloat16)
        attended = attended + jnp.einsum(
            "hij,jhd->ihd", weights, v_heads, preferred_element_type=jnp.float32
        )
    centered = attended - jnp.mean(attended, axis=-1, keepdims=True)
    inv_std = lax.rsqrt(jnp.mean(centered * centered, axis=-1, keepdims=True) + norm_eps)
    normed = centered * inv_std
    gate_heads = gates.reshape(row_count, head_count, DH).astype(jnp.float32)
    mixed = (normed * gate_heads).astype(jnp.bfloat16).reshape(row_count, feature_count)
    column_block = lax.all_gather(grad_out, "head", axis=1, tiled=True)
    grad_mixed = lax.dot_general(
        column_block, w_out, (((1,), (1,)), ((), ())), preferred_element_type=jnp.float32
    )
    product = lax.dot_general(
        mixed, column_block, (((0,), (0,)), ((), ())), preferred_element_type=jnp.float32
    )
    weight_rows = product
    grad_mixed, weight_rows = (grad_mixed, weight_rows)
    grad_w_out = lax.psum_scatter(weight_rows, "seq", scatter_dimension=1, tiled=True)
    grad_mixed = grad_mixed.reshape(row_count, head_count, DH)
    grad_gates = (grad_mixed * normed).reshape(row_count, feature_count)
    grad_normed = grad_mixed * gate_heads
    grad_attended = (
        grad_normed
        - jnp.mean(grad_normed, axis=-1, keepdims=True)
        - normed * jnp.mean(grad_normed * normed, axis=-1, keepdims=True)
    ) * inv_std
    grad_attended = grad_attended.astype(jnp.bfloat16)
    grad_queries = jnp.zeros((row_count, head_count, DH), jnp.float32)
    key_terms = []
    for window_index in range(4):
        k_heads, v_heads, allowed = prepared[window_index]
        scores = pair_scores(q_heads, k_heads)
        key_act, key_deriv = silu_parts(scores)
        key_weights = jnp.where(allowed[None], key_act, 0.0).astype(jnp.bfloat16)
        values_term = jnp.einsum(
            "hij,ihd->jhd", key_weights, grad_attended, preferred_element_type=jnp.float32
        )
        grad_weights = jnp.einsum(
            "ihd,jhd->hij", grad_attended, v_heads, preferred_element_type=jnp.float32
        )
        grad_scores = jnp.where(allowed[None], grad_weights * key_deriv * scale, 0.0).astype(
            jnp.bfloat16
        )
        keys_term = jnp.einsum(
            "hij,ihd->jhd", grad_scores, q_heads, preferred_element_type=jnp.float32
        )
        grad_scores, term_pair = (
            grad_scores,
            jnp.stack(
                [
                    keys_term.reshape(row_count, feature_count),
                    values_term.reshape(row_count, feature_count),
                ]
            ),
        )
        key_terms.append(term_pair)
        grad_queries = grad_queries + jnp.einsum(
            "hij,jhd->ihd", grad_scores, k_heads, preferred_element_type=jnp.float32
        )
    summed = key_terms[0]
    for distance in back_steps:
        summed = summed + shifted(key_terms[distance], "seq", -distance)
    return (
        grad_queries.reshape(row_count, feature_count),
        summed[0],
        summed[1],
        grad_gates,
        grad_w_out,
    )


def solution(mesh):
    return jax.shard_map(
        per_device,
        mesh=mesh,
        in_specs=(
            P("seq", "head"),
            P("seq", "head"),
            P("seq", "head"),
            P("seq", "head"),
            P("seq"),
            P("head"),
            P("seq", "head"),
            P("head", None),
        ),
        out_specs=(
            P("seq", "head"),
            P("seq", "head"),
            P("seq", "head"),
            P("seq", "head"),
            P("head", "seq"),
        ),
        check_vma=False,
    )
```

profile of v0, /device:TPU:109, one launch (start us, length us, event | category | flops | bytes accessed | tf_op | source)
XLA Modules:
  0.0 251.1 jit_solution(9258880873134055670)
XLA Ops:
  8.4 4.6 %collective-permute-start.2 = (bf16[2,1024,128]{2,1,0:T(8,128)(2,1)S(1)}, bf16[2,1024,128]{2,1,0:T(8,128)(2,1)S(1)}, u32[]{:S(2)}, u32[]{:S(2)}) collective-permute-start(bf16[2,1024,128]{2,1,0:T(8,128)(2,1)S(1)} %pad_maximum_fusion.3), channel_id=1, source_target_pairs={{0,16},{8,24},{16,32},{24,40},{32,48},{40,56},{48,64},{56,72},{64,... | collective-permute-start | bytes 1572872 | tf_op jit(solution)/shard_map/ppermute | solution.py:18
  13.0 3.5 %collective-permute-start.4 = (bf16[2,1024,128]{2,1,0:T(8,128)(2,1)S(1)}, bf16[2,1024,128]{2,1,0:T(8,128)(2,1)S(1)}, u32[]{:S(2)}, u32[]{:S(2)}) collective-permute-start(bf16[2,1024,128]{2,1,0:T(8,128)(2,1)S(1)} %pad_maximum_fusion.3), channel_id=1, source_target_pairs={{0,24},{8,32},{16,40},{24,48},{32,56},{40,64},{48,72},{56,80},{64,... | collective-permute-start | bytes 1572872 | tf_op jit(solution)/shard_map/ppermute | solution.py:18
  16.5 2.5 %collective-permute-start = (bf16[2,1024,128]{2,1,0:T(8,128)(2,1)S(1)}, bf16[2,1024,128]{2,1,0:T(8,128)(2,1)S(1)}, u32[]{:S(2)}, u32[]{:S(2)}) collective-permute-start(bf16[2,1024,128]{2,1,0:T(8,128)(2,1)S(1)} %pad_maximum_fusion.3), channel_id=1, source_target_pairs={{0,8},{8,16},{16,24},{24,32},{32,40},{40,48},{48,56},{56,64},{64,7... | collective-permute-start | bytes 1572872 | tf_op jit(solution)/shard_map/ppermute | solution.py:18
  19.0 3.0 %collective-permute-start.1 = (s32[1024]{0:T(1024)}, s32[1024]{0:T(1024)S(1)}, u32[]{:S(2)}, u32[]{:S(2)}) collective-permute-start(s32[1024]{0:T(1024)} %param.12), channel_id=1, source_target_pairs={{0,8},{8,16},{16,24},{24,32},{32,40},{40,48},{48,56},{56,64},{64,7... | collective-permute-start | bytes 12296 | tf_op jit(solution)/shard_map/ppermute | solution.py:18
  22.0 2.5 %collective-permute-start.3 = (s32[1024]{0:T(1024)}, s32[1024]{0:T(1024)S(1)}, u32[]{:S(2)}, u32[]{:S(2)}) collective-permute-start(s32[1024]{0:T(1024)} %param.12), channel_id=1, source_target_pairs={{0,16},{8,24},{16,32},{24,40},{32,48},{40,56},{48,64},{56,72},{64,... | collective-permute-start | bytes 12296 | tf_op jit(solution)/shard_map/ppermute | solution.py:18
  28.1 2.9 %collective-permute-start.5 = (s32[1024]{0:T(1024)S(1)}, s32[1024]{0:T(1024)S(1)}, u32[]{:S(2)}, u32[]{:S(2)}) collective-permute-start(s32[1024]{0:T(1024)S(1)} %copy-done.36), channel_id=1, source_target_pairs={{0,24},{8,32},{16,40},{24,48},{32,56},{40,64},{48,72},{56,80},{64,... | collective-permute-start | bytes 12296 | tf_op jit(solution)/shard_map/ppermute | solution.py:18
  31.8 3.5 %collective-permute-done.4 = bf16[2,1024,128]{2,1,0:T(8,128)(2,1)S(1)} collective-permute-done((bf16[2,1024,128]{2,1,0:T(8,128)(2,1)S(1)}, bf16[2,1024,128]{2,1,0:T(8,128)(2,1)S(1)}, u32[]{:S(2)}, u32[]{:S(2)}) %collective-permute-start.4) | collective-permute-done | bytes 524320 | tf_op jit(solution)/shard_map/ppermute | solution.py:18
  35.9 5.8 %collective-permute-done.1 = s32[1024]{0:T(1024)S(1)} collective-permute-done((s32[1024]{0:T(1024)}, s32[1024]{0:T(1024)S(1)}, u32[]{:S(2)}, u32[]{:S(2)}) %collective-permute-start.1) | collective-permute-done | bytes 4128 | tf_op jit(solution)/shard_map/ppermute | solution.py:18
  42.6 10.4 %fusion.26 = (bf16[1024,1024]{1,0:T(8,128)(2,1)S(1)}, bf16[1024,1024]{1,0:T(8,128)(2,1)S(1)}, bf16[1024,1024]{1,0:T(8,128)(2,1)S(1)}, bf16[1024,1024]{1,0:T(8,128)(2,1)S(1)}, f32[1024,1024]{0,1:T(8,128)}) fusion(s32[1024]{0:T(1024)S(1)} %collective-permute-done.1, f32[]{:T(128)} %bitcast.295, pred[]{:T(512)S(6)} %ge.13, s32[1024]{0:T(1024)S(1)} %copy-done.36, ...), kind=kOutput, calls=%fused_computation.35 | convolution fusion | flops 312475648 | bytes 25711620 | tf_op jit(solution)/shard_map/ihd,jhd->hij/dot_general | solution.py:50
  56.7 26.8 %all-gather.2.cloned.1.call-done = bf16[1024,1024]{1,0:T(8,128)(2,1)} async-done(((bf16[1024,128]{1,0:T(8,128)(2,1)}), bf16[1024,1024]{1,0:T(8,128)(2,1)}) %all-gather.2.cloned.1.call-update) | async-done | bytes 2097168 | tf_op jit(solution)/shard_map/all_gather | solution.py:65
  83.5 2.6 %fusion.44 = (f32[1024]{0:T(1024)S(1)}, f32[1024,128]{0,1:T(8,128)S(1)}) fusion(f32[128,1024]{1,0:T(8,128)S(1)} %get-tuple-element.20, f32[1024]{0:T(1024)S(1)} %add_rsqrt_fusion, f32[1024]{0:T(1024)S(1)} %broadcast_multiply_fusion.1, bf16[1024,128]{0,1:T(8,128)(2,1)S(1)} %copy.13, bf16[1024,1024]{1,0:T(8,128)(2,1)} %all-gather.2.cloned.1.call-done, ...), kind=kOutput, calls=%fused_computation.87 | convolution fusion | flops 269220864 | bytes 3682304 | tf_op jit(solution)/shard_map/dot_general | solution.py:66
  94.3 4.4 %fusion.32 = bf16[1024,1024]{1,0:T(8,128)(2,1)S(1)} fusion(f32[1024,1024]{0,1:T(8,128)} %get-tuple-element.18, bf16[1024,128]{0,1:T(8,128)(2,1)S(1)} %get-tuple-element.11, s32[1024]{0:T(1024)S(1)} %collective-permute-done.1, f32[]{:T(128)} %bitcast.293, pred[]{:T(512)S(6)} %ge.13, s32[1024]{0:T(1024)S(1)} %copy-done.36, bf16[2,1024,128]{2,1,0:T(8,128)(2,1)} %copy-done.32), kind=kOutput, calls=%fused_computation.41 | convolution fusion | flops 284164096 | bytes 6824449 | tf_op jit(solution)/shard_map/ihd,jhd->hij/dot_general | solution.py:94
  100.5 3.9 %collective-permute-start.6 = (f32[2,1024,128]{2,1,0:T(8,128)}, f32[2,1024,128]{2,1,0:T(8,128)}, u32[]{:S(2)}, u32[]{:S(2)}) collective-permute-start(f32[2,1024,128]{2,1,0:T(8,128)} %pad_maximum_fusion), channel_id=1, source_target_pairs={{8,0},{16,8},{24,16},{32,24},{40,32},{48,40},{56,48},{64,56},{72,6... | collective-permute-start | bytes 3145736 | tf_op jit(solution)/shard_map/ppermute | solution.py:18
  104.4 3.1 %fusion.21 = bf16[1024,1024]{1,0:T(8,128)(2,1)S(1)} fusion(f32[1024,1024]{0,1:T(8,128)S(1)} %copy-done.17, bf16[1024,128]{0,1:T(8,128)(2,1)S(1)} %get-tuple-element.11, s32[1024]{0:T(1024)S(1)} %collective-permute-done.3, f32[]{:T(128)} %bitcast.297, pred[]{:T(512)S(6)} %ge.14, s32[1024]{0:T(1024)S(1)} %copy-done.36, bf16[2,1024,128]{2,1,0:T(8,128)(2,1)S(1)} %copy-done.29), kind=kOutput, calls=%fused_computation.27 | convolution fusion | flops 284164096 | bytes 6823941 | tf_op jit(solution)/shard_map/ihd,jhd->hij/dot_general | solution.py:94
  109.4 3.2 %collective-permute-start.7 = (f32[2,1024,128]{2,1,0:T(8,128)}, f32[2,1024,128]{2,1,0:T(8,128)}, u32[]{:S(2)}, u32[]{:S(2)}) collective-permute-start(f32[2,1024,128]{2,1,0:T(8,128)} %pad_maximum_fusion.1), channel_id=1, source_target_pairs={{16,0},{24,8},{32,16},{40,24},{48,32},{56,40},{64,48},{72,56},{80,... | collective-permute-start | bytes 3145736 | tf_op jit(solution)/shard_map/ppermute | solution.py:18
  112.6 2.9 %fusion.10 = bf16[1024,1024]{1,0:T(8,128)(2,1)S(1)} fusion(f32[1024,1024]{0,1:T(8,128)S(1)} %copy-done.15, bf16[1024,128]{0,1:T(8,128)(2,1)S(1)} %get-tuple-element.11, s32[1024]{0:T(1024)S(1)} %collective-permute-done.5, f32[]{:T(128)} %bitcast.296, pred[]{:T(512)S(6)} %ge.15, s32[1024]{0:T(1024)S(1)} %copy-done.36, bf16[2,1024,128]{2,1,0:T(8,128)(2,1)S(1)} %copy-done.25), kind=kOutput, calls=%fused_computation.13 | convolution fusion | flops 284164096 | bytes 6823941 | tf_op jit(solution)/shard_map/ihd,jhd->hij/dot_general | solution.py:94
  117.4 2.4 collective-permute-start.8
  119.8 3.5 %select_convert_fusion = bf16[1024,1024]{1,0:T(8,128)(2,1)S(1)} fusion(f32[1024,1024]{1,0:T(8,128)S(1)} %copy-done.13, bf16[1024,128]{0,1:T(8,128)(2,1)S(1)} %get-tuple-element.11, bf16[1024,128]{1,0:T(8,128)(2,1)S(1)} %copy-done.31, f32[]{:T(128)} %bitcast.294, s32[1024]{0:T(1024)S(1)} %copy-done.36, pred[]{:T(512)S(6)} %ge.12), kind=kOutput, calls=%fused_computation.42 | convolution fusion | flops 286261248 | bytes 6819845 | tf_op jit(solution)/shard_map/ihd,jhd->hij/dot_general | solution.py:94
  125.9 2.4 fusion.57
  128.4 2.5 convolution_bitcast_fusion.7
  134.1 5.0 %collective-permute-done.7 = f32[2,1024,128]{2,1,0:T(8,128)} collective-permute-done((f32[2,1024,128]{2,1,0:T(8,128)}, f32[2,1024,128]{2,1,0:T(8,128)}, u32[]{:S(2)}, u32[]{:S(2)}) %collective-permute-start.7) | collective-permute-done | bytes 1048608 | tf_op jit(solution)/shard_map/ppermute | solution.py:18
  139.2 11.9 %collective-permute-done.8 = f32[2,1024,128]{2,1,0:T(8,128)} collective-permute-done((f32[2,1024,128]{2,1,0:T(8,128)}, f32[2,1024,128]{2,1,0:T(8,128)}, u32[]{:S(2)}, u32[]{:S(2)}) %collective-permute-start.8) | collective-permute-done | bytes 1048608 | tf_op jit(solution)/shard_map/ppermute | solution.py:18
  151.1 2.1 fusion.40
  154.2 90.0 %reduce-scatter.2.cloned.1.call-done = f32[128,32]{0,1:T(8,128)} async-done(((f32[128,1024]{0,1:T(8,128)}), f32[128,32]{0,1:T(8,128)}) %reduce-scatter.2.cloned.1.call-update) | async-done | bytes 16400 | tf_op jit(solution)/shard_map/reduce_scatter | solution.py:74
  (115 shorter events, 30.2 us)
Async XLA Ops:
  7.2 19.2 %copy-start = (bf16[1024,128]{1,0:T(8,128)(2,1)S(1)}, bf16[1024,128]{1,0:T(8,128)(2,1)}, u32[]{:S(2)}) copy-start(bf16[1024,128]{1,0:T(8,128)(2,1)} %param.8) | copy-start | bytes 786436
  7.2 20.9 %copy-start.36 = (s32[1024]{0:T(1024)S(1)}, s32[1024]{0:T(1024)}, u32[]{:S(2)}) copy-start(s32[1024]{0:T(1024)} %param.12) | copy-start | bytes 12292
  7.2 76.3 %all-gather.2.cloned.1.call-start = ((), (), s32[]{:S(2)}) async-start(), calls=%async_computation.1 | async-start | bytes 2359296 | tf_op jit(solution)/shard_map/all_gather | solution.py:65
  8.4 19.7 %collective-permute-start.2 = (bf16[2,1024,128]{2,1,0:T(8,128)(2,1)S(1)}, bf16[2,1024,128]{2,1,0:T(8,128)(2,1)S(1)}, u32[]{:S(2)}, u32[]{:S(2)}) collective-permute-start(bf16[2,1024,128]{2,1,0:T(8,128)(2,1)S(1)} %pad_maximum_fusion.3), channel_id=1, source_target_pairs={{0,16},{8,24},{16,32},{24,40},{32,48},{40,56},{48,64},{56,72},{64,... | collective-permute-start | bytes 1572872 | tf_op jit(solution)/shard_map/ppermute | solution.py:18
  13.0 22.2 %collective-permute-start.4 = (bf16[2,1024,128]{2,1,0:T(8,128)(2,1)S(1)}, bf16[2,1024,128]{2,1,0:T(8,128)(2,1)S(1)}, u32[]{:S(2)}, u32[]{:S(2)}) collective-permute-start(bf16[2,1024,128]{2,1,0:T(8,128)(2,1)S(1)} %pad_maximum_fusion.3), channel_id=1, source_target_pairs={{0,24},{8,32},{16,40},{24,48},{32,56},{40,64},{48,72},{56,80},{64,... | collective-permute-start | bytes 1572872 | tf_op jit(solution)/shard_map/ppermute | solution.py:18
  16.5 25.3 %collective-permute-start = (bf16[2,1024,128]{2,1,0:T(8,128)(2,1)S(1)}, bf16[2,1024,128]{2,1,0:T(8,128)(2,1)S(1)}, u32[]{:S(2)}, u32[]{:S(2)}) collective-permute-start(bf16[2,1024,128]{2,1,0:T(8,128)(2,1)S(1)} %pad_maximum_fusion.3), channel_id=1, source_target_pairs={{0,8},{8,16},{16,24},{24,32},{32,40},{40,48},{48,56},{56,64},{64,7... | collective-permute-start | bytes 1572872 | tf_op jit(solution)/shard_map/ppermute | solution.py:18
  19.0 22.7 %collective-permute-start.1 = (s32[1024]{0:T(1024)}, s32[1024]{0:T(1024)S(1)}, u32[]{:S(2)}, u32[]{:S(2)}) collective-permute-start(s32[1024]{0:T(1024)} %param.12), channel_id=1, source_target_pairs={{0,8},{8,16},{16,24},{24,32},{32,40},{40,48},{48,56},{56,64},{64,7... | collective-permute-start | bytes 12296 | tf_op jit(solution)/shard_map/ppermute | solution.py:18
  22.0 19.8 %collective-permute-start.3 = (s32[1024]{0:T(1024)}, s32[1024]{0:T(1024)S(1)}, u32[]{:S(2)}, u32[]{:S(2)}) collective-permute-start(s32[1024]{0:T(1024)} %param.12), channel_id=1, source_target_pairs={{0,16},{8,24},{16,32},{24,40},{32,48},{40,56},{48,64},{56,72},{64,... | collective-permute-start | bytes 12296 | tf_op jit(solution)/shard_map/ppermute | solution.py:18
  24.6 219.6 %reduce-scatter.2.cloned.1.call-start = ((), (), s32[]{:S(2)}) async-start(), calls=%async_computation.2 | async-start | bytes 540672 | tf_op jit(solution)/shard_map/reduce_scatter | solution.py:74
  28.1 14.6 %copy-start.12 = (f32[1024,1024]{1,0:T(8,128)}, f32[1024,1024]{1,0:T(8,128)S(1)}, u32[]{:S(2)}) copy-start(f32[1024,1024]{1,0:T(8,128)S(1)} %fusion.64) | copy-start | bytes 12582916
  28.1 13.7 %copy-start.27 = (bf16[2,1024,128]{2,1,0:T(8,128)(2,1)}, bf16[2,1024,128]{2,1,0:T(8,128)(2,1)S(1)}, u32[]{:S(2)}) copy-start(bf16[2,1024,128]{2,1,0:T(8,128)(2,1)S(1)} %collective-permute-done.2) | copy-start | bytes 1572868
  28.1 13.7 %collective-permute-start.5 = (s32[1024]{0:T(1024)S(1)}, s32[1024]{0:T(1024)S(1)}, u32[]{:S(2)}, u32[]{:S(2)}) collective-permute-start(s32[1024]{0:T(1024)S(1)} %copy-done.36), channel_id=1, source_target_pairs={{0,24},{8,32},{16,40},{24,48},{32,56},{40,64},{48,72},{56,80},{64,... | collective-permute-start | bytes 12296 | tf_op jit(solution)/shard_map/ppermute | solution.py:18
  31.7 21.3 %copy-start.16 = (f32[1024,1024]{0,1:T(8,128)}, f32[1024,1024]{0,1:T(8,128)S(1)}, u32[]{:S(2)}) copy-start(f32[1024,1024]{0,1:T(8,128)S(1)} %fusion.58) | copy-start | bytes 12582916
  35.2 19.5 %copy-start.24 = (bf16[2,1024,128]{2,1,0:T(8,128)(2,1)}, bf16[2,1024,128]{2,1,0:T(8,128)(2,1)S(1)}, u32[]{:S(2)}) copy-start(bf16[2,1024,128]{2,1,0:T(8,128)(2,1)S(1)} %collective-permute-done.4) | copy-start | bytes 1572868
  35.9 17.1 %copy-start.14 = (f32[1024,1024]{0,1:T(8,128)}, f32[1024,1024]{0,1:T(8,128)S(1)}, u32[]{:S(2)}) copy-start(f32[1024,1024]{0,1:T(8,128)S(1)} %fusion.61) | copy-start | bytes 12582916
  42.6 10.4 %copy-start.30 = (bf16[1024,128]{1,0:T(8,128)(2,1)S(1)}, bf16[1024,128]{1,0:T(8,128)(2,1)}, u32[]{:S(2)}) copy-start(bf16[1024,128]{1,0:T(8,128)(2,1)} %param.10) | copy-start | bytes 786436
  42.6 11.3 %copy-start.28 = (bf16[2,1024,128]{2,1,0:T(8,128)(2,1)S(1)}, bf16[2,1024,128]{2,1,0:T(8,128)(2,1)}, u32[]{:S(2)}) copy-start(bf16[2,1024,128]{2,1,0:T(8,128)(2,1)} %copy-done.27) | copy-start | bytes 1572868
  54.8 28.7 %copy-start.35 = (bf16[128,1024]{1,0:T(8,128)(2,1)S(1)}, bf16[128,1024]{1,0:T(8,128)(2,1)}, u32[]{:S(2)}) copy-start(bf16[128,1024]{1,0:T(8,128)(2,1)} %param.15) | copy-start | bytes 786436
  98.6 5.7 %copy-start.17 = (f32[1024,1024]{0,1:T(8,128)S(1)}, f32[1024,1024]{0,1:T(8,128)}, u32[]{:S(2)}) copy-start(f32[1024,1024]{0,1:T(8,128)} %copy-done.16) | copy-start | bytes 12582916
  100.5 33.6 %collective-permute-start.6 = (f32[2,1024,128]{2,1,0:T(8,128)}, f32[2,1024,128]{2,1,0:T(8,128)}, u32[]{:S(2)}, u32[]{:S(2)}) collective-permute-start(f32[2,1024,128]{2,1,0:T(8,128)} %pad_maximum_fusion), channel_id=1, source_target_pairs={{8,0},{16,8},{24,16},{32,24},{40,32},{48,40},{56,48},{64,56},{72,6... | collective-permute-start | bytes 3145736 | tf_op jit(solution)/shard_map/ppermute | solution.py:18
  107.5 8.0 %copy-start.1 = (bf16[1024,1024]{1,0:T(8,128)(2,1)}, bf16[1024,1024]{1,0:T(8,128)(2,1)S(1)}, u32[]{:S(2)}) copy-start(bf16[1024,1024]{1,0:T(8,128)(2,1)S(1)} %fusion.21) | copy-start | bytes 6291460
  109.4 29.8 %collective-permute-start.7 = (f32[2,1024,128]{2,1,0:T(8,128)}, f32[2,1024,128]{2,1,0:T(8,128)}, u32[]{:S(2)}, u32[]{:S(2)}) collective-permute-start(f32[2,1024,128]{2,1,0:T(8,128)} %pad_maximum_fusion.1), channel_id=1, source_target_pairs={{16,0},{24,8},{32,16},{40,24},{48,32},{56,40},{64,48},{72,56},{80,... | collective-permute-start | bytes 3145736 | tf_op jit(solution)/shard_map/ppermute | solution.py:18
  115.5 7.8 %copy-start.2 = (bf16[1024,1024]{1,0:T(8,128)(2,1)}, bf16[1024,1024]{1,0:T(8,128)(2,1)S(1)}, u32[]{:S(2)}) copy-start(bf16[1024,1024]{1,0:T(8,128)(2,1)S(1)} %fusion.10) | copy-start | bytes 6291460
  117.4 33.7 %collective-permute-start.8 = (f32[2,1024,128]{2,1,0:T(8,128)}, f32[2,1024,128]{2,1,0:T(8,128)}, u32[]{:S(2)}, u32[]{:S(2)}) collective-permute-start(f32[2,1024,128]{2,1,0:T(8,128)} %pad_maximum_fusion.2), channel_id=1, source_target_pairs={{24,0},{32,8},{40,16},{48,24},{56,32},{64,40},{72,48},{80,56},{88,... | collective-permute-start | bytes 3145736 | tf_op jit(solution)/shard_map/ppermute | solution.py:18
  (24 other events, 95.5 us)
Sparse Core Ops, SparseCore 0:
  24.7 58.7 all-gather.1
  94.4 149.8 reduce-scatter.1
where the time goes:
time: 251 us
  waiting for transfers between devices  143 us (57%)
  matrix products  52.2 us (21%)
  starting transfers between devices  28.7 us (11%)
  between operations  15.4 us (6%)
  other arithmetic  7.54 us (3%)
  local copies, waits for them, and re-layouts  4.13 us (2%)
    reduce_scatter x1, waiting for transfers between devices, per_device(): lax.psum_scatter(weight_rows, 'seq', scatter_dimension=1, tiled=True)  90 us
    ppermute x9, starting transfers between devices, shifted(): return lax.ppermute(block, axis, route)  28.6 us
    all_gather x1, waiting for transfers between devices, per_device(): column_block = lax.all_gather(grad_out, 'head', axis=1, tiled=True)  26.8 us
    ppermute x9, waiting for transfers between devices, shifted(): return lax.ppermute(block, axis, route)  26.3 us
    dot_general x4, matrix products, per_device(): jnp.einsum('ihd,jhd->hij', grad_attended, v_heads, preferred_element_type...  13.9 us
    dot_general x4, matrix products, pair_scores(): jnp.einsum('ihd,jhd->hij', query_heads, k_heads, preferred_element_type=j...  13.4 us
    dot_general x4, matrix products, per_device(): jnp.einsum('hij,ihd->jhd', key_weights, grad_attended, preferred_element_...  6.23 us
    dot_general x4, matrix products, per_device(): jnp.einsum('hij,jhd->ihd', grad_scores, k_heads, preferred_element_type=j...  6.22 us
  transfers between devices with their start and end apart: 11, of which 6 were waited for; matrix products, arithmetic and copies ran while one was open for 20% of the time, Pallas kernels for 0%

commit v1 on v0

--- a/solution.py
+++ b/solution.py
@@ -16,6 +16,24 @@
     devices = range(lax.axis_size(axis))
     route = [(i - distance, i) for i in devices if i - distance in devices]
     return lax.ppermute(block, axis, route)
+
+
+def halving_scatter(block, axis):
+    count = lax.axis_size(axis)
+    my_index = lax.axis_index(axis)
+    rows, cols = block.shape
+    levels = count.bit_length() - 1
+    current = block.reshape((rows,) + (2,) * levels + (cols // count,))
+    for level in range(levels):
+        bit = 1 << level
+        axis_pos = current.ndim - 2
+        mine = (my_index // bit) % 2
+        low = lax.index_in_dim(current, 0, axis_pos, keepdims=False)
+        high = lax.index_in_dim(current, 1, axis_pos, keepdims=False)
+        keep = jnp.where(mine == 0, low, high)
+        send = jnp.where(mine == 0, high, low)
+        current = keep + lax.ppermute(send, axis, [(i, i ^ bit) for i in range(count)])
+    return current.reshape(rows, cols // count)
 
 
 def silu_parts(scores):
@@ -62,16 +80,28 @@
     normed = centered * inv_std
     gate_heads = gates.reshape(row_count, head_count, DH).astype(jnp.float32)
     mixed = (normed * gate_heads).astype(jnp.bfloat16).reshape(row_count, feature_count)
-    column_block = lax.all_gather(grad_out, "head", axis=1, tiled=True)
+    head_devices = lax.axis_size("head")
+    head_index = lax.axis_index("head")
+    gathered_blocks = [grad_out] + [
+        lax.ppermute(grad_out, "head", [(i, (i + k) % head_devices) for i in range(head_devices)])
+        for k in range(1, head_devices)
+    ]
+    column_block = jnp.concatenate(gathered_blocks, axis=1)
+    block_width = grad_out.shape[1]
+    source_block = (head_index - jnp.arange(head_devices)) % head_devices
+    w_blocks = w_out.reshape(w_out.shape[0], head_devices, block_width)
+    w_in_order = jnp.take(w_blocks, source_block, axis=1).reshape(w_out.shape)
     grad_mixed = lax.dot_general(
-        column_block, w_out, (((1,), (1,)), ((), ())), preferred_element_type=jnp.float32
+        column_block, w_in_order, (((1,), (1,)), ((), ())), preferred_element_type=jnp.float32
     )
     product = lax.dot_general(
         mixed, column_block, (((0,), (0,)), ((), ())), preferred_element_type=jnp.float32
     )
-    weight_rows = product
-    grad_mixed, weight_rows = (grad_mixed, weight_rows)
-    grad_w_out = lax.psum_scatter(weight_rows, "seq", scatter_dimension=1, tiled=True)
+    gather_back = (head_index - jnp.arange(head_devices)) % head_devices
+    weight_rows = jnp.take(
+        product.reshape(product.shape[0], head_devices, block_width), gather_back, axis=1
+    ).reshape(product.shape)
+    grad_w_out = halving_scatter(weight_rows, "seq")
     grad_mixed = grad_mixed.reshape(row_count, head_count, DH)
     grad_gates = (grad_mixed * normed).reshape(row_count, feature_count)
     grad_normed = grad_mixed * gate_heads

time: 251 us -> 191 us (0.76)
  the two profiles are of different devices: /device:TPU:109 before, /device:TPU:18 now
where the time goes in v1:
time: 191 us; the launch traced here: 190 us
  waiting for transfers between devices  58.8 us (31%)
  starting transfers between devices  57.7 us (30%)
  matrix products  51.9 us (27%)
  local copies, waits for them, and re-layouts  11.3 us (6%)
  other arithmetic  8.57 us (4%)
  between operations  2.18 us (1%)
    ppermute x5, waiting for transfers between devices, halving_scatter(): lax.ppermute(send, axis, [(i, i ^ bit) for i in range(count)])  35.3 us
    ppermute x5, starting transfers between devices, halving_scatter(): lax.ppermute(send, axis, [(i, i ^ bit) for i in range(count)])  23.9 us
    ppermute x7, waiting for transfers between devices, per_device(): lax.ppermute(grad_out, 'head', [(i, (i + k) % head_devices) for i in rang...  23.5 us
    ppermute x9, starting transfers between devices, shifted(): return lax.ppermute(block, axis, route)  22.7 us
    dot_general x4, matrix products, pair_scores(): jnp.einsum('ihd,jhd->hij', query_heads, k_heads, preferred_element_type=j...  16.4 us
    dot_general x4, matrix products, per_device(): jnp.einsum('ihd,jhd->hij', grad_attended, v_heads, preferred_element_type...  14.7 us
    ppermute x7, starting transfers between devices, per_device(): lax.ppermute(grad_out, 'head', [(i, (i + k) % head_devices) for i in rang...  11.2 us
    unnamed x50, local copies, waits for them, and re-layouts  5.76 us
  transfers between devices with their start and end apart: 21, of which 8 were waited for; matrix products, arithmetic and copies ran while one was open for 23% of the time, Pallas kernels for 0%

profile of v1, /device:TPU:18, one launch (start us, length us, event | category | flops | bytes accessed | tf_op | source)
XLA Modules:
  0.0 190.4 jit_solution(11694301431256677569)
XLA Ops:
  2.6 4.0 %collective-permute-start.9 = (bf16[2,1024,128]{2,1,0:T(8,128)(2,1)}, bf16[2,1024,128]{2,1,0:T(8,128)(2,1)}, u32[]{:S(2)}, u32[]{:S(2)}) collective-permute-start(bf16[2,1024,128]{2,1,0:T(8,128)(2,1)} %pad_maximum_fusion.3), channel_id=1, source_target_pairs={{0,16},{8,24},{16,32},{24,40},{32,48},{40,56},{48,64},{56,72},{64,... | collective-permute-start | bytes 1572872 | tf_op jit(solution)/shard_map/ppermute | solution.py:18
  6.6 2.4 %collective-permute-start.11 = (bf16[2,1024,128]{2,1,0:T(8,128)(2,1)}, bf16[2,1024,128]{2,1,0:T(8,128)(2,1)S(1)}, u32[]{:S(2)}, u32[]{:S(2)}) collective-permute-start(bf16[2,1024,128]{2,1,0:T(8,128)(2,1)} %pad_maximum_fusion.3), channel_id=1, source_target_pairs={{0,24},{8,32},{16,40},{24,48},{32,56},{40,64},{48,72},{56,80},{64,... | collective-permute-start | bytes 1572872 | tf_op jit(solution)/shard_map/ppermute | solution.py:18
  11.5 3.1 %collective-permute-start.2 = (bf16[1024,128]{1,0:T(8,128)(2,1)}, bf16[1024,128]{1,0:T(8,128)(2,1)}, u32[]{:S(2)}, u32[]{:S(2)}) collective-permute-start(bf16[1024,128]{1,0:T(8,128)(2,1)} %param.14), channel_id=1, source_target_pairs={{0,3},{1,4},{2,5},{3,6},{4,7},{5,0},{6,1},{7,2},{8,11},{9,12},{10,... | collective-permute-start | bytes 786440 | tf_op jit(solution)/shard_map/ppermute | solution.py:86
  14.7 3.6 %fusion.76 = f32[1024,1024]{1,0:T(8,128)} fusion(bf16[1024,128]{1,0:T(8,128)(2,1)S(1)} %copy-done, bf16[1024,128]{1,0:T(8,128)(2,1)} %param.9), kind=kOutput, calls=%fused_computation.169 | convolution fusion | flops 268435456 | bytes 4718592 | tf_op jit(solution)/shard_map/ihd,jhd->hij/dot_general | solution.py:68
  21.8 13.4 %collective-permute-done = bf16[1024,128]{1,0:T(8,128)(2,1)} collective-permute-done((bf16[1024,128]{1,0:T(8,128)(2,1)}, bf16[1024,128]{1,0:T(8,128)(2,1)}, u32[]{:S(2)}, u32[]{:S(2)}) %collective-permute-start) | collective-permute-done | bytes 262176 | tf_op jit(solution)/shard_map/ppermute | solution.py:86
  35.2 2.1 %collective-permute-start.3 = (bf16[1024,128]{1,0:T(8,128)(2,1)}, bf16[1024,128]{1,0:T(8,128)(2,1)S(1)}, u32[]{:S(2)}, u32[]{:S(2)}) collective-permute-start(bf16[1024,128]{1,0:T(8,128)(2,1)} %param.14), channel_id=1, source_target_pairs={{0,4},{1,5},{2,6},{3,7},{4,0},{5,1},{6,2},{7,3},{8,12},{9,13},{10,... | collective-permute-start | bytes 786440 | tf_op jit(solution)/shard_map/ppermute | solution.py:86
  45.8 6.0 %collective-permute-done.4 = bf16[1024,128]{1,0:T(8,128)(2,1)S(1)} collective-permute-done((bf16[1024,128]{1,0:T(8,128)(2,1)}, bf16[1024,128]{1,0:T(8,128)(2,1)S(1)}, u32[]{:S(2)}, u32[]{:S(2)}) %collective-permute-start.4) | collective-permute-done | bytes 262176 | tf_op jit(solution)/shard_map/ppermute | solution.py:86
  51.8 2.1 %collective-permute-start.7 = (bf16[2,1024,128]{2,1,0:T(8,128)(2,1)}, bf16[2,1024,128]{2,1,0:T(8,128)(2,1)}, u32[]{:S(2)}, u32[]{:S(2)}) collective-permute-start(bf16[2,1024,128]{2,1,0:T(8,128)(2,1)} %pad_maximum_fusion.3), channel_id=1, source_target_pairs={{0,8},{8,16},{16,24},{24,32},{32,40},{40,48},{48,56},{56,64},{64,7... | collective-permute-start | bytes 1572872 | tf_op jit(solution)/shard_map/ppermute | solution.py:18
  55.4 2.3 %collective-permute-done.6 = bf16[1024,128]{1,0:T(8,128)(2,1)S(1)} collective-permute-done((bf16[1024,128]{1,0:T(8,128)(2,1)}, bf16[1024,128]{1,0:T(8,128)(2,1)S(1)}, u32[]{:S(2)}, u32[]{:S(2)}) %collective-permute-start.6) | collective-permute-done | bytes 262176 | tf_op jit(solution)/shard_map/ppermute | solution.py:86
  57.6 4.8 %collective-permute-start.12 = (s32[1024]{0:T(1024)S(1)}, s32[1024]{0:T(1024)S(1)}, u32[]{:S(2)}, u32[]{:S(2)}) collective-permute-start(s32[1024]{0:T(1024)S(1)} %copy-done.19), channel_id=1, source_target_pairs={{0,24},{8,32},{16,40},{24,48},{32,56},{40,64},{48,72},{56,80},{64,... | collective-permute-start | bytes 12296 | tf_op jit(solution)/shard_map/ppermute | solution.py:18
  62.6 2.6 %copy.83 = bf16[1024,1024]{1,0:T(8,128)(2,1)} copy(bf16[1024,1024]{0,1:T(8,128)(2,1)S(1)} %bitcast.387) | data formatting | bytes 4194304 | tf_op jit(solution)/shard_map/dot_general | solution.py:97
  65.1 4.3 %collective-permute-start.8 = (s32[1024]{0:T(1024)S(1)}, s32[1024]{0:T(1024)S(1)}, u32[]{:S(2)}, u32[]{:S(2)}) collective-permute-start(s32[1024]{0:T(1024)S(1)} %copy-done.19), channel_id=1, source_target_pairs={{0,8},{8,16},{16,24},{24,32},{32,40},{40,48},{48,56},{56,64},{64,7... | collective-permute-start | bytes 12296 | tf_op jit(solution)/shard_map/ppermute | solution.py:18
  71.9 10.4 %fusion.26 = (bf16[1024,1024]{1,0:T(8,128)(2,1)S(1)}, bf16[1024,1024]{1,0:T(8,128)(2,1)S(1)}, bf16[1024,1024]{1,0:T(8,128)(2,1)S(1)}, bf16[1024,1024]{1,0:T(8,128)(2,1)S(1)}, f32[1024,1024]{0,1:T(8,128)}) fusion(s32[1024]{0:T(1024)S(1)} %collective-permute-done.8, f32[]{:T(128)} %bitcast.384, pred[]{:T(512)S(6)} %ge.26, s32[1024]{0:T(1024)S(1)} %copy-done.19, ...), kind=kOutput, calls=%fused_computation.37 | convolution fusion | flops 312475648 | bytes 25711620 | tf_op jit(solution)/shard_map/ihd,jhd->hij/dot_general | solution.py:68
  96.1 4.4 %fusion.32 = bf16[1024,1024]{1,0:T(8,128)(2,1)S(1)} fusion(f32[1024,1024]{0,1:T(8,128)} %get-tuple-element.28, bf16[1024,128]{0,1:T(8,128)(2,1)S(1)} %get-tuple-element.21, s32[1024]{0:T(1024)S(1)} %collective-permute-done.8, f32[]{:T(128)} %bitcast.382, pred[]{:T(512)S(6)} %ge.26, s32[1024]{0:T(1024)S(1)} %copy-done.19, ...), kind=kOutput, calls=%fused_computation.43 | convolution fusion | flops 284164096 | bytes 6824449 | tf_op jit(solution)/shard_map/ihd,jhd->hij/dot_general | solution.py:124
  103.7 3.9 %fusion.21 = bf16[1024,1024]{1,0:T(8,128)(2,1)S(1)} fusion(f32[1024,1024]{0,1:T(8,128)S(1)} %copy-done.9, bf16[1024,128]{0,1:T(8,128)(2,1)S(1)} %get-tuple-element.21, s32[1024]{0:T(1024)S(1)} %collective-permute-done.10, f32[]{:T(128)} %bitcast.386, pred[]{:T(512)S(6)} %ge.27, s32[1024]{0:T(1024)S(1)} %copy-done.19, ...), kind=kOutput, calls=%fused_computation.29 | convolution fusion | flops 284164096 | bytes 6824449 | tf_op jit(solution)/shard_map/ihd,jhd->hij/dot_general | solution.py:124
  110.7 2.9 %fusion.10 = bf16[1024,1024]{1,0:T(8,128)(2,1)S(1)} fusion(f32[1024,1024]{0,1:T(8,128)S(1)} %copy-done.7, bf16[1024,128]{0,1:T(8,128)(2,1)S(1)} %get-tuple-element.21, s32[1024]{0:T(1024)S(1)} %collective-permute-done.12, f32[]{:T(128)} %bitcast.385, pred[]{:T(512)S(6)} %ge.28, s32[1024]{0:T(1024)S(1)} %copy-done.19, bf16[2,1024,128]{2,1,0:T(8,128)(2,1)S(1)} %copy-done.14), kind=kOutput, calls=%fused_computation.15 | convolution fusion | flops 284164096 | bytes 6823941 | tf_op jit(solution)/shard_map/ihd,jhd->hij/dot_general | solution.py:124
  116.8 3.5 %select_convert_fusion = bf16[1024,1024]{1,0:T(8,128)(2,1)S(1)} fusion(f32[1024,1024]{1,0:T(8,128)S(1)} %copy-done.5, bf16[1024,128]{0,1:T(8,128)(2,1)S(1)} %get-tuple-element.21, bf16[1024,128]{1,0:T(8,128)(2,1)S(1)} %copy-done.16, f32[]{:T(128)} %bitcast.383, s32[1024]{0:T(1024)S(1)} %copy-done.19, pred[]{:T(512)S(6)} %ge.24), kind=kOutput, calls=%fused_computation.44 | convolution fusion | flops 286261248 | bytes 6819845 | tf_op jit(solution)/shard_map/ihd,jhd->hij/dot_general | solution.py:124
  122.8 9.0 %collective-permute-start.17 = (f32[128,2,2,2,32]{0,4,3,2,1:T(8,128)S(1)}, f32[128,2,2,2,32]{0,4,3,2,1:T(8,128)S(1)}, u32[]{:S(2)}, u32[]{:S(2)}) collective-permute-start(f32[128,2,2,2,32]{0,4,3,2,1:T(8,128)S(1)} %select_bitcast_fusion.1), channel_id=1, source_target_pairs={{0,16},{8,24},{16,0},{24,8},{32,48},{40,56},{48,32},{56,40},{64,80... | collective-permute-start | bytes 393224 | tf_op jit(solution)/shard_map/ppermute | solution.py:35
  132.4 23.7 %collective-permute-done.17 = f32[128,2,2,2,32]{0,4,3,2,1:T(8,128)S(1)} collective-permute-done((f32[128,2,2,2,32]{0,4,3,2,1:T(8,128)S(1)}, f32[128,2,2,2,32]{0,4,3,2,1:T(8,128)S(1)}, u32[]{:S(2)}, u32[]{:S(2)}) %collective-permute-start.17) | collective-permute-done | bytes 131104 | tf_op jit(solution)/shard_map/ppermute | solution.py:35
  156.2 3.6 %collective-permute-start.18 = (f32[128,2,2,32]{0,3,2,1:T(8,128)S(1)}, f32[128,2,2,32]{0,3,2,1:T(8,128)S(1)}, u32[]{:S(2)}, u32[]{:S(2)}) collective-permute-start(f32[128,2,2,32]{0,3,2,1:T(8,128)S(1)} %select_bitcast_fusion.2), channel_id=1, source_target_pairs={{0,32},{8,40},{16,48},{24,56},{32,0},{40,8},{48,16},{56,24},{64,96... | collective-permute-start | bytes 196616 | tf_op jit(solution)/shard_map/ppermute | solution.py:35
  159.8 2.5 %fusion.36 = f32[1024,128]{1,0:T(8,128)} fusion(f32[128,1024]{0,1:T(8,128)S(1)} %fusion.62, f32[128,1024]{0,1:T(8,128)S(1)} %fusion.59, f32[128,1024]{0,1:T(8,128)S(1)} %convolution_bitcast_fusion.8, bf16[1024,1024]{1,0:T(8,128)(2,1)S(1)} %fusion.32, bf16[2,1024,128]{2,1,0:T(8,128)(2,1)} %collective-permute-done.7), kind=kOutput, calls=%fused_computation.69 | convolution fusion | flops 268828672 | bytes 4456448 | tf_op jit(solution)/shard_map/hij,jhd->ihd/dot_general | solution.py:143
  162.3 10.0 %collective-permute-done.18 = f32[128,2,2,32]{0,3,2,1:T(8,128)S(1)} collective-permute-done((f32[128,2,2,32]{0,3,2,1:T(8,128)S(1)}, f32[128,2,2,32]{0,3,2,1:T(8,128)S(1)}, u32[]{:S(2)}, u32[]{:S(2)}) %collective-permute-start.18) | collective-permute-done | bytes 65568 | tf_op jit(solution)/shard_map/ppermute | solution.py:35
  172.3 4.9 %collective-permute-start.19 = (f32[128,2,32]{0,2,1:T(8,128)S(1)}, f32[128,2,32]{0,2,1:T(8,128)S(1)}, u32[]{:S(2)}, u32[]{:S(2)}) collective-permute-start(f32[128,2,32]{0,2,1:T(8,128)S(1)} %select_bitcast_fusion.3), channel_id=1, source_target_pairs={{0,64},{8,72},{16,80},{24,88},{32,96},{40,104},{48,112},{56,120},{... | collective-permute-start | bytes 98312 | tf_op jit(solution)/shard_map/ppermute | solution.py:35
  179.1 5.3 %collective-permute-start.20 = (f32[128,32]{0,1:T(8,128)S(1)}, f32[128,32]{0,1:T(8,128)S(1)}, u32[]{:S(2)}, u32[]{:S(2)}) collective-permute-start(f32[128,32]{0,1:T(8,128)S(1)} %select_bitcast_fusion.4), channel_id=1, source_target_pairs={{0,128},{8,136},{16,144},{24,152},{32,160},{40,168},{48,176},{56,1... | collective-permute-start | bytes 49160 | tf_op jit(solution)/shard_map/ppermute | solution.py:35
  (130 shorter events, 53.6 us)
Async XLA Ops:
  0.7 19.1 %copy-start.18 = (bf16[1024,128]{1,0:T(8,128)(2,1)S(1)}, bf16[1024,128]{1,0:T(8,128)(2,1)}, u32[]{:S(2)}) copy-start(bf16[1024,128]{1,0:T(8,128)(2,1)} %param.14) | copy-start | bytes 786436
  2.6 62.5 %collective-permute-start.9 = (bf16[2,1024,128]{2,1,0:T(8,128)(2,1)}, bf16[2,1024,128]{2,1,0:T(8,128)(2,1)}, u32[]{:S(2)}, u32[]{:S(2)}) collective-permute-start(bf16[2,1024,128]{2,1,0:T(8,128)(2,1)} %pad_maximum_fusion.3), channel_id=1, source_target_pairs={{0,16},{8,24},{16,32},{24,40},{32,48},{40,56},{48,64},{56,72},{64,... | collective-permute-start | bytes 1572872 | tf_op jit(solution)/shard_map/ppermute | solution.py:18
  6.6 64.5 %collective-permute-start.11 = (bf16[2,1024,128]{2,1,0:T(8,128)(2,1)}, bf16[2,1024,128]{2,1,0:T(8,128)(2,1)S(1)}, u32[]{:S(2)}, u32[]{:S(2)}) collective-permute-start(bf16[2,1024,128]{2,1,0:T(8,128)(2,1)} %pad_maximum_fusion.3), channel_id=1, source_target_pairs={{0,24},{8,32},{16,40},{24,48},{32,56},{40,64},{48,72},{56,80},{64,... | collective-permute-start | bytes 1572872 | tf_op jit(solution)/shard_map/ppermute | solution.py:18
  9.0 26.2 %collective-permute-start = (bf16[1024,128]{1,0:T(8,128)(2,1)}, bf16[1024,128]{1,0:T(8,128)(2,1)}, u32[]{:S(2)}, u32[]{:S(2)}) collective-permute-start(bf16[1024,128]{1,0:T(8,128)(2,1)} %param.14), channel_id=1, source_target_pairs={{0,1},{1,2},{2,3},{3,4},{4,5},{5,6},{6,7},{7,0},{8,9},{9,10},{10,1... | collective-permute-start | bytes 786440 | tf_op jit(solution)/shard_map/ppermute | solution.py:86
  10.3 28.0 %collective-permute-start.1 = (bf16[1024,128]{1,0:T(8,128)(2,1)}, bf16[1024,128]{1,0:T(8,128)(2,1)}, u32[]{:S(2)}, u32[]{:S(2)}) collective-permute-start(bf16[1024,128]{1,0:T(8,128)(2,1)} %param.14), channel_id=1, source_target_pairs={{0,2},{1,3},{2,4},{3,5},{4,6},{5,7},{6,0},{7,1},{8,10},{9,11},{10,... | collective-permute-start | bytes 786440 | tf_op jit(solution)/shard_map/ppermute | solution.py:86
  11.5 28.4 %collective-permute-start.2 = (bf16[1024,128]{1,0:T(8,128)(2,1)}, bf16[1024,128]{1,0:T(8,128)(2,1)}, u32[]{:S(2)}, u32[]{:S(2)}) collective-permute-start(bf16[1024,128]{1,0:T(8,128)(2,1)} %param.14), channel_id=1, source_target_pairs={{0,3},{1,4},{2,5},{3,6},{4,7},{5,0},{6,1},{7,2},{8,11},{9,12},{10,... | collective-permute-start | bytes 786440 | tf_op jit(solution)/shard_map/ppermute | solution.py:86
  18.3 35.7 %copy-start.19 = (s32[1024]{0:T(1024)S(1)}, s32[1024]{0:T(1024)}, u32[]{:S(2)}) copy-start(s32[1024]{0:T(1024)} %param.12) | copy-start | bytes 12292
  35.2 8.8 %collective-permute-start.3 = (bf16[1024,128]{1,0:T(8,128)(2,1)}, bf16[1024,128]{1,0:T(8,128)(2,1)S(1)}, u32[]{:S(2)}, u32[]{:S(2)}) collective-permute-start(bf16[1024,128]{1,0:T(8,128)(2,1)} %param.14), channel_id=1, source_target_pairs={{0,4},{1,5},{2,6},{3,7},{4,0},{5,1},{6,2},{7,3},{8,12},{9,13},{10,... | collective-permute-start | bytes 786440 | tf_op jit(solution)/shard_map/ppermute | solution.py:86
  38.4 13.4 %collective-permute-start.4 = (bf16[1024,128]{1,0:T(8,128)(2,1)}, bf16[1024,128]{1,0:T(8,128)(2,1)S(1)}, u32[]{:S(2)}, u32[]{:S(2)}) collective-permute-start(bf16[1024,128]{1,0:T(8,128)(2,1)} %param.14), channel_id=1, source_target_pairs={{0,5},{1,6},{2,7},{3,0},{4,1},{5,2},{6,3},{7,4},{8,13},{9,14},{10,... | collective-permute-start | bytes 786440 | tf_op jit(solution)/shard_map/ppermute | solution.py:86
  39.9 14.0 %collective-permute-start.5 = (bf16[1024,128]{1,0:T(8,128)(2,1)}, bf16[1024,128]{1,0:T(8,128)(2,1)S(1)}, u32[]{:S(2)}, u32[]{:S(2)}) collective-permute-start(bf16[1024,128]{1,0:T(8,128)(2,1)} %param.14), channel_id=1, source_target_pairs={{0,6},{1,7},{2,0},{3,1},{4,2},{5,3},{6,4},{7,5},{8,14},{9,15},{10,... | collective-permute-start | bytes 786440 | tf_op jit(solution)/shard_map/ppermute | solution.py:86
  44.0 13.6 %collective-permute-start.6 = (bf16[1024,128]{1,0:T(8,128)(2,1)}, bf16[1024,128]{1,0:T(8,128)(2,1)S(1)}, u32[]{:S(2)}, u32[]{:S(2)}) collective-permute-start(bf16[1024,128]{1,0:T(8,128)(2,1)} %param.14), channel_id=1, source_target_pairs={{0,7},{1,0},{2,1},{3,2},{4,3},{5,4},{6,5},{7,6},{8,15},{9,8},{10,9... | collective-permute-start | bytes 786440 | tf_op jit(solution)/shard_map/ppermute | solution.py:86
  51.8 20.1 %collective-permute-start.7 = (bf16[2,1024,128]{2,1,0:T(8,128)(2,1)}, bf16[2,1024,128]{2,1,0:T(8,128)(2,1)}, u32[]{:S(2)}, u32[]{:S(2)}) collective-permute-start(bf16[2,1024,128]{2,1,0:T(8,128)(2,1)} %pad_maximum_fusion.3), channel_id=1, source_target_pairs={{0,8},{8,16},{16,24},{24,32},{32,40},{40,48},{48,56},{56,64},{64,7... | collective-permute-start | bytes 1572872 | tf_op jit(solution)/shard_map/ppermute | solution.py:18
  54.0 17.8 %collective-permute-start.10 = (s32[1024]{0:T(1024)S(1)}, s32[1024]{0:T(1024)S(1)}, u32[]{:S(2)}, u32[]{:S(2)}) collective-permute-start(s32[1024]{0:T(1024)S(1)} %copy-done.19), channel_id=1, source_target_pairs={{0,16},{8,24},{16,32},{24,40},{32,48},{40,56},{48,64},{56,72},{64,... | collective-permute-start | bytes 12296 | tf_op jit(solution)/shard_map/ppermute | solution.py:18
  57.6 14.2 %collective-permute-start.12 = (s32[1024]{0:T(1024)S(1)}, s32[1024]{0:T(1024)S(1)}, u32[]{:S(2)}, u32[]{:S(2)}) collective-permute-start(s32[1024]{0:T(1024)S(1)} %copy-done.19), channel_id=1, source_target_pairs={{0,24},{8,32},{16,40},{24,48},{32,56},{40,64},{48,72},{56,80},{64,... | collective-permute-start | bytes 12296 | tf_op jit(solution)/shard_map/ppermute | solution.py:18
  65.1 6.7 %collective-permute-start.8 = (s32[1024]{0:T(1024)S(1)}, s32[1024]{0:T(1024)S(1)}, u32[]{:S(2)}, u32[]{:S(2)}) collective-permute-start(s32[1024]{0:T(1024)S(1)} %copy-done.19), channel_id=1, source_target_pairs={{0,8},{8,16},{16,24},{24,32},{32,40},{40,48},{48,56},{56,64},{64,7... | collective-permute-start | bytes 12296 | tf_op jit(solution)/shard_map/ppermute | solution.py:18
  95.0 27.6 %collective-permute-start.16 = (f32[128,2,2,2,2,32]{0,5,4,3,2,1:T(8,128)S(1)}, f32[128,2,2,2,2,32]{0,5,4,3,2,1:T(8,128)S(1)}, u32[]{:S(2)}, u32[]{:S(2)}) collective-permute-start(f32[128,2,2,2,2,32]{0,5,4,3,2,1:T(8,128)S(1)} %select_bitcast_fusion), channel_id=1, source_target_pairs={{0,8},{8,0},{16,24},{24,16},{32,40},{40,32},{48,56},{56,48},{64,72... | collective-permute-start | bytes 786440 | tf_op jit(solution)/shard_map/ppermute | solution.py:35
  102.4 85.1 %collective-permute-start.13 = (f32[2,1024,128]{2,1,0:T(8,128)}, f32[2,1024,128]{2,1,0:T(8,128)}, u32[]{:S(2)}, u32[]{:S(2)}) collective-permute-start(f32[2,1024,128]{2,1,0:T(8,128)} %pad_maximum_fusion), channel_id=1, source_target_pairs={{8,0},{16,8},{24,16},{32,24},{40,32},{48,40},{56,48},{64,56},{72,6... | collective-permute-start | bytes 3145736 | tf_op jit(solution)/shard_map/ppermute | solution.py:18
  109.4 78.1 %collective-permute-start.14 = (f32[2,1024,128]{2,1,0:T(8,128)}, f32[2,1024,128]{2,1,0:T(8,128)}, u32[]{:S(2)}, u32[]{:S(2)}) collective-permute-start(f32[2,1024,128]{2,1,0:T(8,128)} %pad_maximum_fusion.1), channel_id=1, source_target_pairs={{16,0},{24,8},{32,16},{40,24},{48,32},{56,40},{64,48},{72,56},{80,... | collective-permute-start | bytes 3145736 | tf_op jit(solution)/shard_map/ppermute | solution.py:18
  115.5 72.0 %collective-permute-start.15 = (f32[2,1024,128]{2,1,0:T(8,128)}, f32[2,1024,128]{2,1,0:T(8,128)S(1)}, u32[]{:S(2)}, u32[]{:S(2)}) collective-permute-start(f32[2,1024,128]{2,1,0:T(8,128)} %pad_maximum_fusion.2), channel_id=1, source_target_pairs={{24,0},{32,8},{40,16},{48,24},{56,32},{64,40},{72,48},{80,56},{88,... | collective-permute-start | bytes 3145736 | tf_op jit(solution)/shard_map/ppermute | solution.py:18
  122.8 33.3 %collective-permute-start.17 = (f32[128,2,2,2,32]{0,4,3,2,1:T(8,128)S(1)}, f32[128,2,2,2,32]{0,4,3,2,1:T(8,128)S(1)}, u32[]{:S(2)}, u32[]{:S(2)}) collective-permute-start(f32[128,2,2,2,32]{0,4,3,2,1:T(8,128)S(1)} %select_bitcast_fusion.1), channel_id=1, source_target_pairs={{0,16},{8,24},{16,0},{24,8},{32,48},{40,56},{48,32},{56,40},{64,80... | collective-permute-start | bytes 393224 | tf_op jit(solution)/shard_map/ppermute | solution.py:35
  156.2 28.3 %copy-start.2 = (bf16[1024,1024]{1,0:T(8,128)(2,1)S(1)}, bf16[1024,1024]{1,0:T(8,128)(2,1)}, u32[]{:S(2)}) copy-start(bf16[1024,1024]{1,0:T(8,128)(2,1)} %copy-done.1) | copy-start | bytes 6291460
  156.2 16.1 %collective-permute-start.18 = (f32[128,2,2,32]{0,3,2,1:T(8,128)S(1)}, f32[128,2,2,32]{0,3,2,1:T(8,128)S(1)}, u32[]{:S(2)}, u32[]{:S(2)}) collective-permute-start(f32[128,2,2,32]{0,3,2,1:T(8,128)S(1)} %select_bitcast_fusion.2), channel_id=1, source_target_pairs={{0,32},{8,40},{16,48},{24,56},{32,0},{40,8},{48,16},{56,24},{64,96... | collective-permute-start | bytes 196616 | tf_op jit(solution)/shard_map/ppermute | solution.py:35
  172.3 6.8 %collective-permute-start.19 = (f32[128,2,32]{0,2,1:T(8,128)S(1)}, f32[128,2,32]{0,2,1:T(8,128)S(1)}, u32[]{:S(2)}, u32[]{:S(2)}) collective-permute-start(f32[128,2,32]{0,2,1:T(8,128)S(1)} %select_bitcast_fusion.3), channel_id=1, source_target_pairs={{0,64},{8,72},{16,80},{24,88},{32,96},{40,104},{48,112},{56,120},{... | collective-permute-start | bytes 98312 | tf_op jit(solution)/shard_map/ppermute | solution.py:35
  179.1 7.7 %collective-permute-start.20 = (f32[128,32]{0,1:T(8,128)S(1)}, f32[128,32]{0,1:T(8,128)S(1)}, u32[]{:S(2)}, u32[]{:S(2)}) collective-permute-start(f32[128,32]{0,1:T(8,128)S(1)} %select_bitcast_fusion.4), channel_id=1, source_target_pairs={{0,128},{8,136},{16,144},{24,152},{32,160},{40,168},{48,176},{56,1... | collective-permute-start | bytes 49160 | tf_op jit(solution)/shard_map/ppermute | solution.py:35
  (17 other events, 121.2 us)

commit v2 on v1

--- a/solution.py
+++ b/solution.py
@@ -50,18 +50,23 @@
     q_heads = queries.reshape(row_count, head_count, DH)
     bias_col = score_bias.reshape(head_count, 1, 1)
     offsets = jnp.arange(row_count, dtype=jnp.int32)
-    packed = jnp.stack([keys, values])
-    windows = [(packed, sessions)]
+    session_rows = sessions.astype(jnp.bfloat16).reshape(-1, feature_count)
+    packed = jnp.concatenate([keys, values, session_rows], axis=0)
+    windows = [packed]
     for distance in back_steps:
-        windows.append(shifted((packed, sessions), "seq", distance))
+        windows.append(shifted(packed, "seq", distance))
     prepared = []
     for distance in range(4):
-        key_pack, key_sessions = windows[distance]
+        key_pack = windows[distance]
+        if distance == 0:
+            key_sessions = sessions
+        else:
+            key_sessions = key_pack[2 * row_count :].reshape(-1)[:row_count].astype(jnp.int32)
         allowed = (sessions[:, None] == key_sessions[None, :]) & (my_index >= distance)
         if distance == 0:
             allowed = allowed & (offsets[None, :] <= offsets[:, None])
-        k_heads = key_pack[0].reshape(row_count, head_count, DH)
-        v_heads = key_pack[1].reshape(row_count, head_count, DH)
+        k_heads = key_pack[:row_count].reshape(row_count, head_count, DH)
+        v_heads = key_pack[row_count : 2 * row_count].reshape(row_count, head_count, DH)
         prepared.append((k_heads, v_heads, allowed))
 
     def pair_scores(query_heads, k_heads):
@@ -145,7 +150,8 @@
         )
     summed = key_terms[0]
     for distance in back_steps:
-        summed = summed + shifted(key_terms[distance], "seq", -distance)
+        sent = shifted(key_terms[distance].astype(jnp.bfloat16), "seq", -distance)
+        summed = summed + sent.astype(jnp.float32)
     return (
         grad_queries.reshape(row_count, feature_count),
         summed[0],

time: 191 us -> 182 us (0.953)
  the two profiles are of different devices: /device:TPU:18 before, /device:TPU:50 now
where the time goes in v2:
time: 182 us; the launch traced here: 181 us
  waiting for transfers between devices  53.3 us (29%)
  matrix products  50.8 us (28%)
  starting transfers between devices  43.7 us (24%)
  local copies, waits for them, and re-layouts  17.8 us (10%)
  other arithmetic  13.2 us (7%)
  between operations  2.18 us (1%)
    ppermute x7, waiting for transfers between devices, per_device(): lax.ppermute(grad_out, 'head', [(i, (i + k) % head_devices) for i in rang...  29 us
    ppermute x5, waiting for transfers between devices, halving_scatter(): lax.ppermute(send, axis, [(i, i ^ bit) for i in range(count)])  24.2 us
    ppermute x6, starting transfers between devices, shifted(): return lax.ppermute(block, axis, route)  17.8 us
    dot_general x4, matrix products, pair_scores(): jnp.einsum('ihd,jhd->hij', query_heads, k_heads, preferred_element_type=j...  16.5 us
    ppermute x5, starting transfers between devices, halving_scatter(): lax.ppermute(send, axis, [(i, i ^ bit) for i in range(count)])  16.4 us
    dot_general x4, matrix products, per_device(): jnp.einsum('ihd,jhd->hij', grad_attended, v_heads, preferred_element_type...  14 us
    ppermute x7, starting transfers between devices, per_device(): lax.ppermute(grad_out, 'head', [(i, (i + k) % head_devices) for i in rang...  9.48 us
    unnamed x62, local copies, waits for them, and re-layouts  8.58 us
  transfers between devices with their start and end apart: 18, of which 8 were waited for; matrix products, arithmetic and copies ran while one was open for 27% of the time, Pallas kernels for 0%

profile of v2, /device:TPU:50, one launch (start us, length us, event | category | flops | bytes accessed | tf_op | source)
XLA Modules:
  0.0 181.0 jit_solution(6641136673058947968)
XLA Ops:
  3.4 2.6 %collective-permute-start.9 = (bf16[2056,128]{1,0:T(8,128)(2,1)}, bf16[2056,128]{1,0:T(8,128)(2,1)S(1)}, u32[]{:S(2)}, u32[]{:S(2)}) collective-permute-start(bf16[2056,128]{1,0:T(8,128)(2,1)} %pad_maximum_fusion), channel_id=1, source_target_pairs={{0,24},{8,32},{16,40},{24,48},{32,56},{40,64},{48,72},{56,80},{64,... | collective-permute-start | bytes 1579016 | tf_op jit(solution)/shard_map/ppermute | solution.py:18
  6.0 4.0 %collective-permute-start.8 = (bf16[2056,128]{1,0:T(8,128)(2,1)}, bf16[2056,128]{1,0:T(8,128)(2,1)}, u32[]{:S(2)}, u32[]{:S(2)}) collective-permute-start(bf16[2056,128]{1,0:T(8,128)(2,1)} %pad_maximum_fusion), channel_id=1, source_target_pairs={{0,16},{8,24},{16,32},{24,40},{32,48},{40,56},{48,64},{56,72},{64,... | collective-permute-start | bytes 1579016 | tf_op jit(solution)/shard_map/ppermute | solution.py:18
  12.5 3.1 %collective-permute-start.2 = (bf16[1024,128]{1,0:T(8,128)(2,1)}, bf16[1024,128]{1,0:T(8,128)(2,1)}, u32[]{:S(2)}, u32[]{:S(2)}) collective-permute-start(bf16[1024,128]{1,0:T(8,128)(2,1)} %param.14), channel_id=1, source_target_pairs={{0,3},{1,4},{2,5},{3,6},{4,7},{5,0},{6,1},{7,2},{8,11},{9,12},{10,... | collective-permute-start | bytes 786440 | tf_op jit(solution)/shard_map/ppermute | solution.py:91
  15.7 3.6 %fusion.97 = f32[1024,1024]{1,0:T(8,128)} fusion(bf16[1024,128]{1,0:T(8,128)(2,1)S(1)} %copy-done, bf16[1024,128]{1,0:T(8,128)(2,1)} %param.9), kind=kOutput, calls=%fused_computation.188 | convolution fusion | flops 268435456 | bytes 4718592 | tf_op jit(solution)/shard_map/ihd,jhd->hij/dot_general | solution.py:73
  22.8 13.8 %collective-permute-done = bf16[1024,128]{1,0:T(8,128)(2,1)} collective-permute-done((bf16[1024,128]{1,0:T(8,128)(2,1)}, bf16[1024,128]{1,0:T(8,128)(2,1)}, u32[]{:S(2)}, u32[]{:S(2)}) %collective-permute-start) | collective-permute-done | bytes 262176 | tf_op jit(solution)/shard_map/ppermute | solution.py:91
  43.6 3.9 %collective-permute-done.3 = bf16[1024,128]{1,0:T(8,128)(2,1)S(1)} collective-permute-done((bf16[1024,128]{1,0:T(8,128)(2,1)}, bf16[1024,128]{1,0:T(8,128)(2,1)S(1)}, u32[]{:S(2)}, u32[]{:S(2)}) %collective-permute-start.3) | collective-permute-done | bytes 262176 | tf_op jit(solution)/shard_map/ppermute | solution.py:91
  47.6 5.6 %collective-permute-done.4 = bf16[1024,128]{1,0:T(8,128)(2,1)S(1)} collective-permute-done((bf16[1024,128]{1,0:T(8,128)(2,1)}, bf16[1024,128]{1,0:T(8,128)(2,1)S(1)}, u32[]{:S(2)}, u32[]{:S(2)}) %collective-permute-start.4) | collective-permute-done | bytes 262176 | tf_op jit(solution)/shard_map/ppermute | solution.py:91
  55.9 5.2 %collective-permute-done.6 = bf16[1024,128]{1,0:T(8,128)(2,1)S(1)} collective-permute-done((bf16[1024,128]{1,0:T(8,128)(2,1)}, bf16[1024,128]{1,0:T(8,128)(2,1)S(1)}, u32[]{:S(2)}, u32[]{:S(2)}) %collective-permute-start.6) | collective-permute-done | bytes 262176 | tf_op jit(solution)/shard_map/ppermute | solution.py:91
  61.2 2.6 %copy.83 = bf16[1024,1024]{1,0:T(8,128)(2,1)} copy(bf16[1024,1024]{0,1:T(8,128)(2,1)S(1)} %bitcast.374) | data formatting | bytes 4194304 | tf_op jit(solution)/shard_map/dot_general | solution.py:102
  64.6 2.6 %fusion.91 = s32[1024]{0:T(1024)S(1)} fusion(bf16[2056,128]{1,0:T(8,128)(2,1)} %collective-permute-done.8), kind=kLoop, calls=%fused_computation.173 | loop fusion | flops 1024 | bytes 6144 | tf_op jit(solution)/shard_map/convert_element_type | solution.py:64
  69.5 10.5 %fusion.26 = (bf16[1024,1024]{1,0:T(8,128)(2,1)S(1)}, bf16[1024,1024]{1,0:T(8,128)(2,1)S(1)}, bf16[1024,1024]{1,0:T(8,128)(2,1)S(1)}, bf16[1024,1024]{1,0:T(8,128)(2,1)S(1)}, f32[1024,1024]{0,1:T(8,128)}) fusion(s32[1024]{0:T(1024)S(1)} %fusion.92, f32[]{:T(128)} %bitcast.371, pred[]{:T(512)S(6)} %ge.26, s32[1024]{0:T(1024)S(1)} %copy-done.24, ...), kind=kOutput, calls=%fused_computation.37 | convolution fusion | flops 312475648 | bytes 25711620 | tf_op jit(solution)/shard_map/ihd,jhd->hij/dot_general | solution.py:73
  87.4 2.4 %gather_fusion.1 = f32[8,128,128]{2,1,0:T(8,128)} fusion(f32[128,8,128]{2,0,1:T(8,128)} %fusion.57, s32[1024]{0:T(1024)S(1)} %pad_clamp_fusion), kind=kCustom, calls=%fused_computation.1 | custom fusion | bytes 1048608 | tf_op jit(solution)/shard_map/jit(_take)/gather | solution.py:106
  96.2 3.9 %fusion.32 = bf16[1024,1024]{1,0:T(8,128)(2,1)S(1)} fusion(f32[1024,1024]{0,1:T(8,128)S(1)} %copy-done.25, bf16[1024,128]{0,1:T(8,128)(2,1)S(1)} %get-tuple-element.21, s32[1024]{0:T(1024)S(1)} %fusion.92, f32[]{:T(128)} %bitcast.369, pred[]{:T(512)S(6)} %ge.26, s32[1024]{0:T(1024)S(1)} %copy-done.24, bf16[2056,128]{1,0:T(8,128)(2,1)} %collective-permute-done.7), kind=kOutput, calls=%fused_computation.43 | convolution fusion | flops 284164096 | bytes 6824449 | tf_op jit(solution)/shard_map/ihd,jhd->hij/dot_general | solution.py:129
  101.7 2.1 %collective-permute-start.10 = (bf16[2,1024,128]{2,1,0:T(8,128)(2,1)}, bf16[2,1024,128]{2,1,0:T(8,128)(2,1)S(1)}, u32[]{:S(2)}, u32[]{:S(2)}) collective-permute-start(bf16[2,1024,128]{2,1,0:T(8,128)(2,1)} %pad_maximum_fusion.1), channel_id=1, source_target_pairs={{8,0},{16,8},{24,16},{32,24},{40,32},{48,40},{56,48},{64,56},{72,6... | collective-permute-start | bytes 1572872 | tf_op jit(solution)/shard_map/ppermute | solution.py:18
  103.8 3.9 %fusion.21 = bf16[1024,1024]{1,0:T(8,128)(2,1)S(1)} fusion(f32[1024,1024]{0,1:T(8,128)S(1)} %copy-done.15, bf16[1024,128]{0,1:T(8,128)(2,1)S(1)} %get-tuple-element.21, s32[1024]{0:T(1024)S(1)} %fusion.91, f32[]{:T(128)} %bitcast.373, pred[]{:T(512)S(6)} %ge.27, s32[1024]{0:T(1024)S(1)} %copy-done.24, bf16[2056,128]{1,0:T(8,128)(2,1)} %collective-permute-done.8), kind=kOutput, calls=%fused_computation.29 | convolution fusion | flops 284164096 | bytes 6824449 | tf_op jit(solution)/shard_map/ihd,jhd->hij/dot_general | solution.py:129
  109.9 2.8 %fusion.10 = bf16[1024,1024]{1,0:T(8,128)(2,1)S(1)} fusion(f32[1024,1024]{0,1:T(8,128)S(1)} %copy-done.13, bf16[1024,128]{0,1:T(8,128)(2,1)S(1)} %get-tuple-element.21, s32[1024]{0:T(1024)S(1)} %fusion.90, f32[]{:T(128)} %bitcast.372, pred[]{:T(512)S(6)} %ge.28, s32[1024]{0:T(1024)S(1)} %copy-done.24, bf16[2056,128]{1,0:T(8,128)(2,1)S(1)} %copy-done.19), kind=kOutput, calls=%fused_computation.15 | convolution fusion | flops 284164096 | bytes 6823941 | tf_op jit(solution)/shard_map/ihd,jhd->hij/dot_general | solution.py:129
  114.9 3.4 %select_convert_fusion = bf16[1024,1024]{1,0:T(8,128)(2,1)S(1)} fusion(f32[1024,1024]{1,0:T(8,128)S(1)} %copy-done.11, bf16[1024,128]{0,1:T(8,128)(2,1)S(1)} %get-tuple-element.21, bf16[1024,128]{1,0:T(8,128)(2,1)S(1)} %copy-done.21, f32[]{:T(128)} %bitcast.370, s32[1024]{0:T(1024)S(1)} %copy-done.24, pred[]{:T(512)S(6)} %ge.24), kind=kOutput, calls=%fused_computation.44 | convolution fusion | flops 286261248 | bytes 6819845 | tf_op jit(solution)/shard_map/ihd,jhd->hij/dot_general | solution.py:129
  121.5 2.5 %fusion.36 = f32[1024,128]{1,0:T(8,128)} fusion(f32[128,1024]{0,1:T(8,128)S(1)} %fusion.63, f32[128,1024]{0,1:T(8,128)S(1)} %fusion.70, f32[128,1024]{0,1:T(8,128)S(1)} %convolution_bitcast_fusion.2, bf16[1024,1024]{1,0:T(8,128)(2,1)S(1)} %fusion.32, bf16[2056,128]{1,0:T(8,128)(2,1)} %collective-permute-done.7), kind=kOutput, calls=%fused_computation.63 | convolution fusion | flops 268828672 | bytes 4456448 | tf_op jit(solution)/shard_map/hij,jhd->ihd/dot_general | solution.py:148
  125.8 10.5 %collective-permute-start.14 = (f32[128,2,2,2,32]{0,4,3,2,1:T(8,128)S(1)}, f32[128,2,2,2,32]{0,4,3,2,1:T(8,128)S(1)}, u32[]{:S(2)}, u32[]{:S(2)}) collective-permute-start(f32[128,2,2,2,32]{0,4,3,2,1:T(8,128)S(1)} %select_bitcast_fusion.1), channel_id=1, source_target_pairs={{0,16},{8,24},{16,0},{24,8},{32,48},{40,56},{48,32},{56,40},{64,80... | collective-permute-start | bytes 393224 | tf_op jit(solution)/shard_map/ppermute | solution.py:35
  137.2 3.2 %collective-permute-done.14 = f32[128,2,2,2,32]{0,4,3,2,1:T(8,128)S(1)} collective-permute-done((f32[128,2,2,2,32]{0,4,3,2,1:T(8,128)S(1)}, f32[128,2,2,2,32]{0,4,3,2,1:T(8,128)S(1)}, u32[]{:S(2)}, u32[]{:S(2)}) %collective-permute-start.14) | collective-permute-done | bytes 131104 | tf_op jit(solution)/shard_map/ppermute | solution.py:35
  141.7 5.1 %collective-permute-start.11 = (bf16[2,1024,128]{2,1,0:T(8,128)(2,1)}, bf16[2,1024,128]{2,1,0:T(8,128)(2,1)S(1)}, u32[]{:S(2)}, u32[]{:S(2)}) collective-permute-start(bf16[2,1024,128]{2,1,0:T(8,128)(2,1)} %pad_maximum_fusion.2), channel_id=1, source_target_pairs={{16,0},{24,8},{32,16},{40,24},{48,32},{56,40},{64,48},{72,56},{80,... | collective-permute-start | bytes 1572872 | tf_op jit(solution)/shard_map/ppermute | solution.py:18
  146.8 5.4 %collective-permute-start.16 = (f32[128,2,32]{0,2,1:T(8,128)S(1)}, f32[128,2,32]{0,2,1:T(8,128)S(1)}, u32[]{:S(2)}, u32[]{:S(2)}) collective-permute-start(f32[128,2,32]{0,2,1:T(8,128)S(1)} %select_bitcast_fusion.3), channel_id=1, source_target_pairs={{0,64},{8,72},{16,80},{24,88},{32,96},{40,104},{48,112},{56,120},{... | collective-permute-start | bytes 98312 | tf_op jit(solution)/shard_map/ppermute | solution.py:35
  155.0 10.8 %collective-permute-done.16 = f32[128,2,32]{0,2,1:T(8,128)S(1)} collective-permute-done((f32[128,2,32]{0,2,1:T(8,128)S(1)}, f32[128,2,32]{0,2,1:T(8,128)S(1)}, u32[]{:S(2)}, u32[]{:S(2)}) %collective-permute-start.16) | collective-permute-done | bytes 32800 | tf_op jit(solution)/shard_map/ppermute | solution.py:35
  167.8 10.2 %collective-permute-done.17 = f32[128,32]{0,1:T(8,128)S(1)} collective-permute-done((f32[128,32]{0,1:T(8,128)S(1)}, f32[128,32]{0,1:T(8,128)S(1)}, u32[]{:S(2)}, u32[]{:S(2)}) %collective-permute-start.17) | collective-permute-done | bytes 16416 | tf_op jit(solution)/shard_map/ppermute | solution.py:35
  (140 shorter events, 55.0 us)
Async XLA Ops:
  0.6 18.7 %copy-start.22 = (bf16[128,1024]{1,0:T(8,128)(2,1)S(1)}, bf16[128,1024]{1,0:T(8,128)(2,1)}, u32[]{:S(2)}) copy-start(bf16[128,1024]{1,0:T(8,128)(2,1)} %param.15) | copy-start | bytes 786436
  1.4 19.4 %copy-start.23 = (bf16[1024,128]{1,0:T(8,128)(2,1)S(1)}, bf16[1024,128]{1,0:T(8,128)(2,1)}, u32[]{:S(2)}) copy-start(bf16[1024,128]{1,0:T(8,128)(2,1)} %param.14) | copy-start | bytes 786436
  3.4 60.5 %collective-permute-start.9 = (bf16[2056,128]{1,0:T(8,128)(2,1)}, bf16[2056,128]{1,0:T(8,128)(2,1)S(1)}, u32[]{:S(2)}, u32[]{:S(2)}) collective-permute-start(bf16[2056,128]{1,0:T(8,128)(2,1)} %pad_maximum_fusion), channel_id=1, source_target_pairs={{0,24},{8,32},{16,40},{24,48},{32,56},{40,64},{48,72},{56,80},{64,... | collective-permute-start | bytes 1579016 | tf_op jit(solution)/shard_map/ppermute | solution.py:18
  6.0 58.6 %collective-permute-start.8 = (bf16[2056,128]{1,0:T(8,128)(2,1)}, bf16[2056,128]{1,0:T(8,128)(2,1)}, u32[]{:S(2)}, u32[]{:S(2)}) collective-permute-start(bf16[2056,128]{1,0:T(8,128)(2,1)} %pad_maximum_fusion), channel_id=1, source_target_pairs={{0,16},{8,24},{16,32},{24,40},{32,48},{40,56},{48,64},{56,72},{64,... | collective-permute-start | bytes 1579016 | tf_op jit(solution)/shard_map/ppermute | solution.py:18
  10.0 26.6 %collective-permute-start = (bf16[1024,128]{1,0:T(8,128)(2,1)}, bf16[1024,128]{1,0:T(8,128)(2,1)}, u32[]{:S(2)}, u32[]{:S(2)}) collective-permute-start(bf16[1024,128]{1,0:T(8,128)(2,1)} %param.14), channel_id=1, source_target_pairs={{0,1},{1,2},{2,3},{3,4},{4,5},{5,6},{6,7},{7,0},{8,9},{9,10},{10,1... | collective-permute-start | bytes 786440 | tf_op jit(solution)/shard_map/ppermute | solution.py:91
  11.3 28.4 %collective-permute-start.1 = (bf16[1024,128]{1,0:T(8,128)(2,1)}, bf16[1024,128]{1,0:T(8,128)(2,1)}, u32[]{:S(2)}, u32[]{:S(2)}) collective-permute-start(bf16[1024,128]{1,0:T(8,128)(2,1)} %param.14), channel_id=1, source_target_pairs={{0,2},{1,3},{2,4},{3,5},{4,6},{5,7},{6,0},{7,1},{8,10},{9,11},{10,... | collective-permute-start | bytes 786440 | tf_op jit(solution)/shard_map/ppermute | solution.py:91
  12.5 28.8 %collective-permute-start.2 = (bf16[1024,128]{1,0:T(8,128)(2,1)}, bf16[1024,128]{1,0:T(8,128)(2,1)}, u32[]{:S(2)}, u32[]{:S(2)}) collective-permute-start(bf16[1024,128]{1,0:T(8,128)(2,1)} %param.14), channel_id=1, source_target_pairs={{0,3},{1,4},{2,5},{3,6},{4,7},{5,0},{6,1},{7,2},{8,11},{9,12},{10,... | collective-permute-start | bytes 786440 | tf_op jit(solution)/shard_map/ppermute | solution.py:91
  36.6 10.9 %collective-permute-start.3 = (bf16[1024,128]{1,0:T(8,128)(2,1)}, bf16[1024,128]{1,0:T(8,128)(2,1)S(1)}, u32[]{:S(2)}, u32[]{:S(2)}) collective-permute-start(bf16[1024,128]{1,0:T(8,128)(2,1)} %param.14), channel_id=1, source_target_pairs={{0,4},{1,5},{2,6},{3,7},{4,0},{5,1},{6,2},{7,3},{8,12},{9,13},{10,... | collective-permute-start | bytes 786440 | tf_op jit(solution)/shard_map/ppermute | solution.py:91
  39.8 13.4 %collective-permute-start.4 = (bf16[1024,128]{1,0:T(8,128)(2,1)}, bf16[1024,128]{1,0:T(8,128)(2,1)S(1)}, u32[]{:S(2)}, u32[]{:S(2)}) collective-permute-start(bf16[1024,128]{1,0:T(8,128)(2,1)} %param.14), channel_id=1, source_target_pairs={{0,5},{1,6},{2,7},{3,0},{4,1},{5,2},{6,3},{7,4},{8,13},{9,14},{10,... | collective-permute-start | bytes 786440 | tf_op jit(solution)/shard_map/ppermute | solution.py:91
  41.3 14.5 %collective-permute-start.5 = (bf16[1024,128]{1,0:T(8,128)(2,1)}, bf16[1024,128]{1,0:T(8,128)(2,1)S(1)}, u32[]{:S(2)}, u32[]{:S(2)}) collective-permute-start(bf16[1024,128]{1,0:T(8,128)(2,1)} %param.14), channel_id=1, source_target_pairs={{0,6},{1,7},{2,0},{3,1},{4,2},{5,3},{6,4},{7,5},{8,14},{9,15},{10,... | collective-permute-start | bytes 786440 | tf_op jit(solution)/shard_map/ppermute | solution.py:91
  47.5 13.7 %collective-permute-start.6 = (bf16[1024,128]{1,0:T(8,128)(2,1)}, bf16[1024,128]{1,0:T(8,128)(2,1)S(1)}, u32[]{:S(2)}, u32[]{:S(2)}) collective-permute-start(bf16[1024,128]{1,0:T(8,128)(2,1)} %param.14), channel_id=1, source_target_pairs={{0,7},{1,0},{2,1},{3,2},{4,3},{5,4},{6,5},{7,6},{8,15},{9,8},{10,9... | collective-permute-start | bytes 786440 | tf_op jit(solution)/shard_map/ppermute | solution.py:91
  53.1 15.7 %collective-permute-start.7 = (bf16[2056,128]{1,0:T(8,128)(2,1)}, bf16[2056,128]{1,0:T(8,128)(2,1)}, u32[]{:S(2)}, u32[]{:S(2)}) collective-permute-start(bf16[2056,128]{1,0:T(8,128)(2,1)} %pad_maximum_fusion), channel_id=1, source_target_pairs={{0,8},{8,16},{16,24},{24,32},{32,40},{40,48},{48,56},{56,64},{64,7... | collective-permute-start | bytes 1579016 | tf_op jit(solution)/shard_map/ppermute | solution.py:18
  63.8 19.1 %copy-start.18 = (bf16[2056,128]{1,0:T(8,128)(2,1)}, bf16[2056,128]{1,0:T(8,128)(2,1)S(1)}, u32[]{:S(2)}) copy-start(bf16[2056,128]{1,0:T(8,128)(2,1)S(1)} %collective-permute-done.9) | copy-start | bytes 1579012
  64.6 15.5 %copy-start.12 = (f32[1024,1024]{0,1:T(8,128)}, f32[1024,1024]{0,1:T(8,128)S(1)}, u32[]{:S(2)}) copy-start(f32[1024,1024]{0,1:T(8,128)S(1)} %fusion.65) | copy-start | bytes 12582916
  93.2 32.5 %collective-permute-start.13 = (f32[128,2,2,2,2,32]{0,5,4,3,2,1:T(8,128)S(1)}, f32[128,2,2,2,2,32]{0,5,4,3,2,1:T(8,128)S(1)}, u32[]{:S(2)}, u32[]{:S(2)}) collective-permute-start(f32[128,2,2,2,2,32]{0,5,4,3,2,1:T(8,128)S(1)} %select_bitcast_fusion), channel_id=1, source_target_pairs={{0,8},{8,0},{16,24},{24,16},{32,40},{40,32},{48,56},{56,48},{64,72... | collective-permute-start | bytes 786440 | tf_op jit(solution)/shard_map/ppermute | solution.py:35
  101.7 77.0 %collective-permute-start.10 = (bf16[2,1024,128]{2,1,0:T(8,128)(2,1)}, bf16[2,1024,128]{2,1,0:T(8,128)(2,1)S(1)}, u32[]{:S(2)}, u32[]{:S(2)}) collective-permute-start(bf16[2,1024,128]{2,1,0:T(8,128)(2,1)} %pad_maximum_fusion.1), channel_id=1, source_target_pairs={{8,0},{16,8},{24,16},{32,24},{40,32},{48,40},{56,48},{64,56},{72,6... | collective-permute-start | bytes 1572872 | tf_op jit(solution)/shard_map/ppermute | solution.py:18
  125.7 40.2 %copy-start.8 = (bf16[1024,1024]{1,0:T(8,128)(2,1)S(1)}, bf16[1024,1024]{1,0:T(8,128)(2,1)}, u32[]{:S(2)}) copy-start(bf16[1024,1024]{1,0:T(8,128)(2,1)} %copy-done.7) | copy-start | bytes 6291460
  125.8 41.0 %copy-start.17 = (f32[1024,128]{0,1:T(8,128)S(1)}, f32[1024,128]{0,1:T(8,128)}, u32[]{:S(2)}) copy-start(f32[1024,128]{0,1:T(8,128)} %get-tuple-element.20) | copy-start | bytes 1572868
  125.8 14.6 %collective-permute-start.14 = (f32[128,2,2,2,32]{0,4,3,2,1:T(8,128)S(1)}, f32[128,2,2,2,32]{0,4,3,2,1:T(8,128)S(1)}, u32[]{:S(2)}, u32[]{:S(2)}) collective-permute-start(f32[128,2,2,2,32]{0,4,3,2,1:T(8,128)S(1)} %select_bitcast_fusion.1), channel_id=1, source_target_pairs={{0,16},{8,24},{16,0},{24,8},{32,48},{40,56},{48,32},{56,40},{64,80... | collective-permute-start | bytes 393224 | tf_op jit(solution)/shard_map/ppermute | solution.py:35
  140.5 6.3 %collective-permute-start.15 = (f32[128,2,2,32]{0,3,2,1:T(8,128)S(1)}, f32[128,2,2,32]{0,3,2,1:T(8,128)S(1)}, u32[]{:S(2)}, u32[]{:S(2)}) collective-permute-start(f32[128,2,2,32]{0,3,2,1:T(8,128)S(1)} %select_bitcast_fusion.2), channel_id=1, source_target_pairs={{0,32},{8,40},{16,48},{24,56},{32,0},{40,8},{48,16},{56,24},{64,96... | collective-permute-start | bytes 196616 | tf_op jit(solution)/shard_map/ppermute | solution.py:35
  141.7 37.0 %collective-permute-start.11 = (bf16[2,1024,128]{2,1,0:T(8,128)(2,1)}, bf16[2,1024,128]{2,1,0:T(8,128)(2,1)S(1)}, u32[]{:S(2)}, u32[]{:S(2)}) collective-permute-start(bf16[2,1024,128]{2,1,0:T(8,128)(2,1)} %pad_maximum_fusion.2), channel_id=1, source_target_pairs={{16,0},{24,8},{32,16},{40,24},{48,32},{56,40},{64,48},{72,56},{80,... | collective-permute-start | bytes 1572872 | tf_op jit(solution)/shard_map/ppermute | solution.py:18
  146.8 18.9 %collective-permute-start.16 = (f32[128,2,32]{0,2,1:T(8,128)S(1)}, f32[128,2,32]{0,2,1:T(8,128)S(1)}, u32[]{:S(2)}, u32[]{:S(2)}) collective-permute-start(f32[128,2,32]{0,2,1:T(8,128)S(1)} %select_bitcast_fusion.3), channel_id=1, source_target_pairs={{0,64},{8,72},{16,80},{24,88},{32,96},{40,104},{48,112},{56,120},{... | collective-permute-start | bytes 98312 | tf_op jit(solution)/shard_map/ppermute | solution.py:35
  153.0 25.6 %collective-permute-start.12 = (bf16[2,1024,128]{2,1,0:T(8,128)(2,1)}, bf16[2,1024,128]{2,1,0:T(8,128)(2,1)}, u32[]{:S(2)}, u32[]{:S(2)}) collective-permute-start(bf16[2,1024,128]{2,1,0:T(8,128)(2,1)} %pad_maximum_fusion.3), channel_id=1, source_target_pairs={{24,0},{32,8},{40,16},{48,24},{56,32},{64,40},{72,48},{80,56},{88,... | collective-permute-start | bytes 1572872 | tf_op jit(solution)/shard_map/ppermute | solution.py:18
  165.8 12.3 %collective-permute-start.17 = (f32[128,32]{0,1:T(8,128)S(1)}, f32[128,32]{0,1:T(8,128)S(1)}, u32[]{:S(2)}, u32[]{:S(2)}) collective-permute-start(f32[128,32]{0,1:T(8,128)S(1)} %select_bitcast_fusion.4), channel_id=1, source_target_pairs={{0,128},{8,136},{16,144},{24,152},{32,160},{40,168},{48,176},{56,1... | collective-permute-start | bytes 49160 | tf_op jit(solution)/shard_map/ppermute | solution.py:35
  (20 other events, 107.7 us)

commit v3 on v2

--- a/solution.py
+++ b/solution.py
@@ -18,22 +18,24 @@
     return lax.ppermute(block, axis, route)
 
 
-def halving_scatter(block, axis):
+def halving_start(block, axis):
+    count = lax.axis_size(axis)
+    rows, cols = block.shape
+    levels = count.bit_length() - 1
+    return block.reshape((rows,) + (2,) * levels + (cols // count,))
+
+
+def halving_step(current, axis, level):
     count = lax.axis_size(axis)
     my_index = lax.axis_index(axis)
-    rows, cols = block.shape
-    levels = count.bit_length() - 1
-    current = block.reshape((rows,) + (2,) * levels + (cols // count,))
-    for level in range(levels):
-        bit = 1 << level
-        axis_pos = current.ndim - 2
-        mine = (my_index // bit) % 2
-        low = lax.index_in_dim(current, 0, axis_pos, keepdims=False)
-        high = lax.index_in_dim(current, 1, axis_pos, keepdims=False)
-        keep = jnp.where(mine == 0, low, high)
-        send = jnp.where(mine == 0, high, low)
-        current = keep + lax.ppermute(send, axis, [(i, i ^ bit) for i in range(count)])
-    return current.reshape(rows, cols // count)
+    bit = 1 << level
+    axis_pos = current.ndim - 2
+    mine = (my_index // bit) % 2
+    low = lax.index_in_dim(current, 0, axis_pos, keepdims=False)
+    high = lax.index_in_dim(current, 1, axis_pos, keepdims=False)
+    keep = jnp.where(mine == 0, low, high)
+    send = jnp.where(mine == 0, high, low)
+    return keep + lax.ppermute(send, axis, [(i, i ^ bit) for i in range(count)])
 
 
 def silu_parts(scores):
@@ -106,7 +108,8 @@
     weight_rows = jnp.take(
         product.reshape(product.shape[0], head_devices, block_width), gather_back, axis=1
     ).reshape(product.shape)
-    grad_w_out = halving_scatter(weight_rows, "seq")
+    halving = halving_start(weight_rows, "seq")
+    halving_levels = lax.axis_size("seq").bit_length() - 1
     grad_mixed = grad_mixed.reshape(row_count, head_count, DH)
     grad_gates = (grad_mixed * normed).reshape(row_count, feature_count)
     grad_normed = grad_mixed * gate_heads
@@ -118,7 +121,12 @@
     grad_attended = grad_attended.astype(jnp.bfloat16)
     grad_queries = jnp.zeros((row_count, head_count, DH), jnp.float32)
     key_terms = []
+    done_levels = 0
     for window_index in range(4):
+        if window_index > 0 and done_levels < halving_levels:
+            halving = halving_step(halving, "seq", done_levels)
+            done_levels += 1
+            halving, grad_attended = lax.optimization_barrier((halving, grad_attended))
         k_heads, v_heads, allowed = prepared[window_index]
         scores = pair_scores(q_heads, k_heads)
         key_act, key_deriv = silu_parts(scores)
@@ -152,6 +160,10 @@
     for distance in back_steps:
         sent = shifted(key_terms[distance].astype(jnp.bfloat16), "seq", -distance)
         summed = summed + sent.astype(jnp.float32)
+    while done_levels < halving_levels:
+        halving = halving_step(halving, "seq", done_levels)
+        done_levels += 1
+    grad_w_out = halving.reshape(halving.shape[0], -1)
     return (
         grad_queries.reshape(row_count, feature_count),
         summed[0],

time: 182 us -> 169 us (0.929)
  the two profiles are of different devices: /device:TPU:50 before, /device:TPU:51 now
where the time goes in v3:
time: 169 us; the launch traced here: 168 us
  starting transfers between devices  61.3 us (36%)
  matrix products  57.7 us (34%)
  waiting for transfers between devices  24.8 us (15%)
  local copies, waits for them, and re-layouts  14 us (8%)
  other arithmetic  8.29 us (5%)
  between operations  2.22 us (1%)
    ppermute x6, starting transfers between devices, shifted(): return lax.ppermute(block, axis, route)  30.9 us
    ppermute x5, starting transfers between devices, halving_step(): return keep + lax.ppermute(send, axis, [(i, i ^ bit) for i in range(count)])  20.2 us
    dot_general x4, matrix products, pair_scores(): jnp.einsum('ihd,jhd->hij', query_heads, k_heads, preferred_element_type=j...  17.9 us
    dot_general x4, matrix products, per_device(): jnp.einsum('ihd,jhd->hij', grad_attended, v_heads, preferred_element_type...  16.6 us
    ppermute x7, waiting for transfers between devices, per_device(): lax.ppermute(grad_out, 'head', [(i, (i + k) % head_devices) for i in rang...  16.2 us
    ppermute x7, starting transfers between devices, per_device(): lax.ppermute(grad_out, 'head', [(i, (i + k) % head_devices) for i in rang...  10.2 us
    ppermute x5, waiting for transfers between devices, halving_step(): return keep + lax.ppermute(send, axis, [(i, i ^ bit) for i in range(count)])  8.65 us
    unnamed x66, local copies, waits for them, and re-layouts  8.4 us
  transfers between devices with their start and end apart: 18, of which 4 were waited for; matrix products, arithmetic and copies ran while one was open for 31% of the time, Pallas kernels for 0%

profile of v3, /device:TPU:51, one launch (start us, length us, event | category | flops | bytes accessed | tf_op | source)
XLA Modules:
  0.0 168.3 jit_solution(267416098804744605)
XLA Ops:
  3.3 4.1 %collective-permute-start.9 = (bf16[2056,128]{1,0:T(8,128)(2,1)}, bf16[2056,128]{1,0:T(8,128)(2,1)}, u32[]{:S(2)}, u32[]{:S(2)}) collective-permute-start(bf16[2056,128]{1,0:T(8,128)(2,1)} %pad_maximum_fusion), channel_id=1, source_target_pairs={{0,24},{8,32},{16,40},{24,48},{32,56},{40,64},{48,72},{56,80},{64,... | collective-permute-start | bytes 1579016 | tf_op jit(solution)/shard_map/ppermute | solution.py:18
  7.4 2.9 %collective-permute-start.8 = (bf16[2056,128]{1,0:T(8,128)(2,1)}, bf16[2056,128]{1,0:T(8,128)(2,1)}, u32[]{:S(2)}, u32[]{:S(2)}) collective-permute-start(bf16[2056,128]{1,0:T(8,128)(2,1)} %pad_maximum_fusion), channel_id=1, source_target_pairs={{0,16},{8,24},{16,32},{24,40},{32,48},{40,56},{48,64},{56,72},{64,... | collective-permute-start | bytes 1579016 | tf_op jit(solution)/shard_map/ppermute | solution.py:18
  12.6 2.5 %collective-permute-start.2 = (bf16[1024,128]{1,0:T(8,128)(2,1)}, bf16[1024,128]{1,0:T(8,128)(2,1)}, u32[]{:S(2)}, u32[]{:S(2)}) collective-permute-start(bf16[1024,128]{1,0:T(8,128)(2,1)} %param.14), channel_id=1, source_target_pairs={{0,3},{1,4},{2,5},{3,6},{4,7},{5,0},{6,1},{7,2},{8,11},{9,12},{10,... | collective-permute-start | bytes 786440 | tf_op jit(solution)/shard_map/ppermute | solution.py:93
  15.2 3.7 %fusion.101 = f32[1024,1024]{1,0:T(8,128)} fusion(bf16[1024,128]{1,0:T(8,128)(2,1)S(1)} %copy-done, bf16[1024,128]{1,0:T(8,128)(2,1)} %param.9), kind=kOutput, calls=%fused_computation.195 | convolution fusion | flops 268435456 | bytes 4718592 | tf_op jit(solution)/shard_map/ihd,jhd->hij/dot_general | solution.py:75
  22.3 12.4 %collective-permute-done = bf16[1024,128]{1,0:T(8,128)(2,1)} collective-permute-done((bf16[1024,128]{1,0:T(8,128)(2,1)}, bf16[1024,128]{1,0:T(8,128)(2,1)}, u32[]{:S(2)}, u32[]{:S(2)}) %collective-permute-start) | collective-permute-done | bytes 262176 | tf_op jit(solution)/shard_map/ppermute | solution.py:93
  41.8 2.3 %collective-permute-start.6 = (bf16[1024,128]{1,0:T(8,128)(2,1)}, bf16[1024,128]{1,0:T(8,128)(2,1)S(1)}, u32[]{:S(2)}, u32[]{:S(2)}) collective-permute-start(bf16[1024,128]{1,0:T(8,128)(2,1)} %param.14), channel_id=1, source_target_pairs={{0,7},{1,0},{2,1},{3,2},{4,3},{5,4},{6,5},{7,6},{8,15},{9,8},{10,9... | collective-permute-start | bytes 786440 | tf_op jit(solution)/shard_map/ppermute | solution.py:93
  44.1 3.0 %collective-permute-done.4 = bf16[1024,128]{1,0:T(8,128)(2,1)S(1)} collective-permute-done((bf16[1024,128]{1,0:T(8,128)(2,1)}, bf16[1024,128]{1,0:T(8,128)(2,1)S(1)}, u32[]{:S(2)}, u32[]{:S(2)}) %collective-permute-start.4) | collective-permute-done | bytes 262176 | tf_op jit(solution)/shard_map/ppermute | solution.py:93
  47.2 13.4 %collective-permute-start.7 = (bf16[2056,128]{1,0:T(8,128)(2,1)}, bf16[2056,128]{1,0:T(8,128)(2,1)}, u32[]{:S(2)}, u32[]{:S(2)}) collective-permute-start(bf16[2056,128]{1,0:T(8,128)(2,1)} %pad_maximum_fusion), channel_id=1, source_target_pairs={{0,8},{8,16},{16,24},{24,32},{32,40},{40,48},{48,56},{56,64},{64,7... | collective-permute-start | bytes 1579016 | tf_op jit(solution)/shard_map/ppermute | solution.py:18
  60.9 2.6 %copy.76 = bf16[1024,1024]{1,0:T(8,128)(2,1)} copy(bf16[1024,1024]{0,1:T(8,128)(2,1)S(1)} %bitcast.366) | data formatting | bytes 4194304 | tf_op jit(solution)/shard_map/dot_general | solution.py:104
  69.3 10.6 %fusion.26 = (bf16[1024,1024]{1,0:T(8,128)(2,1)S(1)}, bf16[1024,1024]{1,0:T(8,128)(2,1)S(1)}, bf16[1024,1024]{1,0:T(8,128)(2,1)S(1)}, bf16[1024,1024]{1,0:T(8,128)(2,1)S(1)}, f32[1024,1024]{0,1:T(8,128)}) fusion(s32[1024]{0:T(1024)S(1)} %fusion.96, f32[]{:T(128)} %bitcast.363, pred[]{:T(512)S(6)} %ge.26, s32[1024]{0:T(1024)S(1)} %copy-done.26, ...), kind=kOutput, calls=%fused_computation.37 | convolution fusion | flops 312475648 | bytes 25711620 | tf_op jit(solution)/shard_map/ihd,jhd->hij/dot_general | solution.py:75
  84.6 2.0 %fusion.100 = (f32[1024]{0:T(1024)S(1)}, f32[128,1024]{1,0:T(8,128)S(1)}) fusion(f32[128,1024]{1,0:T(8,128)S(1)} %fusion.75, f32[128,1024]{1,0:T(8,128)S(1)} %fusion.82, f32[128,1024]{1,0:T(8,128)S(1)} %convolution_bitcast_fusion.3, bf16[1024,1024]{1,0:T(8,128)(2,1)S(1)} %get-tuple-element.36, bf16[2056,128]{1,0:T(8,128)(2,1)} %collective-permute-done.7), kind=kOutput, calls=%fused_computation.194 | convolution fusion | flops 268958720 | bytes 4460544 | tf_op jit(solution)/shard_map/hij,jhd->ihd/dot_general | solution.py:82
  93.1 5.1 %select_convert_fusion = bf16[1024,1024]{1,0:T(8,128)(2,1)S(1)} fusion(f32[1024,1024]{1,0:T(8,128)} %fusion.101, bf16[1024,128]{1,0:T(8,128)(2,1)S(1)} %copy-done.23, f32[]{:T(128)} %bitcast.362, s32[1024]{0:T(1024)S(1)} %copy-done.26, pred[]{:T(512)S(6)} %ge.24, bf16[1024,1,128]{0,2,1:T(8,128)(2,1)S(1)} %get-tuple-element.15), kind=kOutput, calls=%fused_computation.44 | convolution fusion | flops 286261248 | bytes 6819845 | tf_op jit(solution)/shard_map/ihd,jhd->hij/dot_general | solution.py:137
  101.5 2.0 %copy.101 = f32[1024,128]{1,0:T(8,128)} copy(f32[1024,128]{0,1:T(8,128)} %get-tuple-element.32) | data formatting | bytes 1048576
  104.3 10.2 %collective-permute-start.11 = (f32[128,2,2,2,32]{0,4,3,2,1:T(8,128)S(1)}, f32[128,2,2,2,32]{0,4,3,2,1:T(8,128)S(1)}, u32[]{:S(2)}, u32[]{:S(2)}) collective-permute-start(f32[128,2,2,2,32]{0,4,3,2,1:T(8,128)S(1)} %fusion.90), channel_id=1, source_target_pairs={{0,16},{8,24},{16,0},{24,8},{32,48},{40,56},{48,32},{56,40},{64,80... | collective-permute-start | bytes 393224 | tf_op jit(solution)/shard_map/ppermute | solution.py:38
  114.5 3.8 %fusion.32 = bf16[1024,1024]{1,0:T(8,128)(2,1)S(1)} fusion(f32[1024,1024]{0,1:T(8,128)S(1)} %copy-done.27, s32[1024]{0:T(1024)S(1)} %fusion.96, f32[]{:T(128)} %bitcast.361, pred[]{:T(512)S(6)} %ge.26, s32[1024]{0:T(1024)S(1)} %copy-done.26, bf16[1024,1,128]{0,2,1:T(8,128)(2,1)S(1)} %get-tuple-element.15, bf16[2056,128]{1,0:T(8,128)(2,1)} %collective-permute-done.7), kind=kOutput, calls=%fused_computation.43 | convolution fusion | flops 284164096 | bytes 6824449 | tf_op jit(solution)/shard_map/ihd,jhd->hij/dot_general | solution.py:137
  120.9 2.3 %collective-permute-start.13 = (bf16[2,1024,128]{2,1,0:T(8,128)(2,1)S(1)}, bf16[2,1024,128]{2,1,0:T(8,128)(2,1)S(1)}, u32[]{:S(2)}, u32[]{:S(2)}) collective-permute-start(bf16[2,1024,128]{2,1,0:T(8,128)(2,1)S(1)} %pad_maximum_fusion.1), channel_id=1, source_target_pairs={{8,0},{16,8},{24,16},{32,24},{40,32},{48,40},{56,48},{64,56},{72,6... | collective-permute-start | bytes 1572872 | tf_op jit(solution)/shard_map/ppermute | solution.py:18
  124.4 3.9 %fusion.21 = bf16[1024,1024]{1,0:T(8,128)(2,1)S(1)} fusion(f32[1024,1024]{0,1:T(8,128)S(1)} %copy-done.18, s32[1024]{0:T(1024)S(1)} %fusion.95, f32[]{:T(128)} %bitcast.365, pred[]{:T(512)S(6)} %ge.27, s32[1024]{0:T(1024)S(1)} %copy-done.26, bf16[1024,1,128]{0,2,1:T(8,128)(2,1)S(1)} %get-tuple-element.15, bf16[2056,128]{1,0:T(8,128)(2,1)} %collective-permute-done.8), kind=kOutput, calls=%fused_computation.29 | convolution fusion | flops 284164096 | bytes 6824449 | tf_op jit(solution)/shard_map/ihd,jhd->hij/dot_general | solution.py:137
  129.1 4.3 %collective-permute-start.14 = (bf16[2,1024,128]{2,1,0:T(8,128)(2,1)S(1)}, bf16[2,1024,128]{2,1,0:T(8,128)(2,1)S(1)}, u32[]{:S(2)}, u32[]{:S(2)}) collective-permute-start(bf16[2,1024,128]{2,1,0:T(8,128)(2,1)S(1)} %pad_maximum_fusion.2), channel_id=1, source_target_pairs={{16,0},{24,8},{32,16},{40,24},{48,32},{56,40},{64,48},{72,56},{80,... | collective-permute-start | bytes 1572872 | tf_op jit(solution)/shard_map/ppermute | solution.py:18
  135.1 5.1 %collective-permute-start.16 = (f32[128,2,32]{0,2,1:T(8,128)S(1)}, f32[128,2,32]{0,2,1:T(8,128)S(1)}, u32[]{:S(2)}, u32[]{:S(2)}) collective-permute-start(f32[128,2,32]{0,2,1:T(8,128)S(1)} %fusion.92), channel_id=1, source_target_pairs={{0,64},{8,72},{16,80},{24,88},{32,96},{40,104},{48,112},{56,120},{... | collective-permute-start | bytes 98312 | tf_op jit(solution)/shard_map/ppermute | solution.py:38
  141.2 3.9 %fusion.10 = bf16[1024,1024]{1,0:T(8,128)(2,1)S(1)} fusion(f32[1024,1024]{0,1:T(8,128)S(1)} %copy-done.16, s32[1024]{0:T(1024)S(1)} %fusion.94, f32[]{:T(128)} %bitcast.364, pred[]{:T(512)S(6)} %ge.28, s32[1024]{0:T(1024)S(1)} %copy-done.26, bf16[1024,1,128]{0,2,1:T(8,128)(2,1)S(1)} %get-tuple-element.15, bf16[2056,128]{1,0:T(8,128)(2,1)} %collective-permute-done.9), kind=kOutput, calls=%fused_computation.15 | convolution fusion | flops 284164096 | bytes 6824449 | tf_op jit(solution)/shard_map/ihd,jhd->hij/dot_general | solution.py:137
  145.9 3.8 %collective-permute-start.15 = (bf16[2,1024,128]{2,1,0:T(8,128)(2,1)S(1)}, bf16[2,1024,128]{2,1,0:T(8,128)(2,1)S(1)}, u32[]{:S(2)}, u32[]{:S(2)}) collective-permute-start(bf16[2,1024,128]{2,1,0:T(8,128)(2,1)S(1)} %pad_maximum_fusion.3), channel_id=1, source_target_pairs={{24,0},{32,8},{40,16},{48,24},{56,32},{64,40},{72,48},{80,56},{88,... | collective-permute-start | bytes 1572872 | tf_op jit(solution)/shard_map/ppermute | solution.py:18
  151.4 3.8 %collective-permute-start.17 = (f32[128,32]{0,1:T(8,128)S(1)}, f32[128,32]{0,1:T(8,128)S(1)}, u32[]{:S(2)}, u32[]{:S(2)}) collective-permute-start(f32[128,32]{0,1:T(8,128)S(1)} %select_bitcast_fusion.1), channel_id=1, source_target_pairs={{0,128},{8,136},{16,144},{24,152},{32,160},{40,168},{48,176},{56,1... | collective-permute-start | bytes 49160 | tf_op jit(solution)/shard_map/ppermute | solution.py:38
  155.3 2.5 %fusion.36 = f32[1024,128]{1,0:T(8,128)} fusion(f32[128,1024]{0,1:T(8,128)S(1)} %fusion.70, f32[128,1024]{0,1:T(8,128)S(1)} %fusion.77, f32[128,1024]{0,1:T(8,128)S(1)} %copy-done.21, bf16[1024,1024]{1,0:T(8,128)(2,1)S(1)} %fusion.32, bf16[2056,128]{1,0:T(8,128)(2,1)} %collective-permute-done.7), kind=kOutput, calls=%fused_computation.63 | convolution fusion | flops 268828672 | bytes 4456448 | tf_op jit(solution)/shard_map/hij,jhd->ihd/dot_general | solution.py:156
  157.8 8.6 %collective-permute-done.17 = f32[128,32]{0,1:T(8,128)S(1)} collective-permute-done((f32[128,32]{0,1:T(8,128)S(1)}, f32[128,32]{0,1:T(8,128)S(1)}, u32[]{:S(2)}, u32[]{:S(2)}) %collective-permute-start.17) | collective-permute-done | bytes 16416 | tf_op jit(solution)/shard_map/ppermute | solution.py:38
  (144 shorter events, 47.3 us)
Async XLA Ops:
  0.6 14.6 %copy-start = (bf16[1024,128]{1,0:T(8,128)(2,1)S(1)}, bf16[1024,128]{1,0:T(8,128)(2,1)}, u32[]{:S(2)}) copy-start(bf16[1024,128]{1,0:T(8,128)(2,1)} %param.8) | copy-start | bytes 786436
  0.6 18.2 %copy-start.24 = (bf16[128,1024]{1,0:T(8,128)(2,1)S(1)}, bf16[128,1024]{1,0:T(8,128)(2,1)}, u32[]{:S(2)}) copy-start(bf16[128,1024]{1,0:T(8,128)(2,1)} %param.15) | copy-start | bytes 786436
  1.4 18.9 %copy-start.25 = (bf16[1024,128]{1,0:T(8,128)(2,1)S(1)}, bf16[1024,128]{1,0:T(8,128)(2,1)}, u32[]{:S(2)}) copy-start(bf16[1024,128]{1,0:T(8,128)(2,1)} %param.14) | copy-start | bytes 786436
  3.3 60.2 %collective-permute-start.9 = (bf16[2056,128]{1,0:T(8,128)(2,1)}, bf16[2056,128]{1,0:T(8,128)(2,1)}, u32[]{:S(2)}, u32[]{:S(2)}) collective-permute-start(bf16[2056,128]{1,0:T(8,128)(2,1)} %pad_maximum_fusion), channel_id=1, source_target_pairs={{0,24},{8,32},{16,40},{24,48},{32,56},{40,64},{48,72},{56,80},{64,... | collective-permute-start | bytes 1579016 | tf_op jit(solution)/shard_map/ppermute | solution.py:18
  7.4 58.6 %collective-permute-start.8 = (bf16[2056,128]{1,0:T(8,128)(2,1)}, bf16[2056,128]{1,0:T(8,128)(2,1)}, u32[]{:S(2)}, u32[]{:S(2)}) collective-permute-start(bf16[2056,128]{1,0:T(8,128)(2,1)} %pad_maximum_fusion), channel_id=1, source_target_pairs={{0,16},{8,24},{16,32},{24,40},{32,48},{40,56},{48,64},{56,72},{64,... | collective-permute-start | bytes 1579016 | tf_op jit(solution)/shard_map/ppermute | solution.py:18
  10.3 24.4 %collective-permute-start = (bf16[1024,128]{1,0:T(8,128)(2,1)}, bf16[1024,128]{1,0:T(8,128)(2,1)}, u32[]{:S(2)}, u32[]{:S(2)}) collective-permute-start(bf16[1024,128]{1,0:T(8,128)(2,1)} %param.14), channel_id=1, source_target_pairs={{0,1},{1,2},{2,3},{3,4},{4,5},{5,6},{6,7},{7,0},{8,9},{9,10},{10,1... | collective-permute-start | bytes 786440 | tf_op jit(solution)/shard_map/ppermute | solution.py:93
  11.7 25.9 %collective-permute-start.1 = (bf16[1024,128]{1,0:T(8,128)(2,1)}, bf16[1024,128]{1,0:T(8,128)(2,1)}, u32[]{:S(2)}, u32[]{:S(2)}) collective-permute-start(bf16[1024,128]{1,0:T(8,128)(2,1)} %param.14), channel_id=1, source_target_pairs={{0,2},{1,3},{2,4},{3,5},{4,6},{5,7},{6,0},{7,1},{8,10},{9,11},{10,... | collective-permute-start | bytes 786440 | tf_op jit(solution)/shard_map/ppermute | solution.py:93
  12.6 26.3 %collective-permute-start.2 = (bf16[1024,128]{1,0:T(8,128)(2,1)}, bf16[1024,128]{1,0:T(8,128)(2,1)}, u32[]{:S(2)}, u32[]{:S(2)}) collective-permute-start(bf16[1024,128]{1,0:T(8,128)(2,1)} %param.14), channel_id=1, source_target_pairs={{0,3},{1,4},{2,5},{3,6},{4,7},{5,0},{6,1},{7,2},{8,11},{9,12},{10,... | collective-permute-start | bytes 786440 | tf_op jit(solution)/shard_map/ppermute | solution.py:93
  34.7 7.0 %collective-permute-start.3 = (bf16[1024,128]{1,0:T(8,128)(2,1)}, bf16[1024,128]{1,0:T(8,128)(2,1)S(1)}, u32[]{:S(2)}, u32[]{:S(2)}) collective-permute-start(bf16[1024,128]{1,0:T(8,128)(2,1)} %param.14), channel_id=1, source_target_pairs={{0,4},{1,5},{2,6},{3,7},{4,0},{5,1},{6,2},{7,3},{8,12},{9,13},{10,... | collective-permute-start | bytes 786440 | tf_op jit(solution)/shard_map/ppermute | solution.py:93
  37.6 9.5 %collective-permute-start.4 = (bf16[1024,128]{1,0:T(8,128)(2,1)}, bf16[1024,128]{1,0:T(8,128)(2,1)S(1)}, u32[]{:S(2)}, u32[]{:S(2)}) collective-permute-start(bf16[1024,128]{1,0:T(8,128)(2,1)} %param.14), channel_id=1, source_target_pairs={{0,5},{1,6},{2,7},{3,0},{4,1},{5,2},{6,3},{7,4},{8,13},{9,14},{10,... | collective-permute-start | bytes 786440 | tf_op jit(solution)/shard_map/ppermute | solution.py:93
  38.9 21.8 %collective-permute-start.5 = (bf16[1024,128]{1,0:T(8,128)(2,1)}, bf16[1024,128]{1,0:T(8,128)(2,1)S(1)}, u32[]{:S(2)}, u32[]{:S(2)}) collective-permute-start(bf16[1024,128]{1,0:T(8,128)(2,1)} %param.14), channel_id=1, source_target_pairs={{0,6},{1,7},{2,0},{3,1},{4,2},{5,3},{6,4},{7,5},{8,14},{9,15},{10,... | collective-permute-start | bytes 786440 | tf_op jit(solution)/shard_map/ppermute | solution.py:93
  41.8 19.0 %collective-permute-start.6 = (bf16[1024,128]{1,0:T(8,128)(2,1)}, bf16[1024,128]{1,0:T(8,128)(2,1)S(1)}, u32[]{:S(2)}, u32[]{:S(2)}) collective-permute-start(bf16[1024,128]{1,0:T(8,128)(2,1)} %param.14), channel_id=1, source_target_pairs={{0,7},{1,0},{2,1},{3,2},{4,3},{5,4},{6,5},{7,6},{8,15},{9,8},{10,9... | collective-permute-start | bytes 786440 | tf_op jit(solution)/shard_map/ppermute | solution.py:93
  47.2 21.4 %collective-permute-start.7 = (bf16[2056,128]{1,0:T(8,128)(2,1)}, bf16[2056,128]{1,0:T(8,128)(2,1)}, u32[]{:S(2)}, u32[]{:S(2)}) collective-permute-start(bf16[2056,128]{1,0:T(8,128)(2,1)} %pad_maximum_fusion), channel_id=1, source_target_pairs={{0,8},{8,16},{16,24},{24,32},{32,40},{40,48},{48,56},{56,64},{64,7... | collective-permute-start | bytes 1579016 | tf_op jit(solution)/shard_map/ppermute | solution.py:18
  66.0 13.9 %copy-start.15 = (f32[1024,1024]{0,1:T(8,128)}, f32[1024,1024]{0,1:T(8,128)S(1)}, u32[]{:S(2)}) copy-start(f32[1024,1024]{0,1:T(8,128)S(1)} %fusion.72) | copy-start | bytes 12582916
  91.1 13.2 %collective-permute-start.10 = (f32[128,2,2,2,2,32]{0,5,4,3,2,1:T(8,128)}, f32[128,2,2,2,2,32]{0,5,4,3,2,1:T(8,128)S(1)}, u32[]{:S(2)}, u32[]{:S(2)}) collective-permute-start(f32[128,2,2,2,2,32]{0,5,4,3,2,1:T(8,128)} %select_bitcast_fusion), channel_id=1, source_target_pairs={{0,8},{8,0},{16,24},{24,16},{32,40},{40,32},{48,56},{56,48},{64,72... | collective-permute-start | bytes 786440 | tf_op jit(solution)/shard_map/ppermute | solution.py:38
  104.3 18.9 %collective-permute-start.11 = (f32[128,2,2,2,32]{0,4,3,2,1:T(8,128)S(1)}, f32[128,2,2,2,32]{0,4,3,2,1:T(8,128)S(1)}, u32[]{:S(2)}, u32[]{:S(2)}) collective-permute-start(f32[128,2,2,2,32]{0,4,3,2,1:T(8,128)S(1)} %fusion.90), channel_id=1, source_target_pairs={{0,16},{8,24},{16,0},{24,8},{32,48},{40,56},{48,32},{56,40},{64,80... | collective-permute-start | bytes 393224 | tf_op jit(solution)/shard_map/ppermute | solution.py:38
  120.9 46.1 %collective-permute-start.13 = (bf16[2,1024,128]{2,1,0:T(8,128)(2,1)S(1)}, bf16[2,1024,128]{2,1,0:T(8,128)(2,1)S(1)}, u32[]{:S(2)}, u32[]{:S(2)}) collective-permute-start(bf16[2,1024,128]{2,1,0:T(8,128)(2,1)S(1)} %pad_maximum_fusion.1), channel_id=1, source_target_pairs={{8,0},{16,8},{24,16},{32,24},{40,32},{48,40},{56,48},{64,56},{72,6... | collective-permute-start | bytes 1572872 | tf_op jit(solution)/shard_map/ppermute | solution.py:18
  123.3 11.7 %collective-permute-start.12 = (f32[128,2,2,32]{0,3,2,1:T(8,128)S(1)}, f32[128,2,2,32]{0,3,2,1:T(8,128)S(1)}, u32[]{:S(2)}, u32[]{:S(2)}) collective-permute-start(f32[128,2,2,32]{0,3,2,1:T(8,128)S(1)} %fusion.91), channel_id=1, source_target_pairs={{0,32},{8,40},{16,48},{24,56},{32,0},{40,8},{48,16},{56,24},{64,96... | collective-permute-start | bytes 196616 | tf_op jit(solution)/shard_map/ppermute | solution.py:38
  129.0 12.2 %copy-start.16 = (f32[1024,1024]{0,1:T(8,128)S(1)}, f32[1024,1024]{0,1:T(8,128)}, u32[]{:S(2)}) copy-start(f32[1024,1024]{0,1:T(8,128)} %copy-done.15) | copy-start | bytes 12582916
  129.1 37.9 %collective-permute-start.14 = (bf16[2,1024,128]{2,1,0:T(8,128)(2,1)S(1)}, bf16[2,1024,128]{2,1,0:T(8,128)(2,1)S(1)}, u32[]{:S(2)}, u32[]{:S(2)}) collective-permute-start(bf16[2,1024,128]{2,1,0:T(8,128)(2,1)S(1)} %pad_maximum_fusion.2), channel_id=1, source_target_pairs={{16,0},{24,8},{32,16},{40,24},{48,32},{56,40},{64,48},{72,56},{80,... | collective-permute-start | bytes 1572872 | tf_op jit(solution)/shard_map/ppermute | solution.py:18
  135.1 16.3 %collective-permute-start.16 = (f32[128,2,32]{0,2,1:T(8,128)S(1)}, f32[128,2,32]{0,2,1:T(8,128)S(1)}, u32[]{:S(2)}, u32[]{:S(2)}) collective-permute-start(f32[128,2,32]{0,2,1:T(8,128)S(1)} %fusion.92), channel_id=1, source_target_pairs={{0,64},{8,72},{16,80},{24,88},{32,96},{40,104},{48,112},{56,120},{... | collective-permute-start | bytes 98312 | tf_op jit(solution)/shard_map/ppermute | solution.py:38
  145.9 21.2 %copy-start.20 = (f32[1,1024,128]{2,1,0:T(8,128)S(1)}, f32[1,1024,128]{2,1,0:T(8,128)}, u32[]{:S(2)}) copy-start(f32[1,1024,128]{2,1,0:T(8,128)} %convolution_bitcast_fusion) | copy-start | bytes 1572868
  145.9 21.1 %collective-permute-start.15 = (bf16[2,1024,128]{2,1,0:T(8,128)(2,1)S(1)}, bf16[2,1024,128]{2,1,0:T(8,128)(2,1)S(1)}, u32[]{:S(2)}, u32[]{:S(2)}) collective-permute-start(bf16[2,1024,128]{2,1,0:T(8,128)(2,1)S(1)} %pad_maximum_fusion.3), channel_id=1, source_target_pairs={{24,0},{32,8},{40,16},{48,24},{56,32},{64,40},{72,48},{80,56},{88,... | collective-permute-start | bytes 1572872 | tf_op jit(solution)/shard_map/ppermute | solution.py:18
  151.4 15.0 %collective-permute-start.17 = (f32[128,32]{0,1:T(8,128)S(1)}, f32[128,32]{0,1:T(8,128)S(1)}, u32[]{:S(2)}, u32[]{:S(2)}) collective-permute-start(f32[128,32]{0,1:T(8,128)S(1)} %select_bitcast_fusion.1), channel_id=1, source_target_pairs={{0,128},{8,136},{16,144},{24,152},{32,160},{40,168},{48,176},{56,1... | collective-permute-start | bytes 49160 | tf_op jit(solution)/shard_map/ppermute | solution.py:38
  (22 other events, 127.3 us)

commit v4 on v3

--- a/solution.py
+++ b/solution.py
@@ -89,13 +89,25 @@
     mixed = (normed * gate_heads).astype(jnp.bfloat16).reshape(row_count, feature_count)
     head_devices = lax.axis_size("head")
     head_index = lax.axis_index("head")
-    gathered_blocks = [grad_out] + [
-        lax.ppermute(grad_out, "head", [(i, (i + k) % head_devices) for i in range(head_devices)])
-        for k in range(1, head_devices)
+    partner = lax.ppermute(grad_out, "head", [(i, i ^ 1) for i in range(head_devices)])
+    own_first = head_index % 2 == 0
+    pair_block = jnp.where(
+        own_first,
+        jnp.concatenate([grad_out, partner], axis=1),
+        jnp.concatenate([partner, grad_out], axis=1),
+    )
+    pair_count = head_devices // 2
+    pair_index = head_index // 2
+    gathered_blocks = [pair_block] + [
+        lax.ppermute(
+            pair_block, "head", [(i, (i + 2 * k) % head_devices) for i in range(head_devices)]
+        )
+        for k in range(1, pair_count)
     ]
     column_block = jnp.concatenate(gathered_blocks, axis=1)
     block_width = grad_out.shape[1]
-    source_block = (head_index - jnp.arange(head_devices)) % head_devices
+    slot = jnp.arange(head_devices)
+    source_block = 2 * ((pair_index - slot // 2) % pair_count) + slot % 2
     w_blocks = w_out.reshape(w_out.shape[0], head_devices, block_width)
     w_in_order = jnp.take(w_blocks, source_block, axis=1).reshape(w_out.shape)
     grad_mixed = lax.dot_general(
@@ -104,9 +116,8 @@
     product = lax.dot_general(
         mixed, column_block, (((0,), (0,)), ((), ())), preferred_element_type=jnp.float32
     )
-    gather_back = (head_index - jnp.arange(head_devices)) % head_devices
     weight_rows = jnp.take(
-        product.reshape(product.shape[0], head_devices, block_width), gather_back, axis=1
+        product.reshape(product.shape[0], head_devices, block_width), source_block, axis=1
     ).reshape(product.shape)
     halving = halving_start(weight_rows, "seq")
     halving_levels = lax.axis_size("seq").bit_length() - 1

time: 169 us -> 144 us (0.85)
  the two profiles are of different devices: /device:TPU:51 before, /device:TPU:1 now
where the time goes in v4:
time: 144 us; the launch traced here: 142 us
  matrix products  47 us (33%)
  starting transfers between devices  40.3 us (28%)
  waiting for transfers between devices  31.3 us (22%)
  local copies, waits for them, and re-layouts  12.4 us (9%)
  other arithmetic  8.32 us (6%)
  between operations  2.17 us (2%)
    ppermute x6, starting transfers between devices, shifted(): return lax.ppermute(block, axis, route)  17 us
    ppermute x1, waiting for transfers between devices, per_device(): lax.ppermute(grad_out, 'head', [(i, i ^ 1) for i in range(head_devices)])  16.3 us
    ppermute x5, starting transfers between devices, halving_step(): return keep + lax.ppermute(send, axis, [(i, i ^ bit) for i in range(count)])  15.7 us
    dot_general x4, matrix products, pair_scores(): jnp.einsum('ihd,jhd->hij', query_heads, k_heads, preferred_element_type=j...  14.2 us
    dot_general x4, matrix products, per_device(): jnp.einsum('ihd,jhd->hij', grad_attended, v_heads, preferred_element_type...  13.7 us
    ppermute x5, waiting for transfers between devices, halving_step(): return keep + lax.ppermute(send, axis, [(i, i ^ bit) for i in range(count)])  7.68 us
    unnamed x69, local copies, waits for them, and re-layouts  6.94 us
    ppermute x3, starting transfers between devices, per_device(): lax.ppermute(pair_block, 'head', [(i, (i + 2 * k) % head_devices) for i i...  4.89 us
  transfers between devices with their start and end apart: 15, of which 5 were waited for; matrix products, arithmetic and copies ran while one was open for 36% of the time, Pallas kernels for 0%

profile of v4, /device:TPU:1, one launch (start us, length us, event | category | flops | bytes accessed | tf_op | source)
XLA Modules:
  0.0 141.5 jit_solution(2147328754416986987)
XLA Ops:
  2.5 5.0 %collective-permute-start.6 = (bf16[2056,128]{1,0:T(8,128)(2,1)S(1)}, bf16[2056,128]{1,0:T(8,128)(2,1)S(1)}, u32[]{:S(2)}, u32[]{:S(2)}) collective-permute-start(bf16[2056,128]{1,0:T(8,128)(2,1)S(1)} %pad_maximum_fusion.1), channel_id=1, source_target_pairs={{0,24},{8,32},{16,40},{24,48},{32,56},{40,64},{48,72},{56,80},{64,... | collective-permute-start | bytes 1579016 | tf_op jit(solution)/shard_map/ppermute | solution.py:18
  7.5 3.2 %collective-permute-start.5 = (bf16[2056,128]{1,0:T(8,128)(2,1)S(1)}, bf16[2056,128]{1,0:T(8,128)(2,1)S(1)}, u32[]{:S(2)}, u32[]{:S(2)}) collective-permute-start(bf16[2056,128]{1,0:T(8,128)(2,1)S(1)} %pad_maximum_fusion.1), channel_id=1, source_target_pairs={{0,16},{8,24},{16,32},{24,40},{32,48},{40,56},{48,64},{56,72},{64,... | collective-permute-start | bytes 1579016 | tf_op jit(solution)/shard_map/ppermute | solution.py:18
  10.7 3.1 %collective-permute-start.4 = (bf16[2056,128]{1,0:T(8,128)(2,1)S(1)}, bf16[2056,128]{1,0:T(8,128)(2,1)S(1)}, u32[]{:S(2)}, u32[]{:S(2)}) collective-permute-start(bf16[2056,128]{1,0:T(8,128)(2,1)S(1)} %pad_maximum_fusion.1), channel_id=1, source_target_pairs={{0,8},{8,16},{16,24},{24,32},{32,40},{40,48},{48,56},{56,64},{64,7... | collective-permute-start | bytes 1579016 | tf_op jit(solution)/shard_map/ppermute | solution.py:18
  13.7 2.7 %collective-permute-start = (bf16[1024,128]{1,0:T(8,128)(2,1)}, bf16[1024,128]{1,0:T(8,128)(2,1)}, u32[]{:S(2)}, u32[]{:S(2)}) collective-permute-start(bf16[1024,128]{1,0:T(8,128)(2,1)} %param.14), channel_id=1, source_target_pairs={{0,1},{1,0},{2,3},{3,2},{4,5},{5,4},{6,7},{7,6},{8,9},{9,8},{10,11... | collective-permute-start | bytes 786440 | tf_op jit(solution)/shard_map/ppermute | solution.py:92
  16.5 3.7 %fusion.113 = f32[1024,1024]{1,0:T(8,128)} fusion(bf16[1024,128]{1,0:T(8,128)(2,1)S(1)} %copy-done, bf16[1024,128]{1,0:T(8,128)(2,1)} %param.9), kind=kOutput, calls=%fused_computation.213 | convolution fusion | flops 268435456 | bytes 4718592 | tf_op jit(solution)/shard_map/ihd,jhd->hij/dot_general | solution.py:75
  22.6 16.3 %collective-permute-done = bf16[1024,128]{1,0:T(8,128)(2,1)} collective-permute-done((bf16[1024,128]{1,0:T(8,128)(2,1)}, bf16[1024,128]{1,0:T(8,128)(2,1)}, u32[]{:S(2)}, u32[]{:S(2)}) %collective-permute-start) | collective-permute-done | bytes 262176 | tf_op jit(solution)/shard_map/ppermute | solution.py:92
  41.6 2.5 %collective-permute-start.2 = (bf16[1024,256]{1,0:T(8,128)(2,1)S(1)}, bf16[1024,256]{1,0:T(8,128)(2,1)S(1)}, u32[]{:S(2)}, u32[]{:S(2)}) collective-permute-start(bf16[1024,256]{1,0:T(8,128)(2,1)S(1)} %maximum_select_fusion), channel_id=1, source_target_pairs={{0,4},{1,5},{2,6},{3,7},{4,0},{5,1},{6,2},{7,3},{8,12},{9,13},{10,... | collective-permute-start | bytes 1572872 | tf_op jit(solution)/shard_map/ppermute | solution.py:102
  46.7 2.0 %copy-done.11 = f32[1024,1024]{1,0:T(8,128)S(1)} copy-done((f32[1024,1024]{1,0:T(8,128)S(1)}, f32[1024,1024]{1,0:T(8,128)}, u32[]{:S(2)}) %copy-start.11) | copy-done | bytes 4194328
  48.7 9.1 %fusion.26 = (bf16[1024,1024]{1,0:T(8,128)(2,1)S(1)}, bf16[1024,1024]{1,0:T(8,128)(2,1)S(1)}, bf16[1024,1024]{1,0:T(8,128)(2,1)S(1)}, bf16[1024,1024]{1,0:T(8,128)(2,1)S(1)}, f32[1024,1024]{0,1:T(8,128)}) fusion(s32[1024]{0:T(1024)S(1)} %fusion.101, f32[]{:T(128)} %bitcast.363, pred[]{:T(512)S(6)} %ge.26, s32[1024]{0:T(1024)S(1)} %copy-done.31, ...), kind=kOutput, calls=%fused_computation.37 | convolution fusion | flops 312475648 | bytes 25711620 | tf_op jit(solution)/shard_map/ihd,jhd->hij/dot_general | solution.py:75
  62.1 2.9 %collective-permute-done.2 = bf16[1024,256]{1,0:T(8,128)(2,1)S(1)} collective-permute-done((bf16[1024,256]{1,0:T(8,128)(2,1)S(1)}, bf16[1024,256]{1,0:T(8,128)(2,1)S(1)}, u32[]{:S(2)}, u32[]{:S(2)}) %collective-permute-start.2) | collective-permute-done | bytes 524320 | tf_op jit(solution)/shard_map/ppermute | solution.py:102
  67.3 2.6 %copy.76 = bf16[1024,1024]{1,0:T(8,128)(2,1)} copy(bf16[1024,1024]{0,1:T(8,128)(2,1)S(1)} %fusion.55) | data formatting | bytes 4194304 | tf_op jit(solution)/shard_map/dot_general | solution.py:116
  69.9 2.5 %fusion.58 = f32[128,8,128]{2,0,1:T(8,128)S(1)} fusion(bf16[8,128,1024]{2,1,0:T(8,128)(2,1)} %bitcast.366, bf16[1024,128]{0,1:T(8,128)(2,1)S(1)} %copy.68, f32[128,1024]{1,0:T(8,128)S(1)} %get-tuple-element.42, f32[1024]{0:T(1024)S(1)} %add_rsqrt_fusion, f32[1024]{0:T(1024)S(1)} %broadcast_multiply_fusion.1), kind=kOutput, calls=%fused_computation.108 | convolution fusion | flops 269090816 | bytes 3416064 | tf_op jit(solution)/shard_map/dot_general | solution.py:116
  75.2 5.1 %select_convert_fusion = bf16[1024,1024]{1,0:T(8,128)(2,1)S(1)} fusion(f32[1024,1024]{1,0:T(8,128)} %fusion.113, bf16[1024,128]{1,0:T(8,128)(2,1)S(1)} %copy-done.26, f32[]{:T(128)} %bitcast.362, s32[1024]{0:T(1024)S(1)} %copy-done.31, pred[]{:T(512)S(6)} %ge.24, bf16[1024,1,128]{0,2,1:T(8,128)(2,1)S(1)} %get-tuple-element.15), kind=kOutput, calls=%fused_computation.44 | convolution fusion | flops 286261248 | bytes 6819845 | tf_op jit(solution)/shard_map/ihd,jhd->hij/dot_general | solution.py:148
  83.6 2.0 %copy.101 = f32[1024,128]{1,0:T(8,128)} copy(f32[1024,128]{0,1:T(8,128)} %get-tuple-element.32) | data formatting | bytes 1048576
  88.1 2.9 %fusion.32 = bf16[1024,1024]{1,0:T(8,128)(2,1)S(1)} fusion(f32[1024,1024]{0,1:T(8,128)S(1)} %copy-done.32, s32[1024]{0:T(1024)S(1)} %fusion.101, f32[]{:T(128)} %bitcast.361, pred[]{:T(512)S(6)} %ge.26, s32[1024]{0:T(1024)S(1)} %copy-done.31, bf16[1024,1,128]{0,2,1:T(8,128)(2,1)S(1)} %get-tuple-element.15, bf16[2056,128]{1,0:T(8,128)(2,1)S(1)} %copy-done.28), kind=kOutput, calls=%fused_computation.43 | convolution fusion | flops 284164096 | bytes 6823941 | tf_op jit(solution)/shard_map/ihd,jhd->hij/dot_general | solution.py:148
  93.5 2.5 %collective-permute-start.10 = (bf16[2,1024,128]{2,1,0:T(8,128)(2,1)S(1)}, bf16[2,1024,128]{2,1,0:T(8,128)(2,1)S(1)}, u32[]{:S(2)}, u32[]{:S(2)}) collective-permute-start(bf16[2,1024,128]{2,1,0:T(8,128)(2,1)S(1)} %pad_maximum_fusion.2), channel_id=1, source_target_pairs={{8,0},{16,8},{24,16},{32,24},{40,32},{48,40},{56,48},{64,56},{72,6... | collective-permute-start | bytes 1572872 | tf_op jit(solution)/shard_map/ppermute | solution.py:18
  96.2 9.3 %collective-permute-start.9 = (f32[128,2,2,32]{0,3,2,1:T(8,128)S(1)}, f32[128,2,2,32]{0,3,2,1:T(8,128)S(1)}, u32[]{:S(2)}, u32[]{:S(2)}) collective-permute-start(f32[128,2,2,32]{0,3,2,1:T(8,128)S(1)} %fusion.93), channel_id=1, source_target_pairs={{0,32},{8,40},{16,48},{24,56},{32,0},{40,8},{48,16},{56,24},{64,96... | collective-permute-start | bytes 196616 | tf_op jit(solution)/shard_map/ppermute | solution.py:38
  106.4 2.9 %fusion.21 = bf16[1024,1024]{1,0:T(8,128)(2,1)S(1)} fusion(f32[1024,1024]{0,1:T(8,128)S(1)} %copy-done.15, s32[1024]{0:T(1024)S(1)} %fusion.100, f32[]{:T(128)} %bitcast.365, pred[]{:T(512)S(6)} %ge.27, s32[1024]{0:T(1024)S(1)} %copy-done.31, bf16[1024,1,128]{0,2,1:T(8,128)(2,1)S(1)} %get-tuple-element.15, bf16[2056,128]{1,0:T(8,128)(2,1)S(1)} %copy-done.24), kind=kOutput, calls=%fused_computation.29 | convolution fusion | flops 284164096 | bytes 6823941 | tf_op jit(solution)/shard_map/ihd,jhd->hij/dot_general | solution.py:148
  112.8 4.0 %collective-permute-start.13 = (f32[128,2,32]{0,2,1:T(8,128)S(1)}, f32[128,2,32]{0,2,1:T(8,128)S(1)}, u32[]{:S(2)}, u32[]{:S(2)}) collective-permute-start(f32[128,2,32]{0,2,1:T(8,128)S(1)} %fusion.94), channel_id=1, source_target_pairs={{0,64},{8,72},{16,80},{24,88},{32,96},{40,104},{48,112},{56,120},{... | collective-permute-start | bytes 98312 | tf_op jit(solution)/shard_map/ppermute | solution.py:38
  117.8 2.9 %fusion.10 = bf16[1024,1024]{1,0:T(8,128)(2,1)S(1)} fusion(f32[1024,1024]{0,1:T(8,128)S(1)} %copy-done.13, s32[1024]{0:T(1024)S(1)} %fusion.99, f32[]{:T(128)} %bitcast.364, pred[]{:T(512)S(6)} %ge.28, s32[1024]{0:T(1024)S(1)} %copy-done.31, bf16[1024,1,128]{0,2,1:T(8,128)(2,1)S(1)} %get-tuple-element.15, bf16[2056,128]{1,0:T(8,128)(2,1)S(1)} %copy-done.22), kind=kOutput, calls=%fused_computation.15 | convolution fusion | flops 284164096 | bytes 6823941 | tf_op jit(solution)/shard_map/ihd,jhd->hij/dot_general | solution.py:148
  123.7 4.9 %collective-permute-done.13 = f32[128,2,32]{0,2,1:T(8,128)S(1)} collective-permute-done((f32[128,2,32]{0,2,1:T(8,128)S(1)}, f32[128,2,32]{0,2,1:T(8,128)S(1)}, u32[]{:S(2)}, u32[]{:S(2)}) %collective-permute-start.13) | collective-permute-done | bytes 32800 | tf_op jit(solution)/shard_map/ppermute | solution.py:38
  128.7 2.3 %collective-permute-start.14 = (f32[128,32]{0,1:T(8,128)S(1)}, f32[128,32]{0,1:T(8,128)S(1)}, u32[]{:S(2)}, u32[]{:S(2)}) collective-permute-start(f32[128,32]{0,1:T(8,128)S(1)} %select_bitcast_fusion.1), channel_id=1, source_target_pairs={{0,128},{8,136},{16,144},{24,152},{32,160},{40,168},{48,176},{56,1... | collective-permute-start | bytes 49160 | tf_op jit(solution)/shard_map/ppermute | solution.py:38
  132.5 2.7 %collective-permute-done.14 = f32[128,32]{0,1:T(8,128)S(1)} collective-permute-done((f32[128,32]{0,1:T(8,128)S(1)}, f32[128,32]{0,1:T(8,128)S(1)}, u32[]{:S(2)}, u32[]{:S(2)}) %collective-permute-start.14) | collective-permute-done | bytes 16416 | tf_op jit(solution)/shard_map/ppermute | solution.py:38
  135.9 4.4 %collective-permute-done.12 = bf16[2,1024,128]{2,1,0:T(8,128)(2,1)S(1)} collective-permute-done((bf16[2,1024,128]{2,1,0:T(8,128)(2,1)S(1)}, bf16[2,1024,128]{2,1,0:T(8,128)(2,1)S(1)}, u32[]{:S(2)}, u32[]{:S(2)}) %collective-permute-start.12) | collective-permute-done | bytes 524320 | tf_op jit(solution)/shard_map/ppermute | solution.py:18
  (142 shorter events, 37.8 us)
Async XLA Ops:
  0.6 15.9 %copy-start = (bf16[1024,128]{1,0:T(8,128)(2,1)S(1)}, bf16[1024,128]{1,0:T(8,128)(2,1)}, u32[]{:S(2)}) copy-start(bf16[1024,128]{1,0:T(8,128)(2,1)} %param.8) | copy-start | bytes 786436
  0.6 20.4 %copy-start.29 = (bf16[128,1024]{1,0:T(8,128)(2,1)S(1)}, bf16[128,1024]{1,0:T(8,128)(2,1)}, u32[]{:S(2)}) copy-start(bf16[128,1024]{1,0:T(8,128)(2,1)} %param.15) | copy-start | bytes 786436
  0.7 21.6 %copy-start.30 = (bf16[1024,128]{1,0:T(8,128)(2,1)S(1)}, bf16[1024,128]{1,0:T(8,128)(2,1)}, u32[]{:S(2)}) copy-start(bf16[1024,128]{1,0:T(8,128)(2,1)} %param.11) | copy-start | bytes 786436
  2.5 41.5 %collective-permute-start.6 = (bf16[2056,128]{1,0:T(8,128)(2,1)S(1)}, bf16[2056,128]{1,0:T(8,128)(2,1)S(1)}, u32[]{:S(2)}, u32[]{:S(2)}) collective-permute-start(bf16[2056,128]{1,0:T(8,128)(2,1)S(1)} %pad_maximum_fusion.1), channel_id=1, source_target_pairs={{0,24},{8,32},{16,40},{24,48},{32,56},{40,64},{48,72},{56,80},{64,... | collective-permute-start | bytes 1579016 | tf_op jit(solution)/shard_map/ppermute | solution.py:18
  7.5 38.4 %collective-permute-start.5 = (bf16[2056,128]{1,0:T(8,128)(2,1)S(1)}, bf16[2056,128]{1,0:T(8,128)(2,1)S(1)}, u32[]{:S(2)}, u32[]{:S(2)}) collective-permute-start(bf16[2056,128]{1,0:T(8,128)(2,1)S(1)} %pad_maximum_fusion.1), channel_id=1, source_target_pairs={{0,16},{8,24},{16,32},{24,40},{32,48},{40,56},{48,64},{56,72},{64,... | collective-permute-start | bytes 1579016 | tf_op jit(solution)/shard_map/ppermute | solution.py:18
  10.7 36.0 %collective-permute-start.4 = (bf16[2056,128]{1,0:T(8,128)(2,1)S(1)}, bf16[2056,128]{1,0:T(8,128)(2,1)S(1)}, u32[]{:S(2)}, u32[]{:S(2)}) collective-permute-start(bf16[2056,128]{1,0:T(8,128)(2,1)S(1)} %pad_maximum_fusion.1), channel_id=1, source_target_pairs={{0,8},{8,16},{16,24},{24,32},{32,40},{40,48},{48,56},{56,64},{64,7... | collective-permute-start | bytes 1579016 | tf_op jit(solution)/shard_map/ppermute | solution.py:18
  13.7 25.2 %collective-permute-start = (bf16[1024,128]{1,0:T(8,128)(2,1)}, bf16[1024,128]{1,0:T(8,128)(2,1)}, u32[]{:S(2)}, u32[]{:S(2)}) collective-permute-start(bf16[1024,128]{1,0:T(8,128)(2,1)} %param.14), channel_id=1, source_target_pairs={{0,1},{1,0},{2,3},{3,2},{4,5},{5,4},{6,7},{7,6},{8,9},{9,8},{10,11... | collective-permute-start | bytes 786440 | tf_op jit(solution)/shard_map/ppermute | solution.py:92
  40.3 21.8 %collective-permute-start.1 = (bf16[1024,256]{1,0:T(8,128)(2,1)S(1)}, bf16[1024,256]{1,0:T(8,128)(2,1)S(1)}, u32[]{:S(2)}, u32[]{:S(2)}) collective-permute-start(bf16[1024,256]{1,0:T(8,128)(2,1)S(1)} %maximum_select_fusion), channel_id=1, source_target_pairs={{0,2},{1,3},{2,4},{3,5},{4,6},{5,7},{6,0},{7,1},{8,10},{9,11},{10,... | collective-permute-start | bytes 1572872 | tf_op jit(solution)/shard_map/ppermute | solution.py:102
  41.6 23.5 %collective-permute-start.2 = (bf16[1024,256]{1,0:T(8,128)(2,1)S(1)}, bf16[1024,256]{1,0:T(8,128)(2,1)S(1)}, u32[]{:S(2)}, u32[]{:S(2)}) collective-permute-start(bf16[1024,256]{1,0:T(8,128)(2,1)S(1)} %maximum_select_fusion), channel_id=1, source_target_pairs={{0,4},{1,5},{2,6},{3,7},{4,0},{5,1},{6,2},{7,3},{8,12},{9,13},{10,... | collective-permute-start | bytes 1572872 | tf_op jit(solution)/shard_map/ppermute | solution.py:102
  44.0 14.7 %copy-start.21 = (bf16[2056,128]{1,0:T(8,128)(2,1)}, bf16[2056,128]{1,0:T(8,128)(2,1)S(1)}, u32[]{:S(2)}) copy-start(bf16[2056,128]{1,0:T(8,128)(2,1)S(1)} %collective-permute-done.6) | copy-start | bytes 1579012
  44.0 21.0 %collective-permute-start.3 = (bf16[1024,256]{1,0:T(8,128)(2,1)S(1)}, bf16[1024,256]{1,0:T(8,128)(2,1)S(1)}, u32[]{:S(2)}, u32[]{:S(2)}) collective-permute-start(bf16[1024,256]{1,0:T(8,128)(2,1)S(1)} %maximum_select_fusion), channel_id=1, source_target_pairs={{0,6},{1,7},{2,0},{3,1},{4,2},{5,3},{6,4},{7,5},{8,14},{9,15},{10,... | collective-permute-start | bytes 1572872 | tf_op jit(solution)/shard_map/ppermute | solution.py:102
  46.7 13.8 %copy-start.27 = (bf16[2056,128]{1,0:T(8,128)(2,1)}, bf16[2056,128]{1,0:T(8,128)(2,1)S(1)}, u32[]{:S(2)}) copy-start(bf16[2056,128]{1,0:T(8,128)(2,1)S(1)} %collective-permute-done.4) | copy-start | bytes 1579012
  74.2 12.2 %collective-permute-start.7 = (f32[128,2,2,2,2,32]{0,5,4,3,2,1:T(8,128)}, f32[128,2,2,2,2,32]{0,5,4,3,2,1:T(8,128)}, u32[]{:S(2)}, u32[]{:S(2)}) collective-permute-start(f32[128,2,2,2,2,32]{0,5,4,3,2,1:T(8,128)} %select_bitcast_fusion), channel_id=1, source_target_pairs={{0,8},{8,0},{16,24},{24,16},{32,40},{40,32},{48,56},{56,48},{64,72... | collective-permute-start | bytes 786440 | tf_op jit(solution)/shard_map/ppermute | solution.py:38
  87.8 8.3 %collective-permute-start.8 = (f32[128,2,2,2,32]{0,4,3,2,1:T(8,128)S(1)}, f32[128,2,2,2,32]{0,4,3,2,1:T(8,128)S(1)}, u32[]{:S(2)}, u32[]{:S(2)}) collective-permute-start(f32[128,2,2,2,32]{0,4,3,2,1:T(8,128)S(1)} %fusion.92), channel_id=1, source_target_pairs={{0,16},{8,24},{16,0},{24,8},{32,48},{40,56},{48,32},{56,40},{64,80... | collective-permute-start | bytes 393224 | tf_op jit(solution)/shard_map/ppermute | solution.py:38
  91.0 14.5 %copy-start.6 = (bf16[1024,1024]{1,0:T(8,128)(2,1)S(1)}, bf16[1024,1024]{1,0:T(8,128)(2,1)}, u32[]{:S(2)}) copy-start(bf16[1024,1024]{1,0:T(8,128)(2,1)} %copy-done.5) | copy-start | bytes 6291460
  92.5 13.9 %copy-start.15 = (f32[1024,1024]{0,1:T(8,128)S(1)}, f32[1024,1024]{0,1:T(8,128)}, u32[]{:S(2)}) copy-start(f32[1024,1024]{0,1:T(8,128)} %copy-done.14) | copy-start | bytes 12582916
  92.5 13.9 %copy-start.24 = (bf16[2056,128]{1,0:T(8,128)(2,1)S(1)}, bf16[2056,128]{1,0:T(8,128)(2,1)}, u32[]{:S(2)}) copy-start(bf16[2056,128]{1,0:T(8,128)(2,1)} %copy-done.23) | copy-start | bytes 1579012
  93.5 42.3 %collective-permute-start.10 = (bf16[2,1024,128]{2,1,0:T(8,128)(2,1)S(1)}, bf16[2,1024,128]{2,1,0:T(8,128)(2,1)S(1)}, u32[]{:S(2)}, u32[]{:S(2)}) collective-permute-start(bf16[2,1024,128]{2,1,0:T(8,128)(2,1)S(1)} %pad_maximum_fusion.2), channel_id=1, source_target_pairs={{8,0},{16,8},{24,16},{32,24},{40,32},{48,40},{56,48},{64,56},{72,6... | collective-permute-start | bytes 1572872 | tf_op jit(solution)/shard_map/ppermute | solution.py:18
  96.2 16.6 %collective-permute-start.9 = (f32[128,2,2,32]{0,3,2,1:T(8,128)S(1)}, f32[128,2,2,32]{0,3,2,1:T(8,128)S(1)}, u32[]{:S(2)}, u32[]{:S(2)}) collective-permute-start(f32[128,2,2,32]{0,3,2,1:T(8,128)S(1)} %fusion.93), channel_id=1, source_target_pairs={{0,32},{8,40},{16,48},{24,56},{32,0},{40,8},{48,16},{56,24},{64,96... | collective-permute-start | bytes 196616 | tf_op jit(solution)/shard_map/ppermute | solution.py:38
  110.2 25.7 %collective-permute-start.11 = (bf16[2,1024,128]{2,1,0:T(8,128)(2,1)S(1)}, bf16[2,1024,128]{2,1,0:T(8,128)(2,1)S(1)}, u32[]{:S(2)}, u32[]{:S(2)}) collective-permute-start(bf16[2,1024,128]{2,1,0:T(8,128)(2,1)S(1)} %pad_maximum_fusion.3), channel_id=1, source_target_pairs={{16,0},{24,8},{32,16},{40,24},{48,32},{56,40},{64,48},{72,56},{80,... | collective-permute-start | bytes 1572872 | tf_op jit(solution)/shard_map/ppermute | solution.py:18
  112.8 15.9 %collective-permute-start.13 = (f32[128,2,32]{0,2,1:T(8,128)S(1)}, f32[128,2,32]{0,2,1:T(8,128)S(1)}, u32[]{:S(2)}, u32[]{:S(2)}) collective-permute-start(f32[128,2,32]{0,2,1:T(8,128)S(1)} %fusion.94), channel_id=1, source_target_pairs={{0,64},{8,72},{16,80},{24,88},{32,96},{40,104},{48,112},{56,120},{... | collective-permute-start | bytes 98312 | tf_op jit(solution)/shard_map/ppermute | solution.py:38
  121.5 18.8 %copy-start.17 = (f32[1,1024,128]{2,1,0:T(8,128)S(1)}, f32[1,1024,128]{2,1,0:T(8,128)}, u32[]{:S(2)}) copy-start(f32[1,1024,128]{2,1,0:T(8,128)} %convolution_bitcast_fusion) | copy-start | bytes 1572868
  121.5 18.7 %collective-permute-start.12 = (bf16[2,1024,128]{2,1,0:T(8,128)(2,1)S(1)}, bf16[2,1024,128]{2,1,0:T(8,128)(2,1)S(1)}, u32[]{:S(2)}, u32[]{:S(2)}) collective-permute-start(bf16[2,1024,128]{2,1,0:T(8,128)(2,1)S(1)} %pad_maximum_fusion.4), channel_id=1, source_target_pairs={{24,0},{32,8},{40,16},{48,24},{56,32},{64,40},{72,48},{80,56},{88,... | collective-permute-start | bytes 1572872 | tf_op jit(solution)/shard_map/ppermute | solution.py:18
  128.7 6.6 %collective-permute-start.14 = (f32[128,32]{0,1:T(8,128)S(1)}, f32[128,32]{0,1:T(8,128)S(1)}, u32[]{:S(2)}, u32[]{:S(2)}) collective-permute-start(f32[128,32]{0,1:T(8,128)S(1)} %select_bitcast_fusion.1), channel_id=1, source_target_pairs={{0,128},{8,136},{16,144},{24,152},{32,160},{40,168},{48,176},{56,1... | collective-permute-start | bytes 49160 | tf_op jit(solution)/shard_map/ppermute | solution.py:38
  (24 other events, 131.0 us)

commit v5 on v4

--- a/solution.py
+++ b/solution.py
@@ -23,6 +23,25 @@
     rows, cols = block.shape
     levels = count.bit_length() - 1
     return block.reshape((rows,) + (2,) * levels + (cols // count,))
+
+
+def radix_finish(current, axis, levels_done):
+    count = lax.axis_size(axis)
+    my_index = lax.axis_index(axis)
+    low_count = 1 << levels_done
+    high_count = count // low_count
+    rows = current.shape[0]
+    chunks = current.reshape(rows, high_count, -1)
+    high = my_index // low_count
+    rolled = jnp.take(chunks, (high + jnp.arange(high_count)) % high_count, axis=1)
+    total = rolled[:, 0]
+    for shift in range(1, high_count):
+        route = [
+            (i, ((i // low_count + shift) % high_count) * low_count + i % low_count)
+            for i in range(count)
+        ]
+        total = total + lax.ppermute(rolled[:, shift], axis, route)
+    return total
 
 
 def halving_step(current, axis, level):
@@ -120,7 +139,7 @@
         product.reshape(product.shape[0], head_devices, block_width), source_block, axis=1
     ).reshape(product.shape)
     halving = halving_start(weight_rows, "seq")
-    halving_levels = lax.axis_size("seq").bit_length() - 1
+    halving_levels = min(2, lax.axis_size("seq").bit_length() - 1)
     grad_mixed = grad_mixed.reshape(row_count, head_count, DH)
     grad_gates = (grad_mixed * normed).reshape(row_count, feature_count)
     grad_normed = grad_mixed * gate_heads
@@ -133,11 +152,16 @@
     grad_queries = jnp.zeros((row_count, head_count, DH), jnp.float32)
     key_terms = []
     done_levels = 0
+    grad_w_out = None
     for window_index in range(4):
-        if window_index > 0 and done_levels < halving_levels:
-            halving = halving_step(halving, "seq", done_levels)
-            done_levels += 1
-            halving, grad_attended = lax.optimization_barrier((halving, grad_attended))
+        if window_index > 0:
+            if done_levels < halving_levels:
+                halving = halving_step(halving, "seq", done_levels)
+                done_levels += 1
+                halving, grad_attended = lax.optimization_barrier((halving, grad_attended))
+            elif grad_w_out is None:
+                grad_w_out = radix_finish(halving, "seq", done_levels)
+                grad_w_out, grad_attended = lax.optimization_barrier((grad_w_out, grad_attended))
         k_heads, v_heads, allowed = prepared[window_index]
         scores = pair_scores(q_heads, k_heads)
         key_act, key_deriv = silu_parts(scores)
@@ -174,7 +198,8 @@
     while done_levels < halving_levels:
         halving = halving_step(halving, "seq", done_levels)
         done_levels += 1
-    grad_w_out = halving.reshape(halving.shape[0], -1)
+    if grad_w_out is None:
+        grad_w_out = radix_finish(halving, "seq", done_levels)
     return (
         grad_queries.reshape(row_count, feature_count),
         summed[0],

time: 144 us -> 169 us (1.17)
  starting transfers between devices: 40.3 us -> 49.8 us
  waiting for transfers between devices: 31.3 us -> 39.4 us
  matrix products: 47 us -> 53.7 us
  local copies, waits for them, and re-layouts: 12.4 us -> 15.5 us
    ppermute x0 -> x7, starting transfers between devices: none -> 23.5 us  [radix_finish(): total = total + lax.ppermute(rolled[:, shift], axis, route)]
    ppermute x5 -> x2, starting transfers between devices: 15.7 us -> 0.1 us  [halving_step(): return keep + lax.ppermute(send, axis, [(i, i ^ bit) for i in range(count)])]
    ppermute x6, waiting for transfers between devices: 4.38 us -> 18.8 us  [shifted(): return lax.ppermute(block, axis, route)]
    ppermute x5 -> x2, waiting for transfers between devices: 7.68 us -> 1.35 us  [halving_step(): return keep + lax.ppermute(send, axis, [(i, i ^ bit) for i in range(count)])]
    dot_general x4, matrix products: 4.46 us -> 7.18 us  [per_device(): jnp.einsum('hij,jhd->ihd', grad_scores, k_heads, preferred_element_type=j...]
    unnamed x69 -> x79, local copies, waits for them, and re-layouts: 6.94 us -> 9.57 us
    add x5 -> x2, other arithmetic: 2.05 us -> 0.08 us  [halving_step(): return keep + lax.ppermute(send, axis, [(i, i ^ bit) for i in range(count)])]
  transfers between devices with their start and end apart: 15 -> 19, of which waited for: 5 -> 6; matrix products, arithmetic and copies ran while one was open for 36% -> 29% of each run, Pallas kernels for 0% -> 0%
where the time goes in v5:
time: 169 us; the launch traced here: 168 us
  matrix products  53.7 us (32%)
  starting transfers between devices  49.8 us (29%)
  waiting for transfers between devices  39.4 us (23%)
  local copies, waits for them, and re-layouts  15.5 us (9%)
  other arithmetic  7.64 us (5%)
  between operations  2.12 us (1%)
    ppermute x7, starting transfers between devices, radix_finish(): total = total + lax.ppermute(rolled[:, shift], axis, route)  23.5 us
    ppermute x6, waiting for transfers between devices, shifted(): return lax.ppermute(block, axis, route)  18.8 us
    ppermute x6, starting transfers between devices, shifted(): return lax.ppermute(block, axis, route)  18.5 us
    ppermute x1, waiting for transfers between devices, per_device(): lax.ppermute(grad_out, 'head', [(i, i ^ 1) for i in range(head_devices)])  16.3 us
    dot_general x4, matrix products, per_device(): jnp.einsum('ihd,jhd->hij', grad_attended, v_heads, preferred_element_type...  14.7 us
    dot_general x4, matrix products, pair_scores(): jnp.einsum('ihd,jhd->hij', query_heads, k_heads, preferred_element_type=j...  14.3 us
    unnamed x79, local copies, waits for them, and re-layouts  9.57 us
    dot_general x4, matrix products, per_device(): jnp.einsum('hij,jhd->ihd', grad_scores, k_heads, preferred_element_type=j...  7.18 us
  transfers between devices with their start and end apart: 19, of which 6 were waited for; matrix products, arithmetic and copies ran while one was open for 29% of the time, Pallas kernels for 0%

profile of v5, /device:TPU:1, one launch (start us, length us, event | category | flops | bytes accessed | tf_op | source)
XLA Modules:
  0.0 168.2 jit_solution(5417127872450691367)
XLA Ops:
  2.5 5.1 %collective-permute-start.6 = (bf16[2056,128]{1,0:T(8,128)(2,1)S(1)}, bf16[2056,128]{1,0:T(8,128)(2,1)S(1)}, u32[]{:S(2)}, u32[]{:S(2)}) collective-permute-start(bf16[2056,128]{1,0:T(8,128)(2,1)S(1)} %pad_maximum_fusion.1), channel_id=1, source_target_pairs={{0,24},{8,32},{16,40},{24,48},{32,56},{40,64},{48,72},{56,80},{64,... | collective-permute-start | bytes 1579016 | tf_op jit(solution)/shard_map/ppermute | solution.py:18
  7.6 3.2 %collective-permute-start.5 = (bf16[2056,128]{1,0:T(8,128)(2,1)S(1)}, bf16[2056,128]{1,0:T(8,128)(2,1)S(1)}, u32[]{:S(2)}, u32[]{:S(2)}) collective-permute-start(bf16[2056,128]{1,0:T(8,128)(2,1)S(1)} %pad_maximum_fusion.1), channel_id=1, source_target_pairs={{0,16},{8,24},{16,32},{24,40},{32,48},{40,56},{48,64},{56,72},{64,... | collective-permute-start | bytes 1579016 | tf_op jit(solution)/shard_map/ppermute | solution.py:18
  10.8 3.1 %collective-permute-start.4 = (bf16[2056,128]{1,0:T(8,128)(2,1)S(1)}, bf16[2056,128]{1,0:T(8,128)(2,1)S(1)}, u32[]{:S(2)}, u32[]{:S(2)}) collective-permute-start(bf16[2056,128]{1,0:T(8,128)(2,1)S(1)} %pad_maximum_fusion.1), channel_id=1, source_target_pairs={{0,8},{8,16},{16,24},{24,32},{32,40},{40,48},{48,56},{56,64},{64,7... | collective-permute-start | bytes 1579016 | tf_op jit(solution)/shard_map/ppermute | solution.py:18
  13.9 2.7 %collective-permute-start = (bf16[1024,128]{1,0:T(8,128)(2,1)}, bf16[1024,128]{1,0:T(8,128)(2,1)}, u32[]{:S(2)}, u32[]{:S(2)}) collective-permute-start(bf16[1024,128]{1,0:T(8,128)(2,1)} %param.14), channel_id=1, source_target_pairs={{0,1},{1,0},{2,3},{3,2},{4,5},{5,4},{6,7},{7,6},{8,9},{9,8},{10,11... | collective-permute-start | bytes 786440 | tf_op jit(solution)/shard_map/ppermute | solution.py:111
  16.6 3.7 %fusion.121 = f32[1024,1024]{1,0:T(8,128)} fusion(bf16[1024,128]{1,0:T(8,128)(2,1)S(1)} %copy-done, bf16[1024,128]{1,0:T(8,128)(2,1)} %param.9), kind=kOutput, calls=%fused_computation.233 | convolution fusion | flops 268435456 | bytes 4718592 | tf_op jit(solution)/shard_map/ihd,jhd->hij/dot_general | solution.py:94
  22.8 16.3 %collective-permute-done = bf16[1024,128]{1,0:T(8,128)(2,1)} collective-permute-done((bf16[1024,128]{1,0:T(8,128)(2,1)}, bf16[1024,128]{1,0:T(8,128)(2,1)}, u32[]{:S(2)}, u32[]{:S(2)}) %collective-permute-start) | collective-permute-done | bytes 262176 | tf_op jit(solution)/shard_map/ppermute | solution.py:111
  41.5 2.5 %collective-permute-start.2 = (bf16[1024,256]{1,0:T(8,128)(2,1)S(1)}, bf16[1024,256]{1,0:T(8,128)(2,1)S(1)}, u32[]{:S(2)}, u32[]{:S(2)}) collective-permute-start(bf16[1024,256]{1,0:T(8,128)(2,1)S(1)} %maximum_select_fusion), channel_id=1, source_target_pairs={{0,4},{1,5},{2,6},{3,7},{4,0},{5,1},{6,2},{7,3},{8,12},{9,13},{10,... | collective-permute-start | bytes 1572872 | tf_op jit(solution)/shard_map/ppermute | solution.py:121
  48.7 9.1 %fusion.26 = (bf16[1024,1024]{1,0:T(8,128)(2,1)S(1)}, bf16[1024,1024]{1,0:T(8,128)(2,1)S(1)}, bf16[1024,1024]{1,0:T(8,128)(2,1)S(1)}, bf16[1024,1024]{1,0:T(8,128)(2,1)S(1)}, f32[1024,1024]{0,1:T(8,128)}) fusion(s32[1024]{0:T(1024)S(1)} %fusion.106, f32[]{:T(128)} %bitcast.366, pred[]{:T(512)S(6)} %ge.33, s32[1024]{0:T(1024)S(1)} %copy-done.36, ...), kind=kOutput, calls=%fused_computation.38 | convolution fusion | flops 312475648 | bytes 25711620 | tf_op jit(solution)/shard_map/ihd,jhd->hij/dot_general | solution.py:94
  62.1 2.9 %collective-permute-done.2 = bf16[1024,256]{1,0:T(8,128)(2,1)S(1)} collective-permute-done((bf16[1024,256]{1,0:T(8,128)(2,1)S(1)}, bf16[1024,256]{1,0:T(8,128)(2,1)S(1)}, u32[]{:S(2)}, u32[]{:S(2)}) %collective-permute-start.2) | collective-permute-done | bytes 524320 | tf_op jit(solution)/shard_map/ppermute | solution.py:121
  67.2 2.6 %copy.75 = bf16[1024,1024]{1,0:T(8,128)(2,1)} copy(bf16[1024,1024]{0,1:T(8,128)(2,1)S(1)} %fusion.55) | data formatting | bytes 4194304 | tf_op jit(solution)/shard_map/dot_general | solution.py:135
  69.8 2.5 %fusion.58 = f32[128,8,128]{2,0,1:T(8,128)S(1)} fusion(bf16[8,128,1024]{2,1,0:T(8,128)(2,1)} %bitcast.369, bf16[1024,128]{0,1:T(8,128)(2,1)S(1)} %copy.67, f32[128,1024]{1,0:T(8,128)S(1)} %get-tuple-element.49, f32[1024]{0:T(1024)S(1)} %add_rsqrt_fusion, f32[1024]{0:T(1024)S(1)} %broadcast_multiply_fusion.1), kind=kOutput, calls=%fused_computation.109 | convolution fusion | flops 269090816 | bytes 3416064 | tf_op jit(solution)/shard_map/dot_general | solution.py:135
  75.1 5.1 %select_convert_fusion = bf16[1024,1024]{1,0:T(8,128)(2,1)S(1)} fusion(f32[1024,1024]{1,0:T(8,128)} %fusion.121, bf16[1024,128]{1,0:T(8,128)(2,1)S(1)} %copy-done.29, f32[]{:T(128)} %bitcast.365, s32[1024]{0:T(1024)S(1)} %copy-done.36, pred[]{:T(512)S(6)} %ge.31, bf16[1024,1,128]{0,2,1:T(8,128)(2,1)S(1)} %get-tuple-element.15), kind=kOutput, calls=%fused_computation.45 | convolution fusion | flops 286261248 | bytes 6819845 | tf_op jit(solution)/shard_map/ihd,jhd->hij/dot_general | solution.py:172
  87.8 3.8 %fusion.32 = bf16[1024,1024]{1,0:T(8,128)(2,1)S(1)} fusion(f32[1024,1024]{0,1:T(8,128)S(1)} %copy-done.37, s32[1024]{0:T(1024)S(1)} %fusion.106, f32[]{:T(128)} %bitcast.364, pred[]{:T(512)S(6)} %ge.33, s32[1024]{0:T(1024)S(1)} %copy-done.36, bf16[1024,1,128]{0,2,1:T(8,128)(2,1)S(1)} %get-tuple-element.15, bf16[2056,128]{1,0:T(8,128)(2,1)} %copy-done.30), kind=kOutput, calls=%fused_computation.44 | convolution fusion | flops 284164096 | bytes 6824449 | tf_op jit(solution)/shard_map/ihd,jhd->hij/dot_general | solution.py:172
  97.2 2.9 %fusion.21 = bf16[1024,1024]{1,0:T(8,128)(2,1)S(1)} fusion(f32[1024,1024]{0,1:T(8,128)S(1)} %copy-done.14, s32[1024]{0:T(1024)S(1)} %fusion.105, f32[]{:T(128)} %bitcast.368, pred[]{:T(512)S(6)} %ge.34, s32[1024]{0:T(1024)S(1)} %copy-done.36, bf16[1024,1,128]{0,2,1:T(8,128)(2,1)S(1)} %get-tuple-element.15, bf16[2056,128]{1,0:T(8,128)(2,1)S(1)} %copy-done.27), kind=kOutput, calls=%fused_computation.30 | convolution fusion | flops 284164096 | bytes 6823941 | tf_op jit(solution)/shard_map/ihd,jhd->hij/dot_general | solution.py:172
  103.6 10.9 %collective-permute-start.10 = (f32[128,32]{0,1:T(8,128)S(1)}, f32[128,32]{0,1:T(8,128)S(1)}, u32[]{:S(2)}, u32[]{:S(2)}) collective-permute-start(f32[128,32]{0,1:T(8,128)S(1)} %get-tuple-element.42), channel_id=1, source_target_pairs={{0,64},{8,72},{16,80},{24,88},{32,96},{40,104},{48,112},{56,120},{... | collective-permute-start | bytes 49160 | tf_op jit(solution)/shard_map/ppermute | solution.py:43
  114.6 3.3 %collective-permute-start.11 = (f32[128,32]{0,1:T(8,128)S(1)}, f32[128,32]{0,1:T(8,128)S(1)}, u32[]{:S(2)}, u32[]{:S(2)}) collective-permute-start(f32[128,32]{0,1:T(8,128)S(1)} %get-tuple-element.41), channel_id=1, source_target_pairs={{0,96},{8,104},{16,112},{24,120},{32,128},{40,136},{48,144},{56,15... | collective-permute-start | bytes 49160 | tf_op jit(solution)/shard_map/ppermute | solution.py:43
  120.3 2.5 %fusion.79 = f32[128,1024]{0,1:T(8,128)S(1)} fusion(bf16[1024,1024]{1,0:T(8,128)(2,1)} %copy-done.19, bf16[2056,128]{1,0:T(8,128)(2,1)S(1)} %copy-done.27), kind=kOutput, calls=%fused_computation.133 | convolution fusion | flops 268435456 | bytes 2883584 | tf_op jit(solution)/shard_map/hij,jhd->ihd/dot_general | solution.py:191
  122.7 2.5 %fusion.42 = bf16[1,1024,128]{2,1,0:T(8,128)(2,1)S(1)} fusion(bf16[1024,1024]{1,0:T(8,128)(2,1)} %copy-done.5, bf16[1024,1,128]{0,2,1:T(8,128)(2,1)S(1)} %get-tuple-element.15), kind=kOutput, calls=%fused_computation.78 | convolution fusion | flops 268566528 | bytes 2621440 | tf_op jit(solution)/shard_map/hij,ihd->jhd/dot_general | solution.py:169
  125.3 5.4 %collective-permute-start.12 = (f32[128,32]{0,1:T(8,128)S(1)}, f32[128,32]{0,1:T(8,128)S(1)}, u32[]{:S(2)}, u32[]{:S(2)}) collective-permute-start(f32[128,32]{0,1:T(8,128)S(1)} %get-tuple-element.40), channel_id=1, source_target_pairs={{0,128},{8,136},{16,144},{24,152},{32,160},{40,168},{48,176},{56,1... | collective-permute-start | bytes 49160 | tf_op jit(solution)/shard_map/ppermute | solution.py:43
  132.3 4.5 %collective-permute-start.16 = (bf16[2,1024,128]{2,1,0:T(8,128)(2,1)S(1)}, bf16[2,1024,128]{2,1,0:T(8,128)(2,1)S(1)}, u32[]{:S(2)}, u32[]{:S(2)}) collective-permute-start(bf16[2,1024,128]{2,1,0:T(8,128)(2,1)S(1)} %copy-done.31), channel_id=1, source_target_pairs={{8,0},{16,8},{24,16},{32,24},{40,32},{48,40},{56,48},{64,56},{72,6... | collective-permute-start | bytes 1572872 | tf_op jit(solution)/shard_map/ppermute | solution.py:18
  139.7 2.9 %fusion.10 = bf16[1024,1024]{1,0:T(8,128)(2,1)S(1)} fusion(f32[1024,1024]{0,1:T(8,128)S(1)} %copy-done.11, s32[1024]{0:T(1024)S(1)} %fusion.104, f32[]{:T(128)} %bitcast.367, pred[]{:T(512)S(6)} %ge.35, s32[1024]{0:T(1024)S(1)} %copy-done.36, bf16[1024,1,128]{0,2,1:T(8,128)(2,1)S(1)} %get-tuple-element.15, bf16[2056,128]{1,0:T(8,128)(2,1)S(1)} %copy-done.25), kind=kOutput, calls=%fused_computation.16 | convolution fusion | flops 284164096 | bytes 6823941 | tf_op jit(solution)/shard_map/ihd,jhd->hij/dot_general | solution.py:172
  145.6 2.5 %fusion.36 = f32[1024,128]{1,0:T(8,128)} fusion(f32[128,1024]{0,1:T(8,128)S(1)} %fusion.72, f32[128,1024]{0,1:T(8,128)S(1)} %fusion.79, f32[128,1024]{0,1:T(8,128)S(1)} %copy-done.21, bf16[1024,1024]{1,0:T(8,128)(2,1)S(1)} %copy-done.18, bf16[2056,128]{1,0:T(8,128)(2,1)} %copy-done.30), kind=kOutput, calls=%fused_computation.65 | convolution fusion | flops 268828672 | bytes 4456448 | tf_op jit(solution)/shard_map/hij,jhd->ihd/dot_general | solution.py:191
  148.8 3.8 %collective-permute-done.17 = bf16[2,1024,128]{2,1,0:T(8,128)(2,1)S(1)} collective-permute-done((bf16[2,1024,128]{2,1,0:T(8,128)(2,1)S(1)}, bf16[2,1024,128]{2,1,0:T(8,128)(2,1)S(1)}, u32[]{:S(2)}, u32[]{:S(2)}) %collective-permute-start.17) | collective-permute-done | bytes 524320 | tf_op jit(solution)/shard_map/ppermute | solution.py:18
  152.6 14.3 %collective-permute-done.18 = bf16[2,1024,128]{2,1,0:T(8,128)(2,1)S(1)} collective-permute-done((bf16[2,1024,128]{2,1,0:T(8,128)(2,1)S(1)}, bf16[2,1024,128]{2,1,0:T(8,128)(2,1)S(1)}, u32[]{:S(2)}, u32[]{:S(2)}) %collective-permute-start.18) | collective-permute-done | bytes 524320 | tf_op jit(solution)/shard_map/ppermute | solution.py:18
  (161 shorter events, 48.0 us)
Async XLA Ops:
  2.5 36.6 %copy-start.34 = (bf16[1024,128]{1,0:T(8,128)(2,1)S(1)}, bf16[1024,128]{1,0:T(8,128)(2,1)}, u32[]{:S(2)}) copy-start(bf16[1024,128]{1,0:T(8,128)(2,1)} %param.14) | copy-start | bytes 786436
  2.5 41.5 %collective-permute-start.6 = (bf16[2056,128]{1,0:T(8,128)(2,1)S(1)}, bf16[2056,128]{1,0:T(8,128)(2,1)S(1)}, u32[]{:S(2)}, u32[]{:S(2)}) collective-permute-start(bf16[2056,128]{1,0:T(8,128)(2,1)S(1)} %pad_maximum_fusion.1), channel_id=1, source_target_pairs={{0,24},{8,32},{16,40},{24,48},{32,56},{40,64},{48,72},{56,80},{64,... | collective-permute-start | bytes 1579016 | tf_op jit(solution)/shard_map/ppermute | solution.py:18
  7.6 38.3 %collective-permute-start.5 = (bf16[2056,128]{1,0:T(8,128)(2,1)S(1)}, bf16[2056,128]{1,0:T(8,128)(2,1)S(1)}, u32[]{:S(2)}, u32[]{:S(2)}) collective-permute-start(bf16[2056,128]{1,0:T(8,128)(2,1)S(1)} %pad_maximum_fusion.1), channel_id=1, source_target_pairs={{0,16},{8,24},{16,32},{24,40},{32,48},{40,56},{48,64},{56,72},{64,... | collective-permute-start | bytes 1579016 | tf_op jit(solution)/shard_map/ppermute | solution.py:18
  10.8 35.8 %collective-permute-start.4 = (bf16[2056,128]{1,0:T(8,128)(2,1)S(1)}, bf16[2056,128]{1,0:T(8,128)(2,1)S(1)}, u32[]{:S(2)}, u32[]{:S(2)}) collective-permute-start(bf16[2056,128]{1,0:T(8,128)(2,1)S(1)} %pad_maximum_fusion.1), channel_id=1, source_target_pairs={{0,8},{8,16},{16,24},{24,32},{32,40},{40,48},{48,56},{56,64},{64,7... | collective-permute-start | bytes 1579016 | tf_op jit(solution)/shard_map/ppermute | solution.py:18
  13.9 25.2 %collective-permute-start = (bf16[1024,128]{1,0:T(8,128)(2,1)}, bf16[1024,128]{1,0:T(8,128)(2,1)}, u32[]{:S(2)}, u32[]{:S(2)}) collective-permute-start(bf16[1024,128]{1,0:T(8,128)(2,1)} %param.14), channel_id=1, source_target_pairs={{0,1},{1,0},{2,3},{3,2},{4,5},{5,4},{6,7},{7,6},{8,9},{9,8},{10,11... | collective-permute-start | bytes 786440 | tf_op jit(solution)/shard_map/ppermute | solution.py:111
  40.3 21.9 %collective-permute-start.1 = (bf16[1024,256]{1,0:T(8,128)(2,1)S(1)}, bf16[1024,256]{1,0:T(8,128)(2,1)S(1)}, u32[]{:S(2)}, u32[]{:S(2)}) collective-permute-start(bf16[1024,256]{1,0:T(8,128)(2,1)S(1)} %maximum_select_fusion), channel_id=1, source_target_pairs={{0,2},{1,3},{2,4},{3,5},{4,6},{5,7},{6,0},{7,1},{8,10},{9,11},{10,... | collective-permute-start | bytes 1572872 | tf_op jit(solution)/shard_map/ppermute | solution.py:121
  41.5 23.5 %collective-permute-start.2 = (bf16[1024,256]{1,0:T(8,128)(2,1)S(1)}, bf16[1024,256]{1,0:T(8,128)(2,1)S(1)}, u32[]{:S(2)}, u32[]{:S(2)}) collective-permute-start(bf16[1024,256]{1,0:T(8,128)(2,1)S(1)} %maximum_select_fusion), channel_id=1, source_target_pairs={{0,4},{1,5},{2,6},{3,7},{4,0},{5,1},{6,2},{7,3},{8,12},{9,13},{10,... | collective-permute-start | bytes 1572872 | tf_op jit(solution)/shard_map/ppermute | solution.py:121
  44.0 21.0 %collective-permute-start.3 = (bf16[1024,256]{1,0:T(8,128)(2,1)S(1)}, bf16[1024,256]{1,0:T(8,128)(2,1)S(1)}, u32[]{:S(2)}, u32[]{:S(2)}) collective-permute-start(bf16[1024,256]{1,0:T(8,128)(2,1)S(1)} %maximum_select_fusion), channel_id=1, source_target_pairs={{0,6},{1,7},{2,0},{3,1},{4,2},{5,3},{6,4},{7,5},{8,14},{9,15},{10,... | collective-permute-start | bytes 1572872 | tf_op jit(solution)/shard_map/ppermute | solution.py:121
  74.0 12.9 %collective-permute-start.7 = (f32[128,2,2,2,2,32]{0,5,4,3,2,1:T(8,128)}, f32[128,2,2,2,2,32]{0,5,4,3,2,1:T(8,128)S(1)}, u32[]{:S(2)}, u32[]{:S(2)}) collective-permute-start(f32[128,2,2,2,2,32]{0,5,4,3,2,1:T(8,128)} %select_bitcast_fusion), channel_id=1, source_target_pairs={{0,8},{8,0},{16,24},{24,16},{32,40},{40,32},{48,56},{56,48},{64,72... | collective-permute-start | bytes 786440 | tf_op jit(solution)/shard_map/ppermute | solution.py:57
  92.5 4.7 %collective-permute-start.8 = (f32[128,2,2,2,32]{0,4,3,2,1:T(8,128)S(1)}, f32[128,2,2,2,32]{0,4,3,2,1:T(8,128)S(1)}, u32[]{:S(2)}, u32[]{:S(2)}) collective-permute-start(f32[128,2,2,2,32]{0,4,3,2,1:T(8,128)S(1)} %fusion.92), channel_id=1, source_target_pairs={{0,16},{8,24},{16,0},{24,8},{32,48},{40,56},{48,32},{56,40},{64,80... | collective-permute-start | bytes 393224 | tf_op jit(solution)/shard_map/ppermute | solution.py:57
  103.0 35.8 %copy-start.4 = (bf16[1024,1024]{1,0:T(8,128)(2,1)S(1)}, bf16[1024,1024]{1,0:T(8,128)(2,1)}, u32[]{:S(2)}) copy-start(bf16[1024,1024]{1,0:T(8,128)(2,1)} %copy-done.3) | copy-start | bytes 6291460
  103.5 28.7 %copy-start.35 = (bf16[1,1024,128]{2,1,0:T(8,128)(2,1)S(1)}, bf16[1,1024,128]{2,1,0:T(8,128)(2,1)}, u32[]{:S(2)}) copy-start(bf16[1,1024,128]{2,1,0:T(8,128)(2,1)} %fusion.41) | copy-start | bytes 786436
  103.5 28.7 %copy-start.31 = (bf16[2,1024,128]{2,1,0:T(8,128)(2,1)S(1)}, bf16[2,1024,128]{2,1,0:T(8,128)(2,1)}, u32[]{:S(2)}) copy-start(bf16[2,1024,128]{2,1,0:T(8,128)(2,1)} %pad_maximum_fusion.2) | copy-start | bytes 1572868
  103.6 27.1 %collective-permute-start.10 = (f32[128,32]{0,1:T(8,128)S(1)}, f32[128,32]{0,1:T(8,128)S(1)}, u32[]{:S(2)}, u32[]{:S(2)}) collective-permute-start(f32[128,32]{0,1:T(8,128)S(1)} %get-tuple-element.42), channel_id=1, source_target_pairs={{0,64},{8,72},{16,80},{24,88},{32,96},{40,104},{48,112},{56,120},{... | collective-permute-start | bytes 49160 | tf_op jit(solution)/shard_map/ppermute | solution.py:43
  114.6 16.2 %collective-permute-start.11 = (f32[128,32]{0,1:T(8,128)S(1)}, f32[128,32]{0,1:T(8,128)S(1)}, u32[]{:S(2)}, u32[]{:S(2)}) collective-permute-start(f32[128,32]{0,1:T(8,128)S(1)} %get-tuple-element.41), channel_id=1, source_target_pairs={{0,96},{8,104},{16,112},{24,120},{32,128},{40,136},{48,144},{56,15... | collective-permute-start | bytes 49160 | tf_op jit(solution)/shard_map/ppermute | solution.py:43
  117.9 18.9 %collective-permute-start.13 = (f32[128,32]{0,1:T(8,128)S(1)}, f32[128,32]{0,1:T(8,128)S(1)}, u32[]{:S(2)}, u32[]{:S(2)}) collective-permute-start(f32[128,32]{0,1:T(8,128)S(1)} %get-tuple-element.39), channel_id=1, source_target_pairs={{0,160},{8,168},{16,176},{24,184},{32,192},{40,200},{48,208},{56,2... | collective-permute-start | bytes 49160 | tf_op jit(solution)/shard_map/ppermute | solution.py:43
  119.0 19.0 %collective-permute-start.14 = (f32[128,32]{0,1:T(8,128)S(1)}, f32[128,32]{0,1:T(8,128)S(1)}, u32[]{:S(2)}, u32[]{:S(2)}) collective-permute-start(f32[128,32]{0,1:T(8,128)S(1)} %get-tuple-element.38), channel_id=1, source_target_pairs={{0,192},{8,200},{16,208},{24,216},{32,224},{40,232},{48,240},{56,2... | collective-permute-start | bytes 49160 | tf_op jit(solution)/shard_map/ppermute | solution.py:43
  125.3 7.0 %collective-permute-start.12 = (f32[128,32]{0,1:T(8,128)S(1)}, f32[128,32]{0,1:T(8,128)S(1)}, u32[]{:S(2)}, u32[]{:S(2)}) collective-permute-start(f32[128,32]{0,1:T(8,128)S(1)} %get-tuple-element.40), channel_id=1, source_target_pairs={{0,128},{8,136},{16,144},{24,152},{32,160},{40,168},{48,176},{56,1... | collective-permute-start | bytes 49160 | tf_op jit(solution)/shard_map/ppermute | solution.py:43
  130.7 7.4 %collective-permute-start.15 = (f32[128,32]{0,1:T(8,128)S(1)}, f32[128,32]{0,1:T(8,128)S(1)}, u32[]{:S(2)}, u32[]{:S(2)}) collective-permute-start(f32[128,32]{0,1:T(8,128)S(1)} %get-tuple-element.37), channel_id=1, source_target_pairs={{0,224},{8,232},{16,240},{24,248},{32,0},{40,8},{48,16},{56,24},{6... | collective-permute-start | bytes 49160 | tf_op jit(solution)/shard_map/ppermute | solution.py:43
  130.7 7.4 %collective-permute-start.9 = (f32[128,32]{0,1:T(8,128)S(1)}, f32[128,32]{0,1:T(8,128)S(1)}, u32[]{:S(2)}, u32[]{:S(2)}) collective-permute-start(f32[128,32]{0,1:T(8,128)S(1)} %get-tuple-element.36), channel_id=1, source_target_pairs={{0,32},{8,40},{16,48},{24,56},{32,64},{40,72},{48,80},{56,88},{64,... | collective-permute-start | bytes 49160 | tf_op jit(solution)/shard_map/ppermute | solution.py:43
  132.3 16.5 %collective-permute-start.16 = (bf16[2,1024,128]{2,1,0:T(8,128)(2,1)S(1)}, bf16[2,1024,128]{2,1,0:T(8,128)(2,1)S(1)}, u32[]{:S(2)}, u32[]{:S(2)}) collective-permute-start(bf16[2,1024,128]{2,1,0:T(8,128)(2,1)S(1)} %copy-done.31), channel_id=1, source_target_pairs={{8,0},{16,8},{24,16},{32,24},{40,32},{48,40},{56,48},{64,56},{72,6... | collective-permute-start | bytes 1572872 | tf_op jit(solution)/shard_map/ppermute | solution.py:18
  136.8 15.8 %collective-permute-start.17 = (bf16[2,1024,128]{2,1,0:T(8,128)(2,1)S(1)}, bf16[2,1024,128]{2,1,0:T(8,128)(2,1)S(1)}, u32[]{:S(2)}, u32[]{:S(2)}) collective-permute-start(bf16[2,1024,128]{2,1,0:T(8,128)(2,1)S(1)} %pad_maximum_fusion.3), channel_id=1, source_target_pairs={{16,0},{24,8},{32,16},{40,24},{48,32},{56,40},{64,48},{72,56},{80,... | collective-permute-start | bytes 1572872 | tf_op jit(solution)/shard_map/ppermute | solution.py:18
  143.4 23.6 %copy-start.16 = (f32[1,1024,128]{2,1,0:T(8,128)S(1)}, f32[1,1024,128]{2,1,0:T(8,128)}, u32[]{:S(2)}) copy-start(f32[1,1024,128]{2,1,0:T(8,128)} %convolution_bitcast_fusion.1) | copy-start | bytes 1572868
  143.4 23.5 %collective-permute-start.18 = (bf16[2,1024,128]{2,1,0:T(8,128)(2,1)S(1)}, bf16[2,1024,128]{2,1,0:T(8,128)(2,1)S(1)}, u32[]{:S(2)}, u32[]{:S(2)}) collective-permute-start(bf16[2,1024,128]{2,1,0:T(8,128)(2,1)S(1)} %pad_maximum_fusion.4), channel_id=1, source_target_pairs={{24,0},{32,8},{40,16},{48,24},{56,32},{64,40},{72,48},{80,56},{88,... | collective-permute-start | bytes 1572872 | tf_op jit(solution)/shard_map/ppermute | solution.py:18
  (33 other events, 272.7 us)

commit v6 on v4

--- a/solution.py
+++ b/solution.py
@@ -16,26 +16,6 @@
     devices = range(lax.axis_size(axis))
     route = [(i - distance, i) for i in devices if i - distance in devices]
     return lax.ppermute(block, axis, route)
-
-
-def halving_start(block, axis):
-    count = lax.axis_size(axis)
-    rows, cols = block.shape
-    levels = count.bit_length() - 1
-    return block.reshape((rows,) + (2,) * levels + (cols // count,))
-
-
-def halving_step(current, axis, level):
-    count = lax.axis_size(axis)
-    my_index = lax.axis_index(axis)
-    bit = 1 << level
-    axis_pos = current.ndim - 2
-    mine = (my_index // bit) % 2
-    low = lax.index_in_dim(current, 0, axis_pos, keepdims=False)
-    high = lax.index_in_dim(current, 1, axis_pos, keepdims=False)
-    keep = jnp.where(mine == 0, low, high)
-    send = jnp.where(mine == 0, high, low)
-    return keep + lax.ppermute(send, axis, [(i, i ^ bit) for i in range(count)])
 
 
 def silu_parts(scores):
@@ -119,8 +99,9 @@
     weight_rows = jnp.take(
         product.reshape(product.shape[0], head_devices, block_width), source_block, axis=1
     ).reshape(product.shape)
-    halving = halving_start(weight_rows, "seq")
-    halving_levels = lax.axis_size("seq").bit_length() - 1
+    seq_n = lax.axis_size("seq")
+    chunks = weight_rows.reshape(weight_rows.shape[0], seq_n, -1).transpose(1, 0, 2)
+    exchanged = lax.all_to_all(chunks, "seq", 0, 0, tiled=True)
     grad_mixed = grad_mixed.reshape(row_count, head_count, DH)
     grad_gates = (grad_mixed * normed).reshape(row_count, feature_count)
     grad_normed = grad_mixed * gate_heads
@@ -130,14 +111,10 @@
         - normed * jnp.mean(grad_normed * normed, axis=-1, keepdims=True)
     ) * inv_std
     grad_attended = grad_attended.astype(jnp.bfloat16)
+    chunks, grad_attended = lax.optimization_barrier((chunks, grad_attended))
     grad_queries = jnp.zeros((row_count, head_count, DH), jnp.float32)
     key_terms = []
-    done_levels = 0
     for window_index in range(4):
-        if window_index > 0 and done_levels < halving_levels:
-            halving = halving_step(halving, "seq", done_levels)
-            done_levels += 1
-            halving, grad_attended = lax.optimization_barrier((halving, grad_attended))
         k_heads, v_heads, allowed = prepared[window_index]
         scores = pair_scores(q_heads, k_heads)
         key_act, key_deriv = silu_parts(scores)
@@ -171,10 +148,7 @@
     for distance in back_steps:
         sent = shifted(key_terms[distance].astype(jnp.bfloat16), "seq", -distance)
         summed = summed + sent.astype(jnp.float32)
-    while done_levels < halving_levels:
-        halving = halving_step(halving, "seq", done_levels)
-        done_levels += 1
-    grad_w_out = halving.reshape(halving.shape[0], -1)
+    grad_w_out = exchanged.sum(0)
     return (
         grad_queries.reshape(row_count, feature_count),
         summed[0],

time: 144 us -> 159 us (1.10)
  matrix products: 47 us -> 57.4 us
  other arithmetic: 8.32 us -> 16.1 us
  waiting for transfers between devices: 31.3 us -> 26 us
  local copies, waits for them, and re-layouts: 12.4 us -> 16.7 us
    all_to_all x0 -> x1, starting transfers between devices: none -> 16.1 us  [per_device(): exchanged = lax.all_to_all(chunks, 'seq', 0, 0, tiled=True)]
    ppermute x5 -> x0, starting transfers between devices: 15.7 us -> none  [halving_step(): return keep + lax.ppermute(send, axis, [(i, i ^ bit) for i in range(count)])]
    ppermute x5 -> x0, waiting for transfers between devices: 7.68 us -> none  [halving_step(): return keep + lax.ppermute(send, axis, [(i, i ^ bit) for i in range(count)])]
    ppermute x6, waiting for transfers between devices: 4.38 us -> 9.35 us  [shifted(): return lax.ppermute(block, axis, route)]
    dot_general x4, matrix products: 4.46 us -> 8.73 us  [per_device(): jnp.einsum('hij,jhd->ihd', grad_scores, k_heads, preferred_element_type=j...]
    gather x2, local copies, waits for them, and re-layouts: 0.78 us -> 4.45 us  [per_device(): jnp.take(product.reshape(product.shape[0], head_devices, block_width), so...]
    ppermute x3, waiting for transfers between devices: 2.93 us -> 0.12 us  [per_device(): lax.ppermute(pair_block, 'head', [(i, (i + 2 * k) % head_devices) for i i...]
    another operation x3, other arithmetic: 0.15 us -> 2.61 us  [per_device(): jnp.stack([keys_term.reshape(row_count, feature_count), values_term.resha...]
  transfers between devices with their start and end apart: 15 -> 11, of which waited for: 5 -> 3; matrix products, arithmetic and copies ran while one was open for 36% -> 34% of each run, Pallas kernels for 0% -> 0%
where the time goes in v6:
time: 159 us; the launch traced here: 158 us
  matrix products  57.4 us (36%)
  starting transfers between devices  39.9 us (25%)
  waiting for transfers between devices  26 us (16%)
  local copies, waits for them, and re-layouts  16.7 us (11%)
  other arithmetic  16.1 us (10%)
  between operations  1.89 us (1%)
    ppermute x1, waiting for transfers between devices, per_device(): lax.ppermute(grad_out, 'head', [(i, i ^ 1) for i in range(head_devices)])  16.5 us
    ppermute x6, starting transfers between devices, shifted(): return lax.ppermute(block, axis, route)  16.2 us
    all_to_all x1, starting transfers between devices, per_device(): exchanged = lax.all_to_all(chunks, 'seq', 0, 0, tiled=True)  16.1 us
    dot_general x4, matrix products, per_device(): jnp.einsum('ihd,jhd->hij', grad_attended, v_heads, preferred_element_type...  15.8 us
    dot_general x4, matrix products, pair_scores(): jnp.einsum('ihd,jhd->hij', query_heads, k_heads, preferred_element_type=j...  15.6 us
    ppermute x6, waiting for transfers between devices, shifted(): return lax.ppermute(block, axis, route)  9.35 us
    dot_general x4, matrix products, per_device(): jnp.einsum('hij,jhd->ihd', grad_scores, k_heads, preferred_element_type=j...  8.73 us
    unnamed x61, local copies, waits for them, and re-layouts  6.05 us
  transfers between devices with their start and end apart: 11, of which 3 were waited for; matrix products, arithmetic and copies ran while one was open for 34% of the time, Pallas kernels for 0%

profile of v6, /device:TPU:1, one launch (start us, length us, event | category | flops | bytes accessed | tf_op | source)
XLA Modules:
  0.0 158.0 jit_solution(4071693390015912531)
XLA Ops:
  3.3 4.9 %collective-permute-start.2 = (bf16[2056,128]{1,0:T(8,128)(2,1)}, bf16[2056,128]{1,0:T(8,128)(2,1)S(1)}, u32[]{:S(2)}, u32[]{:S(2)}) collective-permute-start(bf16[2056,128]{1,0:T(8,128)(2,1)} %pad_maximum_fusion.1), channel_id=1, source_target_pairs={{0,24},{8,32},{16,40},{24,48},{32,56},{40,64},{48,72},{56,80},{64,... | collective-permute-start | bytes 1579016 | tf_op jit(solution)/shard_map/ppermute | solution.py:18
  8.2 3.2 %collective-permute-start.1 = (bf16[2056,128]{1,0:T(8,128)(2,1)}, bf16[2056,128]{1,0:T(8,128)(2,1)S(1)}, u32[]{:S(2)}, u32[]{:S(2)}) collective-permute-start(bf16[2056,128]{1,0:T(8,128)(2,1)} %pad_maximum_fusion.1), channel_id=1, source_target_pairs={{0,16},{8,24},{16,32},{24,40},{32,48},{40,56},{48,64},{56,72},{64,... | collective-permute-start | bytes 1579016 | tf_op jit(solution)/shard_map/ppermute | solution.py:18
  11.4 3.1 %collective-permute-start = (bf16[2056,128]{1,0:T(8,128)(2,1)}, bf16[2056,128]{1,0:T(8,128)(2,1)S(1)}, u32[]{:S(2)}, u32[]{:S(2)}) collective-permute-start(bf16[2056,128]{1,0:T(8,128)(2,1)} %pad_maximum_fusion.1), channel_id=1, source_target_pairs={{0,8},{8,16},{16,24},{24,32},{32,40},{40,48},{48,56},{56,64},{64,7... | collective-permute-start | bytes 1579016 | tf_op jit(solution)/shard_map/ppermute | solution.py:18
  14.5 2.7 %collective-permute-start.3 = (bf16[1024,128]{1,0:T(8,128)(2,1)}, bf16[1024,128]{1,0:T(8,128)(2,1)}, u32[]{:S(2)}, u32[]{:S(2)}) collective-permute-start(bf16[1024,128]{1,0:T(8,128)(2,1)} %param.14), channel_id=1, source_target_pairs={{0,1},{1,0},{2,3},{3,2},{4,5},{5,4},{6,7},{7,6},{8,9},{9,8},{10,11... | collective-permute-start | bytes 786440 | tf_op jit(solution)/shard_map/ppermute | solution.py:72
  17.2 3.7 %fusion.103 = f32[1024,1024]{1,0:T(8,128)} fusion(bf16[1024,128]{1,0:T(8,128)(2,1)S(1)} %copy-done, bf16[1024,128]{1,0:T(8,128)(2,1)} %param.9), kind=kOutput, calls=%fused_computation.184 | convolution fusion | flops 268435456 | bytes 4718592 | tf_op jit(solution)/shard_map/ihd,jhd->hij/dot_general | solution.py:55
  23.4 16.5 %collective-permute-done.3 = bf16[1024,128]{1,0:T(8,128)(2,1)} collective-permute-done((bf16[1024,128]{1,0:T(8,128)(2,1)}, bf16[1024,128]{1,0:T(8,128)(2,1)}, u32[]{:S(2)}, u32[]{:S(2)}) %collective-permute-start.3) | collective-permute-done | bytes 262176 | tf_op jit(solution)/shard_map/ppermute | solution.py:72
  42.6 2.5 %collective-permute-start.5 = (bf16[1024,256]{1,0:T(8,128)(2,1)S(1)}, bf16[1024,256]{1,0:T(8,128)(2,1)S(1)}, u32[]{:S(2)}, u32[]{:S(2)}) collective-permute-start(bf16[1024,256]{1,0:T(8,128)(2,1)S(1)} %maximum_select_fusion), channel_id=1, source_target_pairs={{0,4},{1,5},{2,6},{3,7},{4,0},{5,1},{6,2},{7,3},{8,12},{9,13},{10,... | collective-permute-start | bytes 1572872 | tf_op jit(solution)/shard_map/ppermute | solution.py:82
  49.7 10.6 %fusion.26 = (bf16[1024,1024]{1,0:T(8,128)(2,1)S(1)}, bf16[1024,1024]{1,0:T(8,128)(2,1)S(1)}, bf16[1024,1024]{1,0:T(8,128)(2,1)S(1)}, bf16[1024,1024]{1,0:T(8,128)(2,1)S(1)}, f32[1024,1024]{0,1:T(8,128)}) fusion(s32[1024]{0:T(1024)S(1)} %fusion.91, f32[]{:T(128)} %bitcast.298, pred[]{:T(512)S(6)} %ge.23, s32[1024]{0:T(1024)S(1)} %copy-done.28, ...), kind=kOutput, calls=%fused_computation.37 | convolution fusion | flops 312475648 | bytes 25711620 | tf_op jit(solution)/shard_map/ihd,jhd->hij/dot_general | solution.py:55
  69.7 4.0 %copy.56 = bf16[1024,1024]{1,0:T(8,128)(2,1)} copy(bf16[1024,1024]{0,1:T(8,128)(2,1)} %fusion.55) | data formatting | bytes 4194304 | tf_op jit(solution)/shard_map/dot_general | solution.py:96
  73.6 3.2 %fusion.57 = f32[128,8,128]{2,0,1:T(8,128)} fusion(bf16[8,128,1024]{2,1,0:T(8,128)(2,1)} %bitcast.301, bf16[1024,128]{0,1:T(8,128)(2,1)S(1)} %copy.55, f32[128,1024]{1,0:T(8,128)S(1)} %get-tuple-element.32, f32[1024]{0:T(1024)S(1)} %add_rsqrt_fusion, f32[1024]{0:T(1024)S(1)} %broadcast_multiply_fusion.2), kind=kOutput, calls=%fused_computation.109 | convolution fusion | flops 269090816 | bytes 3416064 | tf_op jit(solution)/shard_map/dot_general | solution.py:96
  76.8 2.4 %gather_fusion = f32[8,128,128]{2,1,0:T(8,128)} fusion(f32[128,8,128]{2,0,1:T(8,128)} %fusion.57, s32[1024]{0:T(1024)S(1)} %pad_clamp_fusion), kind=kCustom, calls=%fused_computation | custom fusion | bytes 1048608 | tf_op jit(solution)/shard_map/jit(_take)/gather | solution.py:99
  79.3 2.0 %copy.57 = f32[128,8,128]{0,2,1:T(8,128)} copy(f32[128,8,128]{2,0,1:T(8,128)} %bitcast.303) | data formatting | bytes 1048576 | tf_op jit(solution)/shard_map/jit(_take)/gather | solution.py:99
  81.3 2.2 %fusion.49 = (f32[1024,128]{0,1:T(8,128)}, bf16[1024,1,128]{0,2,1:T(8,128)(2,1)S(1)}) fusion(f32[1024,128]{0,1:T(8,128)} %copy-done.19, f32[128,1024]{1,0:T(8,128)S(1)} %get-tuple-element.32, f32[1024]{0:T(1024)S(1)} %add_rsqrt_fusion, f32[1024]{0:T(1024)S(1)} %broadcast_multiply_fusion.2, f32[1024]{0:T(1024)S(1)} %get-tuple-element.35, ...), kind=kLoop, calls=%fused_computation.95 | loop fusion | flops 1310720 | bytes 2113536 | tf_op jit(solution)/shard_map/reshape | solution.py:106
  89.0 3.7 %select_convert_fusion = bf16[1024,1024]{1,0:T(8,128)(2,1)S(1)} fusion(f32[1024,1024]{1,0:T(8,128)S(1)} %copy-done.8, bf16[1024,128]{1,0:T(8,128)(2,1)S(1)} %copy-done.24, f32[]{:T(128)} %bitcast.297, s32[1024]{0:T(1024)S(1)} %copy-done.28, pred[]{:T(512)S(6)} %ge.21, bf16[1024,1,128]{0,2,1:T(8,128)(2,1)S(1)} %get-tuple-element.6), kind=kOutput, calls=%fused_computation.44 | convolution fusion | flops 286261248 | bytes 6819845 | tf_op jit(solution)/shard_map/ihd,jhd->hij/dot_general | solution.py:125
  95.2 16.1 %all-to-all-start = ((f32[32,128,32]{1,2,0:T(8,128)}), f32[32,128,32]{1,2,0:T(8,128)}, u32[]{:S(2)}, u32[]{:S(2)}) async-start(f32[32,128,32]{1,2,0:T(8,128)} %select_bitcast_fusion), calls=%async_computation | async-start | bytes 1048576 | tf_op jit(solution)/shard_map/all_to_all | solution.py:104
  111.3 4.4 %fusion.32 = bf16[1024,1024]{1,0:T(8,128)(2,1)S(1)} fusion(f32[1024,1024]{0,1:T(8,128)} %get-tuple-element.30, s32[1024]{0:T(1024)S(1)} %fusion.91, f32[]{:T(128)} %bitcast.296, pred[]{:T(512)S(6)} %ge.23, s32[1024]{0:T(1024)S(1)} %copy-done.28, bf16[1024,1,128]{0,2,1:T(8,128)(2,1)S(1)} %get-tuple-element.6, bf16[2056,128]{1,0:T(8,128)(2,1)} %copy-done.25), kind=kOutput, calls=%fused_computation.43 | convolution fusion | flops 284164096 | bytes 6824449 | tf_op jit(solution)/shard_map/ihd,jhd->hij/dot_general | solution.py:125
  117.4 2.3 %collective-permute-start.7 = (bf16[2,1024,128]{2,1,0:T(8,128)(2,1)}, bf16[2,1024,128]{2,1,0:T(8,128)(2,1)}, u32[]{:S(2)}, u32[]{:S(2)}) collective-permute-start(bf16[2,1024,128]{2,1,0:T(8,128)(2,1)} %pad_maximum_fusion.2), channel_id=1, source_target_pairs={{8,0},{16,8},{24,16},{32,24},{40,32},{48,40},{56,48},{64,56},{72,6... | collective-permute-start | bytes 1572872 | tf_op jit(solution)/shard_map/ppermute | solution.py:18
  119.7 3.8 %fusion.21 = bf16[1024,1024]{1,0:T(8,128)(2,1)S(1)} fusion(f32[1024,1024]{0,1:T(8,128)S(1)} %copy-done.12, s32[1024]{0:T(1024)S(1)} %fusion.90, f32[]{:T(128)} %bitcast.300, pred[]{:T(512)S(6)} %ge.24, s32[1024]{0:T(1024)S(1)} %copy-done.28, bf16[1024,1,128]{0,2,1:T(8,128)(2,1)S(1)} %get-tuple-element.6, bf16[2056,128]{1,0:T(8,128)(2,1)} %copy-done.21), kind=kOutput, calls=%fused_computation.29 | convolution fusion | flops 284164096 | bytes 6824449 | tf_op jit(solution)/shard_map/ihd,jhd->hij/dot_general | solution.py:125
  126.7 3.8 %fusion.10 = bf16[1024,1024]{1,0:T(8,128)(2,1)S(1)} fusion(f32[1024,1024]{0,1:T(8,128)S(1)} %copy-done.10, s32[1024]{0:T(1024)S(1)} %fusion.89, f32[]{:T(128)} %bitcast.299, pred[]{:T(512)S(6)} %ge.25, s32[1024]{0:T(1024)S(1)} %copy-done.28, bf16[1024,1,128]{0,2,1:T(8,128)(2,1)S(1)} %get-tuple-element.6, bf16[2056,128]{1,0:T(8,128)(2,1)} %copy-done.20), kind=kOutput, calls=%fused_computation.15 | convolution fusion | flops 284164096 | bytes 6824449 | tf_op jit(solution)/shard_map/ihd,jhd->hij/dot_general | solution.py:125
  134.1 2.0 %copy.68 = f32[1024,128]{1,0:T(8,128)} copy(f32[1024,128]{0,1:T(8,128)} %get-tuple-element.22) | data formatting | bytes 1048576
  136.1 2.4 %fusion.76 = f32[128,1024]{0,1:T(8,128)S(1)} fusion(bf16[1024,1024]{1,0:T(8,128)(2,1)} %copy-done.16, bf16[2056,128]{1,0:T(8,128)(2,1)} %copy-done.21), kind=kOutput, calls=%fused_computation.128 | convolution fusion | flops 268435456 | bytes 2883584 | tf_op jit(solution)/shard_map/hij,jhd->ihd/dot_general | solution.py:144
  138.6 2.3 %fusion.69 = f32[128,1024]{0,1:T(8,128)S(1)} fusion(bf16[1024,1024]{1,0:T(8,128)(2,1)} %copy-done.17, bf16[2056,128]{1,0:T(8,128)(2,1)} %copy-done.20), kind=kOutput, calls=%fused_computation.121 | convolution fusion | flops 268435456 | bytes 2883584 | tf_op jit(solution)/shard_map/hij,jhd->ihd/dot_general | solution.py:144
  141.8 2.5 %fusion.36 = f32[1024,128]{1,0:T(8,128)} fusion(f32[128,1024]{0,1:T(8,128)S(1)} %fusion.69, f32[128,1024]{0,1:T(8,128)S(1)} %fusion.76, f32[128,1024]{0,1:T(8,128)S(1)} %copy-done.18, bf16[1024,1024]{1,0:T(8,128)(2,1)S(1)} %copy-done.15, bf16[2056,128]{1,0:T(8,128)(2,1)} %copy-done.25), kind=kOutput, calls=%fused_computation.64 | convolution fusion | flops 268828672 | bytes 4456448 | tf_op jit(solution)/shard_map/hij,jhd->ihd/dot_general | solution.py:144
  144.3 9.3 %collective-permute-done.9 = bf16[2,1024,128]{2,1,0:T(8,128)(2,1)} collective-permute-done((bf16[2,1024,128]{2,1,0:T(8,128)(2,1)}, bf16[2,1024,128]{2,1,0:T(8,128)(2,1)}, u32[]{:S(2)}, u32[]{:S(2)}) %collective-permute-start.9) | collective-permute-done | bytes 524320 | tf_op jit(solution)/shard_map/ppermute | solution.py:18
  (118 shorter events, 42.4 us)
Async XLA Ops:
  0.6 16.6 %copy-start = (bf16[1024,128]{1,0:T(8,128)(2,1)S(1)}, bf16[1024,128]{1,0:T(8,128)(2,1)}, u32[]{:S(2)}) copy-start(bf16[1024,128]{1,0:T(8,128)(2,1)} %param.8) | copy-start | bytes 786436
  0.6 21.0 %copy-start.26 = (bf16[128,1024]{1,0:T(8,128)(2,1)S(1)}, bf16[128,1024]{1,0:T(8,128)(2,1)}, u32[]{:S(2)}) copy-start(bf16[128,1024]{1,0:T(8,128)(2,1)} %param.15) | copy-start | bytes 786436
  0.7 22.2 %copy-start.27 = (bf16[1024,128]{1,0:T(8,128)(2,1)S(1)}, bf16[1024,128]{1,0:T(8,128)(2,1)}, u32[]{:S(2)}) copy-start(bf16[1024,128]{1,0:T(8,128)(2,1)} %param.11) | copy-start | bytes 786436
  3.3 41.7 %collective-permute-start.2 = (bf16[2056,128]{1,0:T(8,128)(2,1)}, bf16[2056,128]{1,0:T(8,128)(2,1)S(1)}, u32[]{:S(2)}, u32[]{:S(2)}) collective-permute-start(bf16[2056,128]{1,0:T(8,128)(2,1)} %pad_maximum_fusion.1), channel_id=1, source_target_pairs={{0,24},{8,32},{16,40},{24,48},{32,56},{40,64},{48,72},{56,80},{64,... | collective-permute-start | bytes 1579016 | tf_op jit(solution)/shard_map/ppermute | solution.py:18
  8.2 38.7 %collective-permute-start.1 = (bf16[2056,128]{1,0:T(8,128)(2,1)}, bf16[2056,128]{1,0:T(8,128)(2,1)S(1)}, u32[]{:S(2)}, u32[]{:S(2)}) collective-permute-start(bf16[2056,128]{1,0:T(8,128)(2,1)} %pad_maximum_fusion.1), channel_id=1, source_target_pairs={{0,16},{8,24},{16,32},{24,40},{32,48},{40,56},{48,64},{56,72},{64,... | collective-permute-start | bytes 1579016 | tf_op jit(solution)/shard_map/ppermute | solution.py:18
  11.4 36.2 %collective-permute-start = (bf16[2056,128]{1,0:T(8,128)(2,1)}, bf16[2056,128]{1,0:T(8,128)(2,1)S(1)}, u32[]{:S(2)}, u32[]{:S(2)}) collective-permute-start(bf16[2056,128]{1,0:T(8,128)(2,1)} %pad_maximum_fusion.1), channel_id=1, source_target_pairs={{0,8},{8,16},{16,24},{24,32},{32,40},{40,48},{48,56},{56,64},{64,7... | collective-permute-start | bytes 1579016 | tf_op jit(solution)/shard_map/ppermute | solution.py:18
  14.5 25.4 %collective-permute-start.3 = (bf16[1024,128]{1,0:T(8,128)(2,1)}, bf16[1024,128]{1,0:T(8,128)(2,1)}, u32[]{:S(2)}, u32[]{:S(2)}) collective-permute-start(bf16[1024,128]{1,0:T(8,128)(2,1)} %param.14), channel_id=1, source_target_pairs={{0,1},{1,0},{2,3},{3,2},{4,5},{5,4},{6,7},{7,6},{8,9},{9,8},{10,11... | collective-permute-start | bytes 786440 | tf_op jit(solution)/shard_map/ppermute | solution.py:72
  41.3 24.6 %collective-permute-start.4 = (bf16[1024,256]{1,0:T(8,128)(2,1)S(1)}, bf16[1024,256]{1,0:T(8,128)(2,1)S(1)}, u32[]{:S(2)}, u32[]{:S(2)}) collective-permute-start(bf16[1024,256]{1,0:T(8,128)(2,1)S(1)} %maximum_select_fusion), channel_id=1, source_target_pairs={{0,2},{1,3},{2,4},{3,5},{4,6},{5,7},{6,0},{7,1},{8,10},{9,11},{10,... | collective-permute-start | bytes 1572872 | tf_op jit(solution)/shard_map/ppermute | solution.py:82
  42.6 23.5 %collective-permute-start.5 = (bf16[1024,256]{1,0:T(8,128)(2,1)S(1)}, bf16[1024,256]{1,0:T(8,128)(2,1)S(1)}, u32[]{:S(2)}, u32[]{:S(2)}) collective-permute-start(bf16[1024,256]{1,0:T(8,128)(2,1)S(1)} %maximum_select_fusion), channel_id=1, source_target_pairs={{0,4},{1,5},{2,6},{3,7},{4,0},{5,1},{6,2},{7,3},{8,12},{9,13},{10,... | collective-permute-start | bytes 1572872 | tf_op jit(solution)/shard_map/ppermute | solution.py:82
  45.0 16.1 %copy-start.20 = (bf16[2056,128]{1,0:T(8,128)(2,1)}, bf16[2056,128]{1,0:T(8,128)(2,1)S(1)}, u32[]{:S(2)}) copy-start(bf16[2056,128]{1,0:T(8,128)(2,1)S(1)} %collective-permute-done.2) | copy-start | bytes 1579012
  45.0 21.0 %collective-permute-start.6 = (bf16[1024,256]{1,0:T(8,128)(2,1)S(1)}, bf16[1024,256]{1,0:T(8,128)(2,1)S(1)}, u32[]{:S(2)}, u32[]{:S(2)}) collective-permute-start(bf16[1024,256]{1,0:T(8,128)(2,1)S(1)} %maximum_select_fusion), channel_id=1, source_target_pairs={{0,6},{1,7},{2,0},{3,1},{4,2},{5,3},{6,4},{7,5},{8,14},{9,15},{10,... | collective-permute-start | bytes 1572872 | tf_op jit(solution)/shard_map/ppermute | solution.py:82
  46.9 13.4 %copy-start.9 = (f32[1024,1024]{0,1:T(8,128)}, f32[1024,1024]{0,1:T(8,128)S(1)}, u32[]{:S(2)}) copy-start(f32[1024,1024]{0,1:T(8,128)S(1)} %fusion.71) | copy-start | bytes 12582916
  47.6 12.6 %copy-start.11 = (f32[1024,1024]{0,1:T(8,128)}, f32[1024,1024]{0,1:T(8,128)S(1)}, u32[]{:S(2)}) copy-start(f32[1024,1024]{0,1:T(8,128)S(1)} %fusion.78) | copy-start | bytes 12582916
  49.7 10.6 %copy-start.23 = (bf16[1024,128]{1,0:T(8,128)(2,1)S(1)}, bf16[1024,128]{1,0:T(8,128)(2,1)}, u32[]{:S(2)}) copy-start(bf16[1024,128]{1,0:T(8,128)(2,1)} %param.10) | copy-start | bytes 786436
  81.3 5.8 %copy-start.4 = (bf16[1024,1024]{1,0:T(8,128)(2,1)S(1)}, bf16[1024,1024]{1,0:T(8,128)(2,1)}, u32[]{:S(2)}) copy-start(bf16[1024,1024]{1,0:T(8,128)(2,1)} %copy-done.3) | copy-start | bytes 6291460
  81.3 6.7 %copy-start.2 = (bf16[1024,1024]{1,0:T(8,128)(2,1)S(1)}, bf16[1024,1024]{1,0:T(8,128)(2,1)}, u32[]{:S(2)}) copy-start(bf16[1024,1024]{1,0:T(8,128)(2,1)} %copy-done.1) | copy-start | bytes 6291460
  95.2 61.1 %all-to-all-start = ((f32[32,128,32]{1,2,0:T(8,128)}), f32[32,128,32]{1,2,0:T(8,128)}, u32[]{:S(2)}, u32[]{:S(2)}) async-start(f32[32,128,32]{1,2,0:T(8,128)} %select_bitcast_fusion), calls=%async_computation | async-start | bytes 1048576 | tf_op jit(solution)/shard_map/all_to_all | solution.py:104
  115.7 7.9 %copy-start.14 = (bf16[1024,1024]{1,0:T(8,128)(2,1)}, bf16[1024,1024]{1,0:T(8,128)(2,1)S(1)}, u32[]{:S(2)}) copy-start(bf16[1024,1024]{1,0:T(8,128)(2,1)S(1)} %fusion.32) | copy-start | bytes 6291460
  117.4 27.0 %collective-permute-start.7 = (bf16[2,1024,128]{2,1,0:T(8,128)(2,1)}, bf16[2,1024,128]{2,1,0:T(8,128)(2,1)}, u32[]{:S(2)}, u32[]{:S(2)}) collective-permute-start(bf16[2,1024,128]{2,1,0:T(8,128)(2,1)} %pad_maximum_fusion.2), channel_id=1, source_target_pairs={{8,0},{16,8},{24,16},{32,24},{40,32},{48,40},{56,48},{64,56},{72,6... | collective-permute-start | bytes 1572872 | tf_op jit(solution)/shard_map/ppermute | solution.py:18
  123.6 7.0 %copy-start.16 = (bf16[1024,1024]{1,0:T(8,128)(2,1)}, bf16[1024,1024]{1,0:T(8,128)(2,1)S(1)}, u32[]{:S(2)}) copy-start(bf16[1024,1024]{1,0:T(8,128)(2,1)S(1)} %fusion.21) | copy-start | bytes 6291460
  125.3 19.0 %collective-permute-start.8 = (bf16[2,1024,128]{2,1,0:T(8,128)(2,1)}, bf16[2,1024,128]{2,1,0:T(8,128)(2,1)}, u32[]{:S(2)}, u32[]{:S(2)}) collective-permute-start(bf16[2,1024,128]{2,1,0:T(8,128)(2,1)} %pad_maximum_fusion.3), channel_id=1, source_target_pairs={{16,0},{24,8},{32,16},{40,24},{48,32},{56,40},{64,48},{72,56},{80,... | collective-permute-start | bytes 1572872 | tf_op jit(solution)/shard_map/ppermute | solution.py:18
  132.0 8.9 %copy-start.6 = (bf16[1024,1024]{1,0:T(8,128)(2,1)S(1)}, bf16[1024,1024]{1,0:T(8,128)(2,1)}, u32[]{:S(2)}) copy-start(bf16[1024,1024]{1,0:T(8,128)(2,1)} %copy-done.5) | copy-start | bytes 6291460
  132.8 20.9 %collective-permute-start.9 = (bf16[2,1024,128]{2,1,0:T(8,128)(2,1)}, bf16[2,1024,128]{2,1,0:T(8,128)(2,1)}, u32[]{:S(2)}, u32[]{:S(2)}) collective-permute-start(bf16[2,1024,128]{2,1,0:T(8,128)(2,1)} %pad_maximum_fusion.4), channel_id=1, source_target_pairs={{24,0},{32,8},{40,16},{48,24},{56,32},{64,40},{72,48},{80,56},{88,... | collective-permute-start | bytes 1572872 | tf_op jit(solution)/shard_map/ppermute | solution.py:18
  136.1 5.7 %copy-start.18 = (f32[128,1024]{0,1:T(8,128)S(1)}, f32[128,1024]{0,1:T(8,128)}, u32[]{:S(2)}) copy-start(f32[128,1024]{0,1:T(8,128)} %convolution_bitcast_fusion.2) | copy-start | bytes 1572868
  (16 other events, 48.4 us)

commit v7 on v4

--- a/solution.py
+++ b/solution.py
@@ -131,10 +131,10 @@
     ) * inv_std
     grad_attended = grad_attended.astype(jnp.bfloat16)
     grad_queries = jnp.zeros((row_count, head_count, DH), jnp.float32)
-    key_terms = []
+    key_terms = [None] * 4
     done_levels = 0
-    for window_index in range(4):
-        if window_index > 0 and done_levels < halving_levels:
+    for step_index, window_index in enumerate((3, 2, 1, 0)):
+        if step_index > 0 and done_levels < halving_levels:
             halving = halving_step(halving, "seq", done_levels)
             done_levels += 1
             halving, grad_attended = lax.optimization_barrier((halving, grad_attended))
@@ -163,14 +163,17 @@
                 ]
             ),
         )
-        key_terms.append(term_pair)
+        key_terms[window_index] = term_pair
+        if window_index > 0:
+            key_terms[window_index] = shifted(
+                term_pair.astype(jnp.bfloat16), "seq", -window_index
+            ).astype(jnp.float32)
         grad_queries = grad_queries + jnp.einsum(
             "hij,jhd->ihd", grad_scores, k_heads, preferred_element_type=jnp.float32
         )
     summed = key_terms[0]
     for distance in back_steps:
-        sent = shifted(key_terms[distance].astype(jnp.bfloat16), "seq", -distance)
-        summed = summed + sent.astype(jnp.float32)
+        summed = summed + key_terms[distance]
     while done_levels < halving_levels:
         halving = halving_step(halving, "seq", done_levels)
         done_levels += 1

time: 144 us -> 150 us (1.042)
  waiting for transfers between devices: 31.3 us -> 18 us
  matrix products: 47 us -> 56 us
  other arithmetic: 8.32 us -> 16.7 us
  local copies, waits for them, and re-layouts: 12.4 us -> 17.2 us
  starting transfers between devices: 40.3 us -> 38.4 us
    ppermute x5, waiting for transfers between devices: 7.68 us -> 1.51 us  [halving_step(): return keep + lax.ppermute(send, axis, [(i, i ^ bit) for i in range(count)])]
    ppermute x6, waiting for transfers between devices: 4.38 us -> 0.02 us  [shifted(): return lax.ppermute(block, axis, route)]
    gather x2, local copies, waits for them, and re-layouts: 0.78 us -> 4.45 us  [per_device(): jnp.take(product.reshape(product.shape[0], head_devices, block_width), so...]
    another operation x3, other arithmetic: 0.15 us -> 2.54 us  [per_device(): jnp.stack([keys_term.reshape(row_count, feature_count), values_term.resha...]
    dot_general x4, matrix products: 13.7 us -> 16 us  [per_device(): jnp.einsum('ihd,jhd->hij', grad_attended, v_heads, preferred_element_type...]
    dot_general x4, matrix products: 3.35 us -> 5.44 us  [per_device(): jnp.einsum('hij,jhd->ihd', weights, v_heads, preferred_element_type=jnp.f...]
    dot_general x4, matrix products: 4.46 us -> 6.37 us  [per_device(): jnp.einsum('hij,jhd->ihd', grad_scores, k_heads, preferred_element_type=j...]
    convert_element_type x3, other arithmetic: 0.02 us -> 1.79 us  [per_device(): key_pack[2 * row_count:].reshape(-1)[:row_count].astype(jnp.int32)]
  transfers between devices with their start and end apart: 15 -> 15, of which waited for: 5 -> 4; matrix products, arithmetic and copies ran while one was open for 36% -> 44% of each run, Pallas kernels for 0% -> 0%
where the time goes in v7:
time: 150 us; the launch traced here: 148 us
  matrix products  56 us (37%)
  starting transfers between devices  38.4 us (26%)
  waiting for transfers between devices  18 us (12%)
  local copies, waits for them, and re-layouts  17.2 us (11%)
  other arithmetic  16.7 us (11%)
  between operations  2.07 us (1%)
    dot_general x4, matrix products, per_device(): jnp.einsum('ihd,jhd->hij', grad_attended, v_heads, preferred_element_type...  16 us
    ppermute x6, starting transfers between devices, shifted(): return lax.ppermute(block, axis, route)  15.6 us
    dot_general x4, matrix products, pair_scores(): jnp.einsum('ihd,jhd->hij', query_heads, k_heads, preferred_element_type=j...  15.6 us
    ppermute x5, starting transfers between devices, halving_step(): return keep + lax.ppermute(send, axis, [(i, i ^ bit) for i in range(count)])  15.2 us
    ppermute x1, waiting for transfers between devices, per_device(): lax.ppermute(grad_out, 'head', [(i, i ^ 1) for i in range(head_devices)])  15.2 us
    unnamed x52, local copies, waits for them, and re-layouts  6.73 us
    dot_general x4, matrix products, per_device(): jnp.einsum('hij,jhd->ihd', grad_scores, k_heads, preferred_element_type=j...  6.37 us
    dot_general x4, matrix products, per_device(): jnp.einsum('hij,jhd->ihd', weights, v_heads, preferred_element_type=jnp.f...  5.44 us
  transfers between devices with their start and end apart: 15, of which 4 were waited for; matrix products, arithmetic and copies ran while one was open for 44% of the time, Pallas kernels for 0%

profile of v7, /device:TPU:1, one launch (start us, length us, event | category | flops | bytes accessed | tf_op | source)
XLA Modules:
  0.0 148.5 jit_solution(8250406097299402768)
XLA Ops:
  2.5 4.1 %collective-permute-start.6 = (bf16[2056,128]{1,0:T(8,128)(2,1)S(1)}, bf16[2056,128]{1,0:T(8,128)(2,1)S(1)}, u32[]{:S(2)}, u32[]{:S(2)}) collective-permute-start(bf16[2056,128]{1,0:T(8,128)(2,1)S(1)} %pad_maximum_fusion.1), channel_id=1, source_target_pairs={{0,16},{8,24},{16,32},{24,40},{32,48},{40,56},{48,64},{56,72},{64,... | collective-permute-start | bytes 1579016 | tf_op jit(solution)/shard_map/ppermute | solution.py:18
  6.6 4.4 %collective-permute-start = (bf16[2056,128]{1,0:T(8,128)(2,1)S(1)}, bf16[2056,128]{1,0:T(8,128)(2,1)S(1)}, u32[]{:S(2)}, u32[]{:S(2)}) collective-permute-start(bf16[2056,128]{1,0:T(8,128)(2,1)S(1)} %pad_maximum_fusion.1), channel_id=1, source_target_pairs={{0,24},{8,32},{16,40},{24,48},{32,56},{40,64},{48,72},{56,80},{64,... | collective-permute-start | bytes 1579016 | tf_op jit(solution)/shard_map/ppermute | solution.py:18
  10.9 2.5 %collective-permute-start.5 = (bf16[2056,128]{1,0:T(8,128)(2,1)S(1)}, bf16[2056,128]{1,0:T(8,128)(2,1)}, u32[]{:S(2)}, u32[]{:S(2)}) collective-permute-start(bf16[2056,128]{1,0:T(8,128)(2,1)S(1)} %pad_maximum_fusion.1), channel_id=1, source_target_pairs={{0,8},{8,16},{16,24},{24,32},{32,40},{40,48},{48,56},{56,64},{64,7... | collective-permute-start | bytes 1579016 | tf_op jit(solution)/shard_map/ppermute | solution.py:18
  13.5 2.7 %collective-permute-start.1 = (bf16[1024,128]{1,0:T(8,128)(2,1)}, bf16[1024,128]{1,0:T(8,128)(2,1)}, u32[]{:S(2)}, u32[]{:S(2)}) collective-permute-start(bf16[1024,128]{1,0:T(8,128)(2,1)} %param.14), channel_id=1, source_target_pairs={{0,1},{1,0},{2,3},{3,2},{4,5},{5,4},{6,7},{7,6},{8,9},{9,8},{10,11... | collective-permute-start | bytes 786440 | tf_op jit(solution)/shard_map/ppermute | solution.py:92
  16.2 3.6 %fusion.113 = f32[1024,1024]{1,0:T(8,128)} fusion(bf16[1024,128]{1,0:T(8,128)(2,1)S(1)} %copy-done, bf16[1024,128]{1,0:T(8,128)(2,1)} %param.9), kind=kOutput, calls=%fused_computation.213 | convolution fusion | flops 268435456 | bytes 4718592 | tf_op jit(solution)/shard_map/ihd,jhd->hij/dot_general | solution.py:75
  22.3 15.2 %collective-permute-done.1 = bf16[1024,128]{1,0:T(8,128)(2,1)} collective-permute-done((bf16[1024,128]{1,0:T(8,128)(2,1)}, bf16[1024,128]{1,0:T(8,128)(2,1)}, u32[]{:S(2)}, u32[]{:S(2)}) %collective-permute-start.1) | collective-permute-done | bytes 262176 | tf_op jit(solution)/shard_map/ppermute | solution.py:92
  40.2 2.5 %collective-permute-start.3 = (bf16[1024,256]{1,0:T(8,128)(2,1)S(1)}, bf16[1024,256]{1,0:T(8,128)(2,1)S(1)}, u32[]{:S(2)}, u32[]{:S(2)}) collective-permute-start(bf16[1024,256]{1,0:T(8,128)(2,1)S(1)} %maximum_select_fusion), channel_id=1, source_target_pairs={{0,4},{1,5},{2,6},{3,7},{4,0},{5,1},{6,2},{7,3},{8,12},{9,13},{10,... | collective-permute-start | bytes 1572872 | tf_op jit(solution)/shard_map/ppermute | solution.py:102
  47.2 10.5 %fusion.26 = (bf16[1024,1024]{1,0:T(8,128)(2,1)S(1)}, bf16[1024,1024]{1,0:T(8,128)(2,1)S(1)}, bf16[1024,1024]{1,0:T(8,128)(2,1)S(1)}, bf16[1024,1024]{1,0:T(8,128)(2,1)S(1)}, f32[1024,1024]{0,1:T(8,128)}) fusion(s32[1024]{0:T(1024)S(1)} %fusion.100, f32[]{:T(128)} %bitcast.363, pred[]{:T(512)S(6)} %ge.27, s32[1024]{0:T(1024)S(1)} %copy-done.22, ...), kind=kOutput, calls=%fused_computation.37 | convolution fusion | flops 312475648 | bytes 25711620 | tf_op jit(solution)/shard_map/ihd,jhd->hij/dot_general | solution.py:75
  68.4 4.0 %copy.74 = bf16[1024,1024]{1,0:T(8,128)(2,1)} copy(bf16[1024,1024]{0,1:T(8,128)(2,1)} %fusion.55) | data formatting | bytes 4194304 | tf_op jit(solution)/shard_map/dot_general | solution.py:116
  72.4 3.2 %fusion.58 = f32[128,8,128]{2,0,1:T(8,128)} fusion(bf16[8,128,1024]{2,1,0:T(8,128)(2,1)} %bitcast.366, bf16[1024,128]{0,1:T(8,128)(2,1)S(1)} %copy.66, f32[128,1024]{1,0:T(8,128)S(1)} %get-tuple-element.42, f32[1024]{0:T(1024)S(1)} %add_rsqrt_fusion, f32[1024]{0:T(1024)S(1)} %broadcast_multiply_fusion.1), kind=kOutput, calls=%fused_computation.108 | convolution fusion | flops 269090816 | bytes 3416064 | tf_op jit(solution)/shard_map/dot_general | solution.py:116
  75.6 2.4 %gather_fusion.1 = f32[8,128,128]{2,1,0:T(8,128)} fusion(f32[128,8,128]{2,0,1:T(8,128)} %fusion.58, s32[1024]{0:T(1024)S(1)} %pad_clamp_fusion), kind=kCustom, calls=%fused_computation.1 | custom fusion | bytes 1048608 | tf_op jit(solution)/shard_map/jit(_take)/gather | solution.py:119
  78.0 2.0 %copy.75 = f32[128,8,128]{0,2,1:T(8,128)} copy(f32[128,8,128]{2,0,1:T(8,128)} %bitcast.368) | data formatting | bytes 1048576 | tf_op jit(solution)/shard_map/jit(_take)/gather | solution.py:119
  84.0 2.0 %fusion.49 = (f32[1024,128]{0,1:T(8,128)}, bf16[1024,1,128]{0,2,1:T(8,128)(2,1)S(1)}) fusion(f32[1024,128]{0,1:T(8,128)} %copy-done.15, f32[128,1024]{1,0:T(8,128)S(1)} %get-tuple-element.42, f32[1024]{0:T(1024)S(1)} %add_rsqrt_fusion, f32[1024]{0:T(1024)S(1)} %broadcast_multiply_fusion.1, f32[1024]{0:T(1024)S(1)} %get-tuple-element.45, ...), kind=kLoop, calls=%fused_computation.95 | loop fusion | flops 1310720 | bytes 2113536 | tf_op jit(solution)/shard_map/reshape | solution.py:125
  86.0 4.3 %fusion.10 = bf16[1024,1024]{1,0:T(8,128)(2,1)S(1)} fusion(f32[1024,1024]{0,1:T(8,128)} %copy-done.11, f32[]{:T(128)} %bitcast.364, s32[1024]{0:T(1024)S(1)} %fusion.101, pred[]{:T(512)S(6)} %ge.24, s32[1024]{0:T(1024)S(1)} %copy-done.22, bf16[1024,1,128]{0,2,1:T(8,128)(2,1)S(1)} %get-tuple-element.15, bf16[2056,128]{1,0:T(8,128)(2,1)} %copy-done.16), kind=kOutput, calls=%fused_computation.15 | convolution fusion | flops 284164096 | bytes 6824449 | tf_op jit(solution)/shard_map/ihd,jhd->hij/dot_general | solution.py:148
  95.7 2.0 %copy.98 = f32[1024,128]{1,0:T(8,128)} copy(f32[1024,128]{0,1:T(8,128)} %get-tuple-element.32) | data formatting | bytes 1048576
  98.8 2.3 %collective-permute-start.8 = (f32[128,2,2,2,32]{0,4,3,2,1:T(8,128)S(1)}, f32[128,2,2,2,32]{0,4,3,2,1:T(8,128)S(1)}, u32[]{:S(2)}, u32[]{:S(2)}) collective-permute-start(f32[128,2,2,2,32]{0,4,3,2,1:T(8,128)S(1)} %fusion.92), channel_id=1, source_target_pairs={{0,16},{8,24},{16,0},{24,8},{32,48},{40,56},{48,32},{56,40},{64,80... | collective-permute-start | bytes 393224 | tf_op jit(solution)/shard_map/ppermute | solution.py:38
  101.1 2.5 %fusion.42 = bf16[1,1024,128]{2,1,0:T(8,128)(2,1)S(1)} fusion(bf16[1024,1024]{1,0:T(8,128)(2,1)} %copy-done.1, bf16[1024,1,128]{0,2,1:T(8,128)(2,1)S(1)} %get-tuple-element.15), kind=kOutput, calls=%fused_computation.77 | convolution fusion | flops 268566528 | bytes 2621440 | tf_op jit(solution)/shard_map/hij,ihd->jhd/dot_general | solution.py:145
  103.7 4.3 %fusion.21 = bf16[1024,1024]{1,0:T(8,128)(2,1)S(1)} fusion(f32[1024,1024]{0,1:T(8,128)} %copy-done.10, s32[1024]{0:T(1024)S(1)} %fusion.99, f32[]{:T(128)} %bitcast.365, pred[]{:T(512)S(6)} %ge.28, s32[1024]{0:T(1024)S(1)} %copy-done.22, bf16[1024,1,128]{0,2,1:T(8,128)(2,1)S(1)} %get-tuple-element.15, bf16[2056,128]{1,0:T(8,128)(2,1)} %copy-done.17), kind=kOutput, calls=%fused_computation.29 | convolution fusion | flops 284164096 | bytes 6824449 | tf_op jit(solution)/shard_map/ihd,jhd->hij/dot_general | solution.py:148
  112.9 2.3 %collective-permute-start.9 = (f32[128,2,2,32]{0,3,2,1:T(8,128)S(1)}, f32[128,2,2,32]{0,3,2,1:T(8,128)S(1)}, u32[]{:S(2)}, u32[]{:S(2)}) collective-permute-start(f32[128,2,2,32]{0,3,2,1:T(8,128)S(1)} %fusion.93), channel_id=1, source_target_pairs={{0,32},{8,40},{16,48},{24,56},{32,0},{40,8},{48,16},{56,24},{64,96... | collective-permute-start | bytes 196616 | tf_op jit(solution)/shard_map/ppermute | solution.py:38
  116.2 3.8 %fusion.32 = bf16[1024,1024]{1,0:T(8,128)(2,1)S(1)} fusion(f32[1024,1024]{0,1:T(8,128)S(1)} %copy-done.23, s32[1024]{0:T(1024)S(1)} %fusion.100, f32[]{:T(128)} %bitcast.361, pred[]{:T(512)S(6)} %ge.27, s32[1024]{0:T(1024)S(1)} %copy-done.22, bf16[1024,1,128]{0,2,1:T(8,128)(2,1)S(1)} %get-tuple-element.15, bf16[2056,128]{1,0:T(8,128)(2,1)} %collective-permute-done.5), kind=kOutput, calls=%fused_computation.43 | convolution fusion | flops 284164096 | bytes 6824449 | tf_op jit(solution)/shard_map/ihd,jhd->hij/dot_general | solution.py:148
  127.0 3.2 %collective-permute-start.13 = (f32[128,2,32]{0,2,1:T(8,128)S(1)}, f32[128,2,32]{0,2,1:T(8,128)S(1)}, u32[]{:S(2)}, u32[]{:S(2)}) collective-permute-start(f32[128,2,32]{0,2,1:T(8,128)S(1)} %fusion.94), channel_id=1, source_target_pairs={{0,64},{8,72},{16,80},{24,88},{32,96},{40,104},{48,112},{56,120},{... | collective-permute-start | bytes 98312 | tf_op jit(solution)/shard_map/ppermute | solution.py:38
  130.2 3.5 %select_convert_fusion = bf16[1024,1024]{1,0:T(8,128)(2,1)S(1)} fusion(f32[1024,1024]{1,0:T(8,128)S(1)} %copy-done.9, bf16[1024,128]{1,0:T(8,128)(2,1)S(1)} %copy-done.19, f32[]{:T(128)} %bitcast.362, s32[1024]{0:T(1024)S(1)} %copy-done.22, pred[]{:T(512)S(6)} %ge.26, bf16[1024,1,128]{0,2,1:T(8,128)(2,1)S(1)} %get-tuple-element.15), kind=kOutput, calls=%fused_computation.44 | convolution fusion | flops 286261248 | bytes 6819845 | tf_op jit(solution)/shard_map/ihd,jhd->hij/dot_general | solution.py:148
  135.3 2.0 %fusion.36 = f32[1024,128]{0,1:T(8,128)S(1)} fusion(f32[128,1024]{1,0:T(8,128)S(1)} %convolution_bitcast_fusion.2, f32[128,1024]{1,0:T(8,128)S(1)} %fusion.82, f32[128,1024]{1,0:T(8,128)S(1)} %fusion.75, bf16[1024,1024]{1,0:T(8,128)(2,1)S(1)} %copy-done.14, bf16[2056,128]{1,0:T(8,128)(2,1)} %copy-done.16), kind=kOutput, calls=%fused_computation.64 | convolution fusion | flops 268828672 | bytes 4456448 | tf_op jit(solution)/shard_map/hij,jhd->ihd/dot_general | solution.py:171
  138.1 5.4 %collective-permute-start.14 = (f32[128,32]{0,1:T(8,128)S(1)}, f32[128,32]{0,1:T(8,128)S(1)}, u32[]{:S(2)}, u32[]{:S(2)}) collective-permute-start(f32[128,32]{0,1:T(8,128)S(1)} %select_bitcast_fusion.1), channel_id=1, source_target_pairs={{0,128},{8,136},{16,144},{24,152},{32,160},{40,168},{48,176},{56,1... | collective-permute-start | bytes 49160 | tf_op jit(solution)/shard_map/ppermute | solution.py:38
  (125 shorter events, 51.5 us)
Async XLA Ops:
  0.6 15.6 %copy-start = (bf16[1024,128]{1,0:T(8,128)(2,1)S(1)}, bf16[1024,128]{1,0:T(8,128)(2,1)}, u32[]{:S(2)}) copy-start(bf16[1024,128]{1,0:T(8,128)(2,1)} %param.8) | copy-start | bytes 786436
  0.6 20.1 %copy-start.20 = (bf16[128,1024]{1,0:T(8,128)(2,1)S(1)}, bf16[128,1024]{1,0:T(8,128)(2,1)}, u32[]{:S(2)}) copy-start(bf16[128,1024]{1,0:T(8,128)(2,1)} %param.15) | copy-start | bytes 786436
  0.7 21.3 %copy-start.21 = (bf16[1024,128]{1,0:T(8,128)(2,1)S(1)}, bf16[1024,128]{1,0:T(8,128)(2,1)}, u32[]{:S(2)}) copy-start(bf16[1024,128]{1,0:T(8,128)(2,1)} %param.11) | copy-start | bytes 786436
  2.5 40.1 %collective-permute-start.6 = (bf16[2056,128]{1,0:T(8,128)(2,1)S(1)}, bf16[2056,128]{1,0:T(8,128)(2,1)S(1)}, u32[]{:S(2)}, u32[]{:S(2)}) collective-permute-start(bf16[2056,128]{1,0:T(8,128)(2,1)S(1)} %pad_maximum_fusion.1), channel_id=1, source_target_pairs={{0,16},{8,24},{16,32},{24,40},{32,48},{40,56},{48,64},{56,72},{64,... | collective-permute-start | bytes 1579016 | tf_op jit(solution)/shard_map/ppermute | solution.py:18
  6.6 37.9 %collective-permute-start = (bf16[2056,128]{1,0:T(8,128)(2,1)S(1)}, bf16[2056,128]{1,0:T(8,128)(2,1)S(1)}, u32[]{:S(2)}, u32[]{:S(2)}) collective-permute-start(bf16[2056,128]{1,0:T(8,128)(2,1)S(1)} %pad_maximum_fusion.1), channel_id=1, source_target_pairs={{0,24},{8,32},{16,40},{24,48},{32,56},{40,64},{48,72},{56,80},{64,... | collective-permute-start | bytes 1579016 | tf_op jit(solution)/shard_map/ppermute | solution.py:18
  10.9 34.3 %collective-permute-start.5 = (bf16[2056,128]{1,0:T(8,128)(2,1)S(1)}, bf16[2056,128]{1,0:T(8,128)(2,1)}, u32[]{:S(2)}, u32[]{:S(2)}) collective-permute-start(bf16[2056,128]{1,0:T(8,128)(2,1)S(1)} %pad_maximum_fusion.1), channel_id=1, source_target_pairs={{0,8},{8,16},{16,24},{24,32},{32,40},{40,48},{48,56},{56,64},{64,7... | collective-permute-start | bytes 1579016 | tf_op jit(solution)/shard_map/ppermute | solution.py:18
  13.5 24.0 %collective-permute-start.1 = (bf16[1024,128]{1,0:T(8,128)(2,1)}, bf16[1024,128]{1,0:T(8,128)(2,1)}, u32[]{:S(2)}, u32[]{:S(2)}) collective-permute-start(bf16[1024,128]{1,0:T(8,128)(2,1)} %param.14), channel_id=1, source_target_pairs={{0,1},{1,0},{2,3},{3,2},{4,5},{5,4},{6,7},{7,6},{8,9},{9,8},{10,11... | collective-permute-start | bytes 786440 | tf_op jit(solution)/shard_map/ppermute | solution.py:92
  38.9 24.6 %collective-permute-start.2 = (bf16[1024,256]{1,0:T(8,128)(2,1)S(1)}, bf16[1024,256]{1,0:T(8,128)(2,1)S(1)}, u32[]{:S(2)}, u32[]{:S(2)}) collective-permute-start(bf16[1024,256]{1,0:T(8,128)(2,1)S(1)} %maximum_select_fusion), channel_id=1, source_target_pairs={{0,2},{1,3},{2,4},{3,5},{4,6},{5,7},{6,0},{7,1},{8,10},{9,11},{10,... | collective-permute-start | bytes 1572872 | tf_op jit(solution)/shard_map/ppermute | solution.py:102
  40.2 24.2 %collective-permute-start.3 = (bf16[1024,256]{1,0:T(8,128)(2,1)S(1)}, bf16[1024,256]{1,0:T(8,128)(2,1)S(1)}, u32[]{:S(2)}, u32[]{:S(2)}) collective-permute-start(bf16[1024,256]{1,0:T(8,128)(2,1)S(1)} %maximum_select_fusion), channel_id=1, source_target_pairs={{0,4},{1,5},{2,6},{3,7},{4,0},{5,1},{6,2},{7,3},{8,12},{9,13},{10,... | collective-permute-start | bytes 1572872 | tf_op jit(solution)/shard_map/ppermute | solution.py:102
  42.6 22.2 %collective-permute-start.4 = (bf16[1024,256]{1,0:T(8,128)(2,1)S(1)}, bf16[1024,256]{1,0:T(8,128)(2,1)S(1)}, u32[]{:S(2)}, u32[]{:S(2)}) collective-permute-start(bf16[1024,256]{1,0:T(8,128)(2,1)S(1)} %maximum_select_fusion), channel_id=1, source_target_pairs={{0,6},{1,7},{2,0},{3,1},{4,2},{5,3},{6,4},{7,5},{8,14},{9,15},{10,... | collective-permute-start | bytes 1572872 | tf_op jit(solution)/shard_map/ppermute | solution.py:102
  44.5 13.3 %copy-start.10 = (f32[1024,1024]{0,1:T(8,128)}, f32[1024,1024]{0,1:T(8,128)S(1)}, u32[]{:S(2)}) copy-start(f32[1024,1024]{0,1:T(8,128)S(1)} %fusion.77) | copy-start | bytes 12582916
  44.5 14.2 %copy-start.16 = (bf16[2056,128]{1,0:T(8,128)(2,1)}, bf16[2056,128]{1,0:T(8,128)(2,1)S(1)}, u32[]{:S(2)}) copy-start(bf16[2056,128]{1,0:T(8,128)(2,1)S(1)} %collective-permute-done) | copy-start | bytes 1579012
  45.2 12.5 %copy-start.11 = (f32[1024,1024]{0,1:T(8,128)}, f32[1024,1024]{0,1:T(8,128)S(1)}, u32[]{:S(2)}) copy-start(f32[1024,1024]{0,1:T(8,128)S(1)} %fusion.89) | copy-start | bytes 12582916
  47.2 10.6 %copy-start.18 = (bf16[1024,128]{1,0:T(8,128)(2,1)S(1)}, bf16[1024,128]{1,0:T(8,128)(2,1)}, u32[]{:S(2)}) copy-start(bf16[1024,128]{1,0:T(8,128)(2,1)} %param.10) | copy-start | bytes 786436
  82.0 15.8 %collective-permute-start.7 = (f32[128,2,2,2,2,32]{0,5,4,3,2,1:T(8,128)}, f32[128,2,2,2,2,32]{0,5,4,3,2,1:T(8,128)}, u32[]{:S(2)}, u32[]{:S(2)}) collective-permute-start(f32[128,2,2,2,2,32]{0,5,4,3,2,1:T(8,128)} %select_bitcast_fusion), channel_id=1, source_target_pairs={{0,8},{8,0},{16,24},{24,16},{32,40},{40,32},{48,56},{56,48},{64,72... | collective-permute-start | bytes 786440 | tf_op jit(solution)/shard_map/ppermute | solution.py:38
  94.4 51.6 %collective-permute-start.12 = (bf16[2,1024,128]{2,1,0:T(8,128)(2,1)}, bf16[2,1024,128]{2,1,0:T(8,128)(2,1)}, u32[]{:S(2)}, u32[]{:S(2)}) collective-permute-start(bf16[2,1024,128]{2,1,0:T(8,128)(2,1)} %pad_maximum_fusion.4), channel_id=1, source_target_pairs={{24,0},{32,8},{40,16},{48,24},{56,32},{64,40},{72,48},{80,56},{88,... | collective-permute-start | bytes 1572872 | tf_op jit(solution)/shard_map/ppermute | solution.py:18
  98.8 14.0 %collective-permute-start.8 = (f32[128,2,2,2,32]{0,4,3,2,1:T(8,128)S(1)}, f32[128,2,2,2,32]{0,4,3,2,1:T(8,128)S(1)}, u32[]{:S(2)}, u32[]{:S(2)}) collective-permute-start(f32[128,2,2,2,32]{0,4,3,2,1:T(8,128)S(1)} %fusion.92), channel_id=1, source_target_pairs={{0,16},{8,24},{16,0},{24,8},{32,48},{40,56},{48,32},{56,40},{64,80... | collective-permute-start | bytes 393224 | tf_op jit(solution)/shard_map/ppermute | solution.py:38
  109.6 36.4 %collective-permute-start.11 = (bf16[2,1024,128]{2,1,0:T(8,128)(2,1)}, bf16[2,1024,128]{2,1,0:T(8,128)(2,1)S(1)}, u32[]{:S(2)}, u32[]{:S(2)}) collective-permute-start(bf16[2,1024,128]{2,1,0:T(8,128)(2,1)} %pad_maximum_fusion.3), channel_id=1, source_target_pairs={{16,0},{24,8},{32,16},{40,24},{48,32},{56,40},{64,48},{72,56},{80,... | collective-permute-start | bytes 1572872 | tf_op jit(solution)/shard_map/ppermute | solution.py:18
  112.9 14.0 %collective-permute-start.9 = (f32[128,2,2,32]{0,3,2,1:T(8,128)S(1)}, f32[128,2,2,32]{0,3,2,1:T(8,128)S(1)}, u32[]{:S(2)}, u32[]{:S(2)}) collective-permute-start(f32[128,2,2,32]{0,3,2,1:T(8,128)S(1)} %fusion.93), channel_id=1, source_target_pairs={{0,32},{8,40},{16,48},{24,56},{32,0},{40,8},{48,16},{56,24},{64,96... | collective-permute-start | bytes 196616 | tf_op jit(solution)/shard_map/ppermute | solution.py:38
  120.1 10.1 %copy-start.9 = (f32[1024,1024]{1,0:T(8,128)S(1)}, f32[1024,1024]{1,0:T(8,128)}, u32[]{:S(2)}) copy-start(f32[1024,1024]{1,0:T(8,128)} %fusion.113) | copy-start | bytes 12582916
  120.1 10.1 %copy-start.19 = (bf16[1024,128]{1,0:T(8,128)(2,1)S(1)}, bf16[1024,128]{1,0:T(8,128)(2,1)}, u32[]{:S(2)}) copy-start(bf16[1024,128]{1,0:T(8,128)(2,1)} %param.10) | copy-start | bytes 786436
  121.7 24.3 %collective-permute-start.10 = (bf16[2,1024,128]{2,1,0:T(8,128)(2,1)}, bf16[2,1024,128]{2,1,0:T(8,128)(2,1)}, u32[]{:S(2)}, u32[]{:S(2)}) collective-permute-start(bf16[2,1024,128]{2,1,0:T(8,128)(2,1)} %pad_maximum_fusion.2), channel_id=1, source_target_pairs={{8,0},{16,8},{24,16},{32,24},{40,32},{48,40},{56,48},{64,56},{72,6... | collective-permute-start | bytes 1572872 | tf_op jit(solution)/shard_map/ppermute | solution.py:18
  127.0 11.1 %collective-permute-start.13 = (f32[128,2,32]{0,2,1:T(8,128)S(1)}, f32[128,2,32]{0,2,1:T(8,128)S(1)}, u32[]{:S(2)}, u32[]{:S(2)}) collective-permute-start(f32[128,2,32]{0,2,1:T(8,128)S(1)} %fusion.94), channel_id=1, source_target_pairs={{0,64},{8,72},{16,80},{24,88},{32,96},{40,104},{48,112},{56,120},{... | collective-permute-start | bytes 98312 | tf_op jit(solution)/shard_map/ppermute | solution.py:38
  138.1 7.3 %collective-permute-start.14 = (f32[128,32]{0,1:T(8,128)S(1)}, f32[128,32]{0,1:T(8,128)S(1)}, u32[]{:S(2)}, u32[]{:S(2)}) collective-permute-start(f32[128,32]{0,1:T(8,128)S(1)} %select_bitcast_fusion.1), channel_id=1, source_target_pairs={{0,128},{8,136},{16,144},{24,152},{32,160},{40,168},{48,176},{56,1... | collective-permute-start | bytes 49160 | tf_op jit(solution)/shard_map/ppermute | solution.py:38
  (15 other events, 58.0 us)

commit v8 on v4

--- a/solution.py
+++ b/solution.py
@@ -104,17 +104,27 @@
         )
         for k in range(1, pair_count)
     ]
-    column_block = jnp.concatenate(gathered_blocks, axis=1)
     block_width = grad_out.shape[1]
     slot = jnp.arange(head_devices)
     source_block = 2 * ((pair_index - slot // 2) % pair_count) + slot % 2
     w_blocks = w_out.reshape(w_out.shape[0], head_devices, block_width)
-    w_in_order = jnp.take(w_blocks, source_block, axis=1).reshape(w_out.shape)
-    grad_mixed = lax.dot_general(
-        column_block, w_in_order, (((1,), (1,)), ((), ())), preferred_element_type=jnp.float32
-    )
-    product = lax.dot_general(
-        mixed, column_block, (((0,), (0,)), ((), ())), preferred_element_type=jnp.float32
+    w_in_order = jnp.take(w_blocks, source_block, axis=1).reshape(
+        w_out.shape[0], len(gathered_blocks), -1
+    )
+    grad_mixed = sum(
+        lax.dot_general(
+            gathered, w_in_order[:, k], (((1,), (1,)), ((), ())), preferred_element_type=jnp.float32
+        )
+        for k, gathered in enumerate(gathered_blocks)
+    )
+    product = jnp.concatenate(
+        [
+            lax.dot_general(
+                mixed, gathered, (((0,), (0,)), ((), ())), preferred_element_type=jnp.float32
+            )
+            for gathered in gathered_blocks
+        ],
+        axis=1,
     )
     weight_rows = jnp.take(
         product.reshape(product.shape[0], head_devices, block_width), source_block, axis=1

time: 144 us -> 140 us (0.972)
  local copies, waits for them, and re-layouts: 12.4 us -> 8.92 us
  waiting for transfers between devices: 31.3 us -> 34.1 us
  starting transfers between devices: 40.3 us -> 38.7 us
    ppermute x3, waiting for transfers between devices: 2.93 us -> 5.85 us  [per_device(): lax.ppermute(pair_block, 'head', [(i, (i + 2 * k) % head_devices) for i i...]
    dot_general x1 -> x0, local copies, waits for them, and re-layouts: 2.64 us -> none  [per_device(): lax.dot_general(mixed, column_block, (((0,), (0,)), ((), ())), preferred_...]
    dot_general x2 -> x8, matrix products: 3.53 us -> 2.27 us  [the longest x4 1.31 us: per_device(): lax.dot_general(gathered, w_in_order[:, k], (((1,), (1,)), ((), ())), pre...]
    unnamed x69 -> x61, local copies, waits for them, and re-layouts: 6.94 us -> 6.07 us
  transfers between devices with their start and end apart: 15 -> 15, of which waited for: 5 -> 6; matrix products, arithmetic and copies ran while one was open for 36% -> 36% of each run, Pallas kernels for 0% -> 0%
where the time goes in v8:
time: 140 us; the launch traced here: 138 us
  matrix products  45.6 us (33%)
  starting transfers between devices  38.7 us (28%)
  waiting for transfers between devices  34.1 us (24%)
  local copies, waits for them, and re-layouts  8.92 us (6%)
  other arithmetic  8.09 us (6%)
  between operations  2.17 us (2%)
    ppermute x6, starting transfers between devices, shifted(): return lax.ppermute(block, axis, route)  16.6 us
    ppermute x1, waiting for transfers between devices, per_device(): lax.ppermute(grad_out, 'head', [(i, i ^ 1) for i in range(head_devices)])  16.3 us
    ppermute x5, starting transfers between devices, halving_step(): return keep + lax.ppermute(send, axis, [(i, i ^ bit) for i in range(count)])  15.7 us
    dot_general x4, matrix products, pair_scores(): jnp.einsum('ihd,jhd->hij', query_heads, k_heads, preferred_element_type=j...  14.2 us
    dot_general x4, matrix products, per_device(): jnp.einsum('ihd,jhd->hij', grad_attended, v_heads, preferred_element_type...  13.7 us
    ppermute x5, waiting for transfers between devices, halving_step(): return keep + lax.ppermute(send, axis, [(i, i ^ bit) for i in range(count)])  7.42 us
    unnamed x61, local copies, waits for them, and re-layouts  6.07 us
    ppermute x3, waiting for transfers between devices, per_device(): lax.ppermute(pair_block, 'head', [(i, (i + 2 * k) % head_devices) for i i...  5.85 us
  transfers between devices with their start and end apart: 15, of which 6 were waited for; matrix products, arithmetic and copies ran while one was open for 36% of the time, Pallas kernels for 0%

profile of v8, /device:TPU:1, one launch (start us, length us, event | category | flops | bytes accessed | tf_op | source)
XLA Modules:
  0.0 137.6 jit_solution(3691250831761158655)
XLA Ops:
  2.5 5.0 %collective-permute-start.6 = (bf16[2056,128]{1,0:T(8,128)(2,1)S(1)}, bf16[2056,128]{1,0:T(8,128)(2,1)S(1)}, u32[]{:S(2)}, u32[]{:S(2)}) collective-permute-start(bf16[2056,128]{1,0:T(8,128)(2,1)S(1)} %pad_maximum_fusion), channel_id=1, source_target_pairs={{0,24},{8,32},{16,40},{24,48},{32,56},{40,64},{48,72},{56,80},{64,... | collective-permute-start | bytes 1579016 | tf_op jit(solution)/shard_map/ppermute | solution.py:18
  7.5 3.2 %collective-permute-start.5 = (bf16[2056,128]{1,0:T(8,128)(2,1)S(1)}, bf16[2056,128]{1,0:T(8,128)(2,1)S(1)}, u32[]{:S(2)}, u32[]{:S(2)}) collective-permute-start(bf16[2056,128]{1,0:T(8,128)(2,1)S(1)} %pad_maximum_fusion), channel_id=1, source_target_pairs={{0,16},{8,24},{16,32},{24,40},{32,48},{40,56},{48,64},{56,72},{64,... | collective-permute-start | bytes 1579016 | tf_op jit(solution)/shard_map/ppermute | solution.py:18
  10.7 3.1 %collective-permute-start.4 = (bf16[2056,128]{1,0:T(8,128)(2,1)S(1)}, bf16[2056,128]{1,0:T(8,128)(2,1)S(1)}, u32[]{:S(2)}, u32[]{:S(2)}) collective-permute-start(bf16[2056,128]{1,0:T(8,128)(2,1)S(1)} %pad_maximum_fusion), channel_id=1, source_target_pairs={{0,8},{8,16},{16,24},{24,32},{32,40},{40,48},{48,56},{56,64},{64,7... | collective-permute-start | bytes 1579016 | tf_op jit(solution)/shard_map/ppermute | solution.py:18
  13.7 2.7 %collective-permute-start = (bf16[1024,128]{1,0:T(8,128)(2,1)}, bf16[1024,128]{1,0:T(8,128)(2,1)}, u32[]{:S(2)}, u32[]{:S(2)}) collective-permute-start(bf16[1024,128]{1,0:T(8,128)(2,1)} %param.14), channel_id=1, source_target_pairs={{0,1},{1,0},{2,3},{3,2},{4,5},{5,4},{6,7},{7,6},{8,9},{9,8},{10,11... | collective-permute-start | bytes 786440 | tf_op jit(solution)/shard_map/ppermute | solution.py:92
  16.5 3.7 %fusion.111 = f32[1024,1024]{1,0:T(8,128)} fusion(bf16[1024,128]{1,0:T(8,128)(2,1)S(1)} %copy-done, bf16[1024,128]{1,0:T(8,128)(2,1)} %param.9), kind=kOutput, calls=%fused_computation.215 | convolution fusion | flops 268435456 | bytes 4718592 | tf_op jit(solution)/shard_map/ihd,jhd->hij/dot_general | solution.py:75
  22.6 16.3 %collective-permute-done = bf16[1024,128]{1,0:T(8,128)(2,1)} collective-permute-done((bf16[1024,128]{1,0:T(8,128)(2,1)}, bf16[1024,128]{1,0:T(8,128)(2,1)}, u32[]{:S(2)}, u32[]{:S(2)}) %collective-permute-start) | collective-permute-done | bytes 262176 | tf_op jit(solution)/shard_map/ppermute | solution.py:92
  40.4 2.6 %collective-permute-start.3 = (bf16[1024,256]{1,0:T(8,128)(2,1)S(1)}, bf16[1024,256]{1,0:T(8,128)(2,1)S(1)}, u32[]{:S(2)}, u32[]{:S(2)}) collective-permute-start(bf16[1024,256]{1,0:T(8,128)(2,1)S(1)} %maximum_select_fusion), channel_id=1, source_target_pairs={{0,6},{1,7},{2,0},{3,1},{4,2},{5,3},{6,4},{7,5},{8,14},{9,15},{10,... | collective-permute-start | bytes 1572872 | tf_op jit(solution)/shard_map/ppermute | solution.py:102
  45.6 1.9 %copy-done.9 = f32[1024,1024]{1,0:T(8,128)S(1)} copy-done((f32[1024,1024]{1,0:T(8,128)S(1)}, f32[1024,1024]{1,0:T(8,128)}, u32[]{:S(2)}) %copy-start.9) | copy-done | bytes 4194328
  47.5 9.1 %fusion.26 = (bf16[1024,1024]{1,0:T(8,128)(2,1)S(1)}, bf16[1024,1024]{1,0:T(8,128)(2,1)S(1)}, bf16[1024,1024]{1,0:T(8,128)(2,1)S(1)}, bf16[1024,1024]{1,0:T(8,128)(2,1)S(1)}, f32[1024,1024]{0,1:T(8,128)}) fusion(s32[1024]{0:T(1024)S(1)} %fusion.100, f32[]{:T(128)} %bitcast.389, pred[]{:T(512)S(6)} %ge.27, s32[1024]{0:T(1024)S(1)} %copy-done.27, ...), kind=kOutput, calls=%fused_computation.37 | convolution fusion | flops 312475648 | bytes 25711620 | tf_op jit(solution)/shard_map/ihd,jhd->hij/dot_general | solution.py:75
  60.9 2.6 %collective-permute-done.3 = bf16[1024,256]{1,0:T(8,128)(2,1)S(1)} collective-permute-done((bf16[1024,256]{1,0:T(8,128)(2,1)S(1)}, bf16[1024,256]{1,0:T(8,128)(2,1)S(1)}, u32[]{:S(2)}, u32[]{:S(2)}) %collective-permute-start.3) | collective-permute-done | bytes 524320 | tf_op jit(solution)/shard_map/ppermute | solution.py:102
  64.2 3.3 %collective-permute-done.1 = bf16[1024,256]{1,0:T(8,128)(2,1)S(1)} collective-permute-done((bf16[1024,256]{1,0:T(8,128)(2,1)S(1)}, bf16[1024,256]{1,0:T(8,128)(2,1)S(1)}, u32[]{:S(2)}, u32[]{:S(2)}) %collective-permute-start.1) | collective-permute-done | bytes 524320 | tf_op jit(solution)/shard_map/ppermute | solution.py:102
  72.3 5.1 %select_convert_fusion = bf16[1024,1024]{1,0:T(8,128)(2,1)S(1)} fusion(f32[1024,1024]{1,0:T(8,128)} %fusion.111, bf16[1024,128]{1,0:T(8,128)(2,1)S(1)} %copy-done.22, f32[]{:T(128)} %bitcast.388, s32[1024]{0:T(1024)S(1)} %copy-done.27, pred[]{:T(512)S(6)} %ge.25, bf16[1024,1,128]{0,2,1:T(8,128)(2,1)S(1)} %get-tuple-element.15), kind=kOutput, calls=%fused_computation.44 | convolution fusion | flops 286261248 | bytes 6819845 | tf_op jit(solution)/shard_map/ihd,jhd->hij/dot_general | solution.py:158
  80.7 2.0 %copy.103 = f32[1024,128]{1,0:T(8,128)} copy(f32[1024,128]{0,1:T(8,128)} %get-tuple-element.32) | data formatting | bytes 1048576
  85.1 2.9 %fusion.32 = bf16[1024,1024]{1,0:T(8,128)(2,1)S(1)} fusion(f32[1024,1024]{0,1:T(8,128)S(1)} %copy-done.28, s32[1024]{0:T(1024)S(1)} %fusion.100, f32[]{:T(128)} %bitcast.387, pred[]{:T(512)S(6)} %ge.27, s32[1024]{0:T(1024)S(1)} %copy-done.27, bf16[1024,1,128]{0,2,1:T(8,128)(2,1)S(1)} %get-tuple-element.15, bf16[2056,128]{1,0:T(8,128)(2,1)S(1)} %copy-done.24), kind=kOutput, calls=%fused_computation.43 | convolution fusion | flops 284164096 | bytes 6823941 | tf_op jit(solution)/shard_map/ihd,jhd->hij/dot_general | solution.py:158
  90.6 2.1 %collective-permute-start.10 = (bf16[2,1024,128]{2,1,0:T(8,128)(2,1)S(1)}, bf16[2,1024,128]{2,1,0:T(8,128)(2,1)S(1)}, u32[]{:S(2)}, u32[]{:S(2)}) collective-permute-start(bf16[2,1024,128]{2,1,0:T(8,128)(2,1)S(1)} %pad_maximum_fusion.1), channel_id=1, source_target_pairs={{8,0},{16,8},{24,16},{32,24},{40,32},{48,40},{56,48},{64,56},{72,6... | collective-permute-start | bytes 1572872 | tf_op jit(solution)/shard_map/ppermute | solution.py:18
  92.8 8.8 %collective-permute-start.9 = (f32[128,2,2,32]{0,3,2,1:T(8,128)S(1)}, f32[128,2,2,32]{0,3,2,1:T(8,128)S(1)}, u32[]{:S(2)}, u32[]{:S(2)}) collective-permute-start(f32[128,2,2,32]{0,3,2,1:T(8,128)S(1)} %fusion.92), channel_id=1, source_target_pairs={{0,32},{8,40},{16,48},{24,56},{32,0},{40,8},{48,16},{56,24},{64,96... | collective-permute-start | bytes 196616 | tf_op jit(solution)/shard_map/ppermute | solution.py:38
  102.6 2.9 %fusion.21 = bf16[1024,1024]{1,0:T(8,128)(2,1)S(1)} fusion(f32[1024,1024]{0,1:T(8,128)S(1)} %copy-done.13, s32[1024]{0:T(1024)S(1)} %fusion.99, f32[]{:T(128)} %bitcast.391, pred[]{:T(512)S(6)} %ge.28, s32[1024]{0:T(1024)S(1)} %copy-done.27, bf16[1024,1,128]{0,2,1:T(8,128)(2,1)S(1)} %get-tuple-element.15, bf16[2056,128]{1,0:T(8,128)(2,1)S(1)} %copy-done.20), kind=kOutput, calls=%fused_computation.29 | convolution fusion | flops 284164096 | bytes 6823941 | tf_op jit(solution)/shard_map/ihd,jhd->hij/dot_general | solution.py:158
  106.4 1.8 %collective-permute-start.11 = (bf16[2,1024,128]{2,1,0:T(8,128)(2,1)S(1)}, bf16[2,1024,128]{2,1,0:T(8,128)(2,1)S(1)}, u32[]{:S(2)}, u32[]{:S(2)}) collective-permute-start(bf16[2,1024,128]{2,1,0:T(8,128)(2,1)S(1)} %pad_maximum_fusion.2), channel_id=1, source_target_pairs={{16,0},{24,8},{32,16},{40,24},{48,32},{56,40},{64,48},{72,56},{80,... | collective-permute-start | bytes 1572872 | tf_op jit(solution)/shard_map/ppermute | solution.py:18
  109.0 4.0 %collective-permute-start.13 = (f32[128,2,32]{0,2,1:T(8,128)S(1)}, f32[128,2,32]{0,2,1:T(8,128)S(1)}, u32[]{:S(2)}, u32[]{:S(2)}) collective-permute-start(f32[128,2,32]{0,2,1:T(8,128)S(1)} %fusion.93), channel_id=1, source_target_pairs={{0,64},{8,72},{16,80},{24,88},{32,96},{40,104},{48,112},{56,120},{... | collective-permute-start | bytes 98312 | tf_op jit(solution)/shard_map/ppermute | solution.py:38
  114.0 2.9 %fusion.10 = bf16[1024,1024]{1,0:T(8,128)(2,1)S(1)} fusion(f32[1024,1024]{0,1:T(8,128)S(1)} %copy-done.11, s32[1024]{0:T(1024)S(1)} %fusion.98, f32[]{:T(128)} %bitcast.390, pred[]{:T(512)S(6)} %ge.29, s32[1024]{0:T(1024)S(1)} %copy-done.27, bf16[1024,1,128]{0,2,1:T(8,128)(2,1)S(1)} %get-tuple-element.15, bf16[2056,128]{1,0:T(8,128)(2,1)S(1)} %copy-done.18), kind=kOutput, calls=%fused_computation.15 | convolution fusion | flops 284164096 | bytes 6823941 | tf_op jit(solution)/shard_map/ihd,jhd->hij/dot_general | solution.py:158
  119.9 4.7 %collective-permute-done.13 = f32[128,2,32]{0,2,1:T(8,128)S(1)} collective-permute-done((f32[128,2,32]{0,2,1:T(8,128)S(1)}, f32[128,2,32]{0,2,1:T(8,128)S(1)}, u32[]{:S(2)}, u32[]{:S(2)}) %collective-permute-start.13) | collective-permute-done | bytes 32800 | tf_op jit(solution)/shard_map/ppermute | solution.py:38
  124.6 2.3 %collective-permute-start.14 = (f32[128,32]{0,1:T(8,128)S(1)}, f32[128,32]{0,1:T(8,128)S(1)}, u32[]{:S(2)}, u32[]{:S(2)}) collective-permute-start(f32[128,32]{0,1:T(8,128)S(1)} %select_bitcast_fusion.1), channel_id=1, source_target_pairs={{0,128},{8,136},{16,144},{24,152},{32,160},{40,168},{48,176},{56,1... | collective-permute-start | bytes 49160 | tf_op jit(solution)/shard_map/ppermute | solution.py:38
  128.5 2.7 %collective-permute-done.14 = f32[128,32]{0,1:T(8,128)S(1)} collective-permute-done((f32[128,32]{0,1:T(8,128)S(1)}, f32[128,32]{0,1:T(8,128)S(1)}, u32[]{:S(2)}, u32[]{:S(2)}) %collective-permute-start.14) | collective-permute-done | bytes 16416 | tf_op jit(solution)/shard_map/ppermute | solution.py:38
  131.8 4.5 %collective-permute-done.12 = bf16[2,1024,128]{2,1,0:T(8,128)(2,1)S(1)} collective-permute-done((bf16[2,1024,128]{2,1,0:T(8,128)(2,1)S(1)}, bf16[2,1024,128]{2,1,0:T(8,128)(2,1)S(1)}, u32[]{:S(2)}, u32[]{:S(2)}) %collective-permute-start.12) | collective-permute-done | bytes 524320 | tf_op jit(solution)/shard_map/ppermute | solution.py:18
  (139 shorter events, 35.2 us)
Async XLA Ops:
  0.6 15.9 %copy-start = (bf16[1024,128]{1,0:T(8,128)(2,1)S(1)}, bf16[1024,128]{1,0:T(8,128)(2,1)}, u32[]{:S(2)}) copy-start(bf16[1024,128]{1,0:T(8,128)(2,1)} %param.8) | copy-start | bytes 786436
  0.6 20.4 %copy-start.25 = (bf16[128,1024]{1,0:T(8,128)(2,1)S(1)}, bf16[128,1024]{1,0:T(8,128)(2,1)}, u32[]{:S(2)}) copy-start(bf16[128,1024]{1,0:T(8,128)(2,1)} %param.15) | copy-start | bytes 786436
  0.7 21.5 %copy-start.26 = (bf16[1024,128]{1,0:T(8,128)(2,1)S(1)}, bf16[1024,128]{1,0:T(8,128)(2,1)}, u32[]{:S(2)}) copy-start(bf16[1024,128]{1,0:T(8,128)(2,1)} %param.11) | copy-start | bytes 786436
  2.5 41.0 %collective-permute-start.6 = (bf16[2056,128]{1,0:T(8,128)(2,1)S(1)}, bf16[2056,128]{1,0:T(8,128)(2,1)S(1)}, u32[]{:S(2)}, u32[]{:S(2)}) collective-permute-start(bf16[2056,128]{1,0:T(8,128)(2,1)S(1)} %pad_maximum_fusion), channel_id=1, source_target_pairs={{0,24},{8,32},{16,40},{24,48},{32,56},{40,64},{48,72},{56,80},{64,... | collective-permute-start | bytes 1579016 | tf_op jit(solution)/shard_map/ppermute | solution.py:18
  7.5 37.3 %collective-permute-start.5 = (bf16[2056,128]{1,0:T(8,128)(2,1)S(1)}, bf16[2056,128]{1,0:T(8,128)(2,1)S(1)}, u32[]{:S(2)}, u32[]{:S(2)}) collective-permute-start(bf16[2056,128]{1,0:T(8,128)(2,1)S(1)} %pad_maximum_fusion), channel_id=1, source_target_pairs={{0,16},{8,24},{16,32},{24,40},{32,48},{40,56},{48,64},{56,72},{64,... | collective-permute-start | bytes 1579016 | tf_op jit(solution)/shard_map/ppermute | solution.py:18
  10.7 34.9 %collective-permute-start.4 = (bf16[2056,128]{1,0:T(8,128)(2,1)S(1)}, bf16[2056,128]{1,0:T(8,128)(2,1)S(1)}, u32[]{:S(2)}, u32[]{:S(2)}) collective-permute-start(bf16[2056,128]{1,0:T(8,128)(2,1)S(1)} %pad_maximum_fusion), channel_id=1, source_target_pairs={{0,8},{8,16},{16,24},{24,32},{32,40},{40,48},{48,56},{56,64},{64,7... | collective-permute-start | bytes 1579016 | tf_op jit(solution)/shard_map/ppermute | solution.py:18
  13.7 25.2 %collective-permute-start = (bf16[1024,128]{1,0:T(8,128)(2,1)}, bf16[1024,128]{1,0:T(8,128)(2,1)}, u32[]{:S(2)}, u32[]{:S(2)}) collective-permute-start(bf16[1024,128]{1,0:T(8,128)(2,1)} %param.14), channel_id=1, source_target_pairs={{0,1},{1,0},{2,3},{3,2},{4,5},{5,4},{6,7},{7,6},{8,9},{9,8},{10,11... | collective-permute-start | bytes 786440 | tf_op jit(solution)/shard_map/ppermute | solution.py:92
  40.4 23.1 %collective-permute-start.3 = (bf16[1024,256]{1,0:T(8,128)(2,1)S(1)}, bf16[1024,256]{1,0:T(8,128)(2,1)S(1)}, u32[]{:S(2)}, u32[]{:S(2)}) collective-permute-start(bf16[1024,256]{1,0:T(8,128)(2,1)S(1)} %maximum_select_fusion), channel_id=1, source_target_pairs={{0,6},{1,7},{2,0},{3,1},{4,2},{5,3},{6,4},{7,5},{8,14},{9,15},{10,... | collective-permute-start | bytes 1572872 | tf_op jit(solution)/shard_map/ppermute | solution.py:102
  42.9 20.9 %collective-permute-start.2 = (bf16[1024,256]{1,0:T(8,128)(2,1)S(1)}, bf16[1024,256]{1,0:T(8,128)(2,1)S(1)}, u32[]{:S(2)}, u32[]{:S(2)}) collective-permute-start(bf16[1024,256]{1,0:T(8,128)(2,1)S(1)} %maximum_select_fusion), channel_id=1, source_target_pairs={{0,4},{1,5},{2,6},{3,7},{4,0},{5,1},{6,2},{7,3},{8,12},{9,13},{10,... | collective-permute-start | bytes 1572872 | tf_op jit(solution)/shard_map/ppermute | solution.py:102
  43.5 14.9 %copy-start.17 = (bf16[2056,128]{1,0:T(8,128)(2,1)}, bf16[2056,128]{1,0:T(8,128)(2,1)S(1)}, u32[]{:S(2)}) copy-start(bf16[2056,128]{1,0:T(8,128)(2,1)S(1)} %collective-permute-done.6) | copy-start | bytes 1579012
  43.5 23.9 %collective-permute-start.1 = (bf16[1024,256]{1,0:T(8,128)(2,1)S(1)}, bf16[1024,256]{1,0:T(8,128)(2,1)S(1)}, u32[]{:S(2)}, u32[]{:S(2)}) collective-permute-start(bf16[1024,256]{1,0:T(8,128)(2,1)S(1)} %maximum_select_fusion), channel_id=1, source_target_pairs={{0,2},{1,3},{2,4},{3,5},{4,6},{5,7},{6,0},{7,1},{8,10},{9,11},{10,... | collective-permute-start | bytes 1572872 | tf_op jit(solution)/shard_map/ppermute | solution.py:102
  45.6 13.7 %copy-start.23 = (bf16[2056,128]{1,0:T(8,128)(2,1)}, bf16[2056,128]{1,0:T(8,128)(2,1)S(1)}, u32[]{:S(2)}) copy-start(bf16[2056,128]{1,0:T(8,128)(2,1)S(1)} %collective-permute-done.4) | copy-start | bytes 1579012
  71.9 11.6 %collective-permute-start.7 = (f32[128,2,2,2,2,32]{0,5,4,3,2,1:T(8,128)}, f32[128,2,2,2,2,32]{0,5,4,3,2,1:T(8,128)}, u32[]{:S(2)}, u32[]{:S(2)}) collective-permute-start(f32[128,2,2,2,2,32]{0,5,4,3,2,1:T(8,128)} %select_bitcast_fusion), channel_id=1, source_target_pairs={{0,8},{8,0},{16,24},{24,16},{32,40},{40,32},{48,56},{56,48},{64,72... | collective-permute-start | bytes 786440 | tf_op jit(solution)/shard_map/ppermute | solution.py:38
  84.9 7.9 %collective-permute-start.8 = (f32[128,2,2,2,32]{0,4,3,2,1:T(8,128)S(1)}, f32[128,2,2,2,32]{0,4,3,2,1:T(8,128)S(1)}, u32[]{:S(2)}, u32[]{:S(2)}) collective-permute-start(f32[128,2,2,2,32]{0,4,3,2,1:T(8,128)S(1)} %fusion.88), channel_id=1, source_target_pairs={{0,16},{8,24},{16,0},{24,8},{32,48},{40,56},{48,32},{56,40},{64,80... | collective-permute-start | bytes 393224 | tf_op jit(solution)/shard_map/ppermute | solution.py:38
  88.0 13.7 %copy-start.6 = (bf16[1024,1024]{1,0:T(8,128)(2,1)S(1)}, bf16[1024,1024]{1,0:T(8,128)(2,1)}, u32[]{:S(2)}) copy-start(bf16[1024,1024]{1,0:T(8,128)(2,1)} %copy-done.5) | copy-start | bytes 6291460
  89.6 13.0 %copy-start.13 = (f32[1024,1024]{0,1:T(8,128)S(1)}, f32[1024,1024]{0,1:T(8,128)}, u32[]{:S(2)}) copy-start(f32[1024,1024]{0,1:T(8,128)} %copy-done.12) | copy-start | bytes 12582916
  89.6 13.0 %copy-start.20 = (bf16[2056,128]{1,0:T(8,128)(2,1)S(1)}, bf16[2056,128]{1,0:T(8,128)(2,1)}, u32[]{:S(2)}) copy-start(bf16[2056,128]{1,0:T(8,128)(2,1)} %copy-done.19) | copy-start | bytes 1579012
  90.6 41.2 %collective-permute-start.10 = (bf16[2,1024,128]{2,1,0:T(8,128)(2,1)S(1)}, bf16[2,1024,128]{2,1,0:T(8,128)(2,1)S(1)}, u32[]{:S(2)}, u32[]{:S(2)}) collective-permute-start(bf16[2,1024,128]{2,1,0:T(8,128)(2,1)S(1)} %pad_maximum_fusion.1), channel_id=1, source_target_pairs={{8,0},{16,8},{24,16},{32,24},{40,32},{48,40},{56,48},{64,56},{72,6... | collective-permute-start | bytes 1572872 | tf_op jit(solution)/shard_map/ppermute | solution.py:18
  92.8 16.1 %collective-permute-start.9 = (f32[128,2,2,32]{0,3,2,1:T(8,128)S(1)}, f32[128,2,2,32]{0,3,2,1:T(8,128)S(1)}, u32[]{:S(2)}, u32[]{:S(2)}) collective-permute-start(f32[128,2,2,32]{0,3,2,1:T(8,128)S(1)} %fusion.92), channel_id=1, source_target_pairs={{0,32},{8,40},{16,48},{24,56},{32,0},{40,8},{48,16},{56,24},{64,96... | collective-permute-start | bytes 196616 | tf_op jit(solution)/shard_map/ppermute | solution.py:38
  106.4 25.4 %collective-permute-start.11 = (bf16[2,1024,128]{2,1,0:T(8,128)(2,1)S(1)}, bf16[2,1024,128]{2,1,0:T(8,128)(2,1)S(1)}, u32[]{:S(2)}, u32[]{:S(2)}) collective-permute-start(bf16[2,1024,128]{2,1,0:T(8,128)(2,1)S(1)} %pad_maximum_fusion.2), channel_id=1, source_target_pairs={{16,0},{24,8},{32,16},{40,24},{48,32},{56,40},{64,48},{72,56},{80,... | collective-permute-start | bytes 1572872 | tf_op jit(solution)/shard_map/ppermute | solution.py:18
  109.0 15.6 %collective-permute-start.13 = (f32[128,2,32]{0,2,1:T(8,128)S(1)}, f32[128,2,32]{0,2,1:T(8,128)S(1)}, u32[]{:S(2)}, u32[]{:S(2)}) collective-permute-start(f32[128,2,32]{0,2,1:T(8,128)S(1)} %fusion.93), channel_id=1, source_target_pairs={{0,64},{8,72},{16,80},{24,88},{32,96},{40,104},{48,112},{56,120},{... | collective-permute-start | bytes 98312 | tf_op jit(solution)/shard_map/ppermute | solution.py:38
  117.7 18.6 %copy-start.15 = (f32[1,1024,128]{2,1,0:T(8,128)S(1)}, f32[1,1024,128]{2,1,0:T(8,128)}, u32[]{:S(2)}) copy-start(f32[1,1024,128]{2,1,0:T(8,128)} %convolution_bitcast_fusion) | copy-start | bytes 1572868
  117.8 18.5 %collective-permute-start.12 = (bf16[2,1024,128]{2,1,0:T(8,128)(2,1)S(1)}, bf16[2,1024,128]{2,1,0:T(8,128)(2,1)S(1)}, u32[]{:S(2)}, u32[]{:S(2)}) collective-permute-start(bf16[2,1024,128]{2,1,0:T(8,128)(2,1)S(1)} %pad_maximum_fusion.3), channel_id=1, source_target_pairs={{24,0},{32,8},{40,16},{48,24},{56,32},{64,40},{72,48},{80,56},{88,... | collective-permute-start | bytes 1572872 | tf_op jit(solution)/shard_map/ppermute | solution.py:18
  124.6 6.6 %collective-permute-start.14 = (f32[128,32]{0,1:T(8,128)S(1)}, f32[128,32]{0,1:T(8,128)S(1)}, u32[]{:S(2)}, u32[]{:S(2)}) collective-permute-start(f32[128,32]{0,1:T(8,128)S(1)} %select_bitcast_fusion.1), channel_id=1, source_target_pairs={{0,128},{8,136},{16,144},{24,152},{32,160},{40,168},{48,176},{56,1... | collective-permute-start | bytes 49160 | tf_op jit(solution)/shard_map/ppermute | solution.py:38
  (20 other events, 116.7 us)

commit v9 on v8

--- a/solution.py
+++ b/solution.py
@@ -4,6 +4,7 @@
 import jax.numpy as jnp
 from jax import lax
 from jax.sharding import PartitionSpec as P
+
 
 DH = 128
 
@@ -28,8 +29,9 @@
 def halving_step(current, axis, level):
     count = lax.axis_size(axis)
     my_index = lax.axis_index(axis)
-    bit = 1 << level
-    axis_pos = current.ndim - 2
+    levels = count.bit_length() - 1
+    bit = 1 << (levels - 1 - level)
+    axis_pos = 1
     mine = (my_index // bit) % 2
     low = lax.index_in_dim(current, 0, axis_pos, keepdims=False)
     high = lax.index_in_dim(current, 1, axis_pos, keepdims=False)
@@ -77,7 +79,7 @@
 
     attended = jnp.zeros((row_count, head_count, DH), jnp.float32)
     for k_heads, v_heads, allowed in prepared:
-        act, deriv = silu_parts(pair_scores(q_heads, k_heads))
+        act, _ = silu_parts(pair_scores(q_heads, k_heads))
         weights = jnp.where(allowed[None], act, 0.0).astype(jnp.bfloat16)
         attended = attended + jnp.einsum(
             "hij,jhd->ihd", weights, v_heads, preferred_element_type=jnp.float32

time: 140 us -> 145 us (1.036); the launches traced: 138 us -> 144 us
  starting transfers between devices: 38.7 us -> 44.1 us
  waiting for transfers between devices: 34.1 us -> 35.6 us
    ppermute x5, starting transfers between devices: 15.7 us -> 19.8 us  [halving_step(): return keep + lax.ppermute(send, axis, [(i, i ^ bit) for i in range(count)])]
    ppermute x6, waiting for transfers between devices: 4.48 us -> 7.39 us  [shifted(): return lax.ppermute(block, axis, route)]
  transfers between devices with their start and end apart: 15 -> 15, of which waited for: 6 -> 5; matrix products, arithmetic and copies ran while one was open for 36% -> 35% of each run, Pallas kernels for 0% -> 0%
where the time goes in v9:
time: 145 us; the launch traced here: 144 us
  matrix products  45.6 us (31%)
  starting transfers between devices  44.1 us (30%)
  waiting for transfers between devices  35.6 us (25%)
  local copies, waits for them, and re-layouts  8.76 us (6%)
  other arithmetic  8.1 us (6%)
  between operations  2.15 us (1%)
    ppermute x5, starting transfers between devices, halving_step(): return keep + lax.ppermute(send, axis, [(i, i ^ bit) for i in range(count)])  19.8 us
    ppermute x6, starting transfers between devices, shifted(): return lax.ppermute(block, axis, route)  17.9 us
    ppermute x1, waiting for transfers between devices, per_device(): lax.ppermute(grad_out, 'head', [(i, i ^ 1) for i in range(head_devices)])  16.3 us
    dot_general x4, matrix products, pair_scores(): jnp.einsum('ihd,jhd->hij', query_heads, k_heads, preferred_element_type=j...  14.2 us
    dot_general x4, matrix products, per_device(): jnp.einsum('ihd,jhd->hij', grad_attended, v_heads, preferred_element_type...  13.7 us
    ppermute x6, waiting for transfers between devices, shifted(): return lax.ppermute(block, axis, route)  7.39 us
    ppermute x5, waiting for transfers between devices, halving_step(): return keep + lax.ppermute(send, axis, [(i, i ^ bit) for i in range(count)])  6.06 us
    unnamed x61, local copies, waits for them, and re-layouts  5.91 us
  transfers between devices with their start and end apart: 15, of which 5 were waited for; matrix products, arithmetic and copies ran while one was open for 35% of the time, Pallas kernels for 0%

profile of v9, /device:TPU:1, one launch (start us, length us, event | category | flops | bytes accessed | tf_op | source)
XLA Modules:
  0.0 144.3 jit_solution(5186085954264949988)
XLA Ops:
  2.5 5.0 %collective-permute-start.6 = (bf16[2056,128]{1,0:T(8,128)(2,1)S(1)}, bf16[2056,128]{1,0:T(8,128)(2,1)S(1)}, u32[]{:S(2)}, u32[]{:S(2)}) collective-permute-start(bf16[2056,128]{1,0:T(8,128)(2,1)S(1)} %pad_maximum_fusion), channel_id=1, source_target_pairs={{0,24},{8,32},{16,40},{24,48},{32,56},{40,64},{48,72},{56,80},{64,... | collective-permute-start | bytes 1579016 | tf_op jit(solution)/shard_map/ppermute | solution.py:19
  7.5 3.2 %collective-permute-start.5 = (bf16[2056,128]{1,0:T(8,128)(2,1)S(1)}, bf16[2056,128]{1,0:T(8,128)(2,1)S(1)}, u32[]{:S(2)}, u32[]{:S(2)}) collective-permute-start(bf16[2056,128]{1,0:T(8,128)(2,1)S(1)} %pad_maximum_fusion), channel_id=1, source_target_pairs={{0,16},{8,24},{16,32},{24,40},{32,48},{40,56},{48,64},{56,72},{64,... | collective-permute-start | bytes 1579016 | tf_op jit(solution)/shard_map/ppermute | solution.py:19
  10.7 3.1 %collective-permute-start.4 = (bf16[2056,128]{1,0:T(8,128)(2,1)S(1)}, bf16[2056,128]{1,0:T(8,128)(2,1)S(1)}, u32[]{:S(2)}, u32[]{:S(2)}) collective-permute-start(bf16[2056,128]{1,0:T(8,128)(2,1)S(1)} %pad_maximum_fusion), channel_id=1, source_target_pairs={{0,8},{8,16},{16,24},{24,32},{32,40},{40,48},{48,56},{56,64},{64,7... | collective-permute-start | bytes 1579016 | tf_op jit(solution)/shard_map/ppermute | solution.py:19
  13.7 2.7 %collective-permute-start = (bf16[1024,128]{1,0:T(8,128)(2,1)}, bf16[1024,128]{1,0:T(8,128)(2,1)}, u32[]{:S(2)}, u32[]{:S(2)}) collective-permute-start(bf16[1024,128]{1,0:T(8,128)(2,1)} %param.14), channel_id=1, source_target_pairs={{0,1},{1,0},{2,3},{3,2},{4,5},{5,4},{6,7},{7,6},{8,9},{9,8},{10,11... | collective-permute-start | bytes 786440 | tf_op jit(solution)/shard_map/ppermute | solution.py:94
  16.5 3.7 %fusion.106 = f32[1024,1024]{1,0:T(8,128)} fusion(bf16[1024,128]{1,0:T(8,128)(2,1)S(1)} %copy-done, bf16[1024,128]{1,0:T(8,128)(2,1)} %param.9), kind=kOutput, calls=%fused_computation.207 | convolution fusion | flops 268435456 | bytes 4718592 | tf_op jit(solution)/shard_map/ihd,jhd->hij/dot_general | solution.py:77
  22.6 16.3 %collective-permute-done = bf16[1024,128]{1,0:T(8,128)(2,1)} collective-permute-done((bf16[1024,128]{1,0:T(8,128)(2,1)}, bf16[1024,128]{1,0:T(8,128)(2,1)}, u32[]{:S(2)}, u32[]{:S(2)}) %collective-permute-start) | collective-permute-done | bytes 262176 | tf_op jit(solution)/shard_map/ppermute | solution.py:94
  40.4 2.6 %collective-permute-start.3 = (bf16[1024,256]{1,0:T(8,128)(2,1)S(1)}, bf16[1024,256]{1,0:T(8,128)(2,1)S(1)}, u32[]{:S(2)}, u32[]{:S(2)}) collective-permute-start(bf16[1024,256]{1,0:T(8,128)(2,1)S(1)} %maximum_select_fusion), channel_id=1, source_target_pairs={{0,6},{1,7},{2,0},{3,1},{4,2},{5,3},{6,4},{7,5},{8,14},{9,15},{10,... | collective-permute-start | bytes 1572872 | tf_op jit(solution)/shard_map/ppermute | solution.py:104
  45.6 1.9 %copy-done.9 = f32[1024,1024]{1,0:T(8,128)S(1)} copy-done((f32[1024,1024]{1,0:T(8,128)S(1)}, f32[1024,1024]{1,0:T(8,128)}, u32[]{:S(2)}) %copy-start.9) | copy-done | bytes 4194328
  47.5 9.1 %fusion.26 = (bf16[1024,1024]{1,0:T(8,128)(2,1)S(1)}, bf16[1024,1024]{1,0:T(8,128)(2,1)S(1)}, bf16[1024,1024]{1,0:T(8,128)(2,1)S(1)}, bf16[1024,1024]{1,0:T(8,128)(2,1)S(1)}, f32[1024,1024]{0,1:T(8,128)}) fusion(s32[1024]{0:T(1024)S(1)} %fusion.95, f32[]{:T(128)} %bitcast.345, pred[]{:T(512)S(6)} %ge.27, s32[1024]{0:T(1024)S(1)} %copy-done.27, ...), kind=kOutput, calls=%fused_computation.37 | convolution fusion | flops 312475648 | bytes 25711620 | tf_op jit(solution)/shard_map/ihd,jhd->hij/dot_general | solution.py:77
  60.9 2.6 %collective-permute-done.3 = bf16[1024,256]{1,0:T(8,128)(2,1)S(1)} collective-permute-done((bf16[1024,256]{1,0:T(8,128)(2,1)S(1)}, bf16[1024,256]{1,0:T(8,128)(2,1)S(1)}, u32[]{:S(2)}, u32[]{:S(2)}) %collective-permute-start.3) | collective-permute-done | bytes 524320 | tf_op jit(solution)/shard_map/ppermute | solution.py:104
  64.2 3.3 %collective-permute-done.1 = bf16[1024,256]{1,0:T(8,128)(2,1)S(1)} collective-permute-done((bf16[1024,256]{1,0:T(8,128)(2,1)S(1)}, bf16[1024,256]{1,0:T(8,128)(2,1)S(1)}, u32[]{:S(2)}, u32[]{:S(2)}) %collective-permute-start.1) | collective-permute-done | bytes 524320 | tf_op jit(solution)/shard_map/ppermute | solution.py:104
  71.9 7.8 %collective-permute-start.7 = (f32[128,2,2,2,2,32]{0,5,4,3,2,1:T(8,128)}, f32[128,2,2,2,2,32]{0,5,4,3,2,1:T(8,128)}, u32[]{:S(2)}, u32[]{:S(2)}) collective-permute-start(f32[128,2,2,2,2,32]{0,5,4,3,2,1:T(8,128)} %select_bitcast_fusion), channel_id=1, source_target_pairs={{0,128},{8,136},{16,144},{24,152},{32,160},{40,168},{48,176},{56,1... | collective-permute-start | bytes 786440 | tf_op jit(solution)/shard_map/ppermute | solution.py:40
  79.7 5.1 %select_convert_fusion = bf16[1024,1024]{1,0:T(8,128)(2,1)S(1)} fusion(f32[1024,1024]{1,0:T(8,128)} %fusion.106, bf16[1024,128]{1,0:T(8,128)(2,1)S(1)} %copy-done.22, f32[]{:T(128)} %bitcast.344, s32[1024]{0:T(1024)S(1)} %copy-done.27, pred[]{:T(512)S(6)} %ge.25, bf16[1024,1,128]{0,2,1:T(8,128)(2,1)S(1)} %get-tuple-element.15), kind=kOutput, calls=%fused_computation.44 | convolution fusion | flops 286261248 | bytes 6819845 | tf_op jit(solution)/shard_map/ihd,jhd->hij/dot_general | solution.py:160
  86.3 1.8 %convolution_bitcast_fusion = f32[1,1024,128]{2,1,0:T(8,128)} fusion(bf16[1024,1024]{1,0:T(8,128)(2,1)S(1)} %copy-done.8, bf16[1024,1,128]{0,2,1:T(8,128)(2,1)S(1)} %get-tuple-element.15), kind=kOutput, calls=%fused_computation.56 | convolution fusion | flops 268435456 | bytes 2883584 | tf_op jit(solution)/shard_map/hij,ihd->jhd/dot_general | solution.py:157
  88.1 2.0 %copy.72 = f32[1024,128]{1,0:T(8,128)} copy(f32[1024,128]{0,1:T(8,128)} %get-tuple-element.32) | data formatting | bytes 1048576
  92.3 2.0 %collective-permute-start.8 = (f32[128,2,2,2,32]{0,4,3,2,1:T(8,128)S(1)}, f32[128,2,2,2,32]{0,4,3,2,1:T(8,128)S(1)}, u32[]{:S(2)}, u32[]{:S(2)}) collective-permute-start(f32[128,2,2,2,32]{0,4,3,2,1:T(8,128)S(1)} %select_bitcast_fusion.1), channel_id=1, source_target_pairs={{0,64},{8,72},{16,80},{24,88},{32,96},{40,104},{48,112},{56,120},{... | collective-permute-start | bytes 393224 | tf_op jit(solution)/shard_map/ppermute | solution.py:40
  94.3 2.9 %fusion.32 = bf16[1024,1024]{1,0:T(8,128)(2,1)S(1)} fusion(f32[1024,1024]{0,1:T(8,128)S(1)} %copy-done.28, s32[1024]{0:T(1024)S(1)} %fusion.95, f32[]{:T(128)} %bitcast.343, pred[]{:T(512)S(6)} %ge.27, s32[1024]{0:T(1024)S(1)} %copy-done.27, bf16[1024,1,128]{0,2,1:T(8,128)(2,1)S(1)} %get-tuple-element.15, bf16[2056,128]{1,0:T(8,128)(2,1)S(1)} %copy-done.24), kind=kOutput, calls=%fused_computation.43 | convolution fusion | flops 284164096 | bytes 6823941 | tf_op jit(solution)/shard_map/ihd,jhd->hij/dot_general | solution.py:160
  99.7 3.5 %collective-permute-start.10 = (bf16[2,1024,128]{2,1,0:T(8,128)(2,1)S(1)}, bf16[2,1024,128]{2,1,0:T(8,128)(2,1)S(1)}, u32[]{:S(2)}, u32[]{:S(2)}) collective-permute-start(bf16[2,1024,128]{2,1,0:T(8,128)(2,1)S(1)} %pad_maximum_fusion.1), channel_id=1, source_target_pairs={{8,0},{16,8},{24,16},{32,24},{40,32},{48,40},{56,48},{64,56},{72,6... | collective-permute-start | bytes 1572872 | tf_op jit(solution)/shard_map/ppermute | solution.py:19
  105.2 2.9 %fusion.21 = bf16[1024,1024]{1,0:T(8,128)(2,1)S(1)} fusion(f32[1024,1024]{0,1:T(8,128)S(1)} %copy-done.13, s32[1024]{0:T(1024)S(1)} %fusion.94, f32[]{:T(128)} %bitcast.347, pred[]{:T(512)S(6)} %ge.28, s32[1024]{0:T(1024)S(1)} %copy-done.27, bf16[1024,1,128]{0,2,1:T(8,128)(2,1)S(1)} %get-tuple-element.15, bf16[2056,128]{1,0:T(8,128)(2,1)S(1)} %copy-done.20), kind=kOutput, calls=%fused_computation.29 | convolution fusion | flops 284164096 | bytes 6823941 | tf_op jit(solution)/shard_map/ihd,jhd->hij/dot_general | solution.py:160
  109.0 1.8 %collective-permute-start.11 = (bf16[2,1024,128]{2,1,0:T(8,128)(2,1)S(1)}, bf16[2,1024,128]{2,1,0:T(8,128)(2,1)S(1)}, u32[]{:S(2)}, u32[]{:S(2)}) collective-permute-start(bf16[2,1024,128]{2,1,0:T(8,128)(2,1)S(1)} %pad_maximum_fusion.2), channel_id=1, source_target_pairs={{16,0},{24,8},{32,16},{40,24},{48,32},{56,40},{64,48},{72,56},{80,... | collective-permute-start | bytes 1572872 | tf_op jit(solution)/shard_map/ppermute | solution.py:19
  111.6 8.0 %collective-permute-start.13 = (f32[128,2,32]{0,2,1:T(8,128)S(1)}, f32[128,2,32]{0,2,1:T(8,128)S(1)}, u32[]{:S(2)}, u32[]{:S(2)}) collective-permute-start(f32[128,2,32]{0,2,1:T(8,128)S(1)} %select_bitcast_fusion.3), channel_id=1, source_target_pairs={{0,16},{8,24},{16,0},{24,8},{32,48},{40,56},{48,32},{56,40},{64,80... | collective-permute-start | bytes 98312 | tf_op jit(solution)/shard_map/ppermute | solution.py:40
  120.5 2.9 %fusion.10 = bf16[1024,1024]{1,0:T(8,128)(2,1)S(1)} fusion(f32[1024,1024]{0,1:T(8,128)S(1)} %copy-done.11, s32[1024]{0:T(1024)S(1)} %fusion.93, f32[]{:T(128)} %bitcast.346, pred[]{:T(512)S(6)} %ge.29, s32[1024]{0:T(1024)S(1)} %copy-done.27, bf16[1024,1,128]{0,2,1:T(8,128)(2,1)S(1)} %get-tuple-element.15, bf16[2056,128]{1,0:T(8,128)(2,1)S(1)} %copy-done.18), kind=kOutput, calls=%fused_computation.15 | convolution fusion | flops 284164096 | bytes 6823941 | tf_op jit(solution)/shard_map/ihd,jhd->hij/dot_general | solution.py:160
  126.4 6.0 %collective-permute-done.13 = f32[128,2,32]{0,2,1:T(8,128)S(1)} collective-permute-done((f32[128,2,32]{0,2,1:T(8,128)S(1)}, f32[128,2,32]{0,2,1:T(8,128)S(1)}, u32[]{:S(2)}, u32[]{:S(2)}) %collective-permute-start.13) | collective-permute-done | bytes 32800 | tf_op jit(solution)/shard_map/ppermute | solution.py:40
  135.7 7.4 %collective-permute-done.12 = bf16[2,1024,128]{2,1,0:T(8,128)(2,1)S(1)} collective-permute-done((bf16[2,1024,128]{2,1,0:T(8,128)(2,1)S(1)}, bf16[2,1024,128]{2,1,0:T(8,128)(2,1)S(1)}, u32[]{:S(2)}, u32[]{:S(2)}) %collective-permute-start.12) | collective-permute-done | bytes 524320 | tf_op jit(solution)/shard_map/ppermute | solution.py:19
  (139 shorter events, 34.8 us)
Async XLA Ops:
  0.6 15.9 %copy-start = (bf16[1024,128]{1,0:T(8,128)(2,1)S(1)}, bf16[1024,128]{1,0:T(8,128)(2,1)}, u32[]{:S(2)}) copy-start(bf16[1024,128]{1,0:T(8,128)(2,1)} %param.8) | copy-start | bytes 786436
  0.6 20.4 %copy-start.25 = (bf16[128,1024]{1,0:T(8,128)(2,1)S(1)}, bf16[128,1024]{1,0:T(8,128)(2,1)}, u32[]{:S(2)}) copy-start(bf16[128,1024]{1,0:T(8,128)(2,1)} %param.15) | copy-start | bytes 786436
  0.7 21.5 %copy-start.26 = (bf16[1024,128]{1,0:T(8,128)(2,1)S(1)}, bf16[1024,128]{1,0:T(8,128)(2,1)}, u32[]{:S(2)}) copy-start(bf16[1024,128]{1,0:T(8,128)(2,1)} %param.11) | copy-start | bytes 786436
  2.5 41.0 %collective-permute-start.6 = (bf16[2056,128]{1,0:T(8,128)(2,1)S(1)}, bf16[2056,128]{1,0:T(8,128)(2,1)S(1)}, u32[]{:S(2)}, u32[]{:S(2)}) collective-permute-start(bf16[2056,128]{1,0:T(8,128)(2,1)S(1)} %pad_maximum_fusion), channel_id=1, source_target_pairs={{0,24},{8,32},{16,40},{24,48},{32,56},{40,64},{48,72},{56,80},{64,... | collective-permute-start | bytes 1579016 | tf_op jit(solution)/shard_map/ppermute | solution.py:19
  7.5 37.3 %collective-permute-start.5 = (bf16[2056,128]{1,0:T(8,128)(2,1)S(1)}, bf16[2056,128]{1,0:T(8,128)(2,1)S(1)}, u32[]{:S(2)}, u32[]{:S(2)}) collective-permute-start(bf16[2056,128]{1,0:T(8,128)(2,1)S(1)} %pad_maximum_fusion), channel_id=1, source_target_pairs={{0,16},{8,24},{16,32},{24,40},{32,48},{40,56},{48,64},{56,72},{64,... | collective-permute-start | bytes 1579016 | tf_op jit(solution)/shard_map/ppermute | solution.py:19
  10.7 34.9 %collective-permute-start.4 = (bf16[2056,128]{1,0:T(8,128)(2,1)S(1)}, bf16[2056,128]{1,0:T(8,128)(2,1)S(1)}, u32[]{:S(2)}, u32[]{:S(2)}) collective-permute-start(bf16[2056,128]{1,0:T(8,128)(2,1)S(1)} %pad_maximum_fusion), channel_id=1, source_target_pairs={{0,8},{8,16},{16,24},{24,32},{32,40},{40,48},{48,56},{56,64},{64,7... | collective-permute-start | bytes 1579016 | tf_op jit(solution)/shard_map/ppermute | solution.py:19
  13.7 25.2 %collective-permute-start = (bf16[1024,128]{1,0:T(8,128)(2,1)}, bf16[1024,128]{1,0:T(8,128)(2,1)}, u32[]{:S(2)}, u32[]{:S(2)}) collective-permute-start(bf16[1024,128]{1,0:T(8,128)(2,1)} %param.14), channel_id=1, source_target_pairs={{0,1},{1,0},{2,3},{3,2},{4,5},{5,4},{6,7},{7,6},{8,9},{9,8},{10,11... | collective-permute-start | bytes 786440 | tf_op jit(solution)/shard_map/ppermute | solution.py:94
  40.4 23.1 %collective-permute-start.3 = (bf16[1024,256]{1,0:T(8,128)(2,1)S(1)}, bf16[1024,256]{1,0:T(8,128)(2,1)S(1)}, u32[]{:S(2)}, u32[]{:S(2)}) collective-permute-start(bf16[1024,256]{1,0:T(8,128)(2,1)S(1)} %maximum_select_fusion), channel_id=1, source_target_pairs={{0,6},{1,7},{2,0},{3,1},{4,2},{5,3},{6,4},{7,5},{8,14},{9,15},{10,... | collective-permute-start | bytes 1572872 | tf_op jit(solution)/shard_map/ppermute | solution.py:104
  42.9 20.9 %collective-permute-start.2 = (bf16[1024,256]{1,0:T(8,128)(2,1)S(1)}, bf16[1024,256]{1,0:T(8,128)(2,1)S(1)}, u32[]{:S(2)}, u32[]{:S(2)}) collective-permute-start(bf16[1024,256]{1,0:T(8,128)(2,1)S(1)} %maximum_select_fusion), channel_id=1, source_target_pairs={{0,4},{1,5},{2,6},{3,7},{4,0},{5,1},{6,2},{7,3},{8,12},{9,13},{10,... | collective-permute-start | bytes 1572872 | tf_op jit(solution)/shard_map/ppermute | solution.py:104
  43.5 14.9 %copy-start.17 = (bf16[2056,128]{1,0:T(8,128)(2,1)}, bf16[2056,128]{1,0:T(8,128)(2,1)S(1)}, u32[]{:S(2)}) copy-start(bf16[2056,128]{1,0:T(8,128)(2,1)S(1)} %collective-permute-done.6) | copy-start | bytes 1579012
  43.5 23.9 %collective-permute-start.1 = (bf16[1024,256]{1,0:T(8,128)(2,1)S(1)}, bf16[1024,256]{1,0:T(8,128)(2,1)S(1)}, u32[]{:S(2)}, u32[]{:S(2)}) collective-permute-start(bf16[1024,256]{1,0:T(8,128)(2,1)S(1)} %maximum_select_fusion), channel_id=1, source_target_pairs={{0,2},{1,3},{2,4},{3,5},{4,6},{5,7},{6,0},{7,1},{8,10},{9,11},{10,... | collective-permute-start | bytes 1572872 | tf_op jit(solution)/shard_map/ppermute | solution.py:104
  44.8 11.9 %copy-start.10 = (f32[1024,1024]{0,1:T(8,128)}, f32[1024,1024]{0,1:T(8,128)S(1)}, u32[]{:S(2)}) copy-start(f32[1024,1024]{0,1:T(8,128)S(1)} %fusion.68) | copy-start | bytes 12582916
  44.8 12.7 %copy-start.19 = (bf16[2056,128]{1,0:T(8,128)(2,1)}, bf16[2056,128]{1,0:T(8,128)(2,1)S(1)}, u32[]{:S(2)}) copy-start(bf16[2056,128]{1,0:T(8,128)(2,1)S(1)} %collective-permute-done.5) | copy-start | bytes 1579012
  45.6 13.7 %copy-start.23 = (bf16[2056,128]{1,0:T(8,128)(2,1)}, bf16[2056,128]{1,0:T(8,128)(2,1)S(1)}, u32[]{:S(2)}) copy-start(bf16[2056,128]{1,0:T(8,128)(2,1)S(1)} %collective-permute-done.4) | copy-start | bytes 1579012
  71.9 19.0 %collective-permute-start.7 = (f32[128,2,2,2,2,32]{0,5,4,3,2,1:T(8,128)}, f32[128,2,2,2,2,32]{0,5,4,3,2,1:T(8,128)}, u32[]{:S(2)}, u32[]{:S(2)}) collective-permute-start(f32[128,2,2,2,2,32]{0,5,4,3,2,1:T(8,128)} %select_bitcast_fusion), channel_id=1, source_target_pairs={{0,128},{8,136},{16,144},{24,152},{32,160},{40,168},{48,176},{56,1... | collective-permute-start | bytes 786440 | tf_op jit(solution)/shard_map/ppermute | solution.py:40
  92.3 10.9 %collective-permute-start.8 = (f32[128,2,2,2,32]{0,4,3,2,1:T(8,128)S(1)}, f32[128,2,2,2,32]{0,4,3,2,1:T(8,128)S(1)}, u32[]{:S(2)}, u32[]{:S(2)}) collective-permute-start(f32[128,2,2,2,32]{0,4,3,2,1:T(8,128)S(1)} %select_bitcast_fusion.1), channel_id=1, source_target_pairs={{0,64},{8,72},{16,80},{24,88},{32,96},{40,104},{48,112},{56,120},{... | collective-permute-start | bytes 393224 | tf_op jit(solution)/shard_map/ppermute | solution.py:40
  99.7 36.0 %collective-permute-start.10 = (bf16[2,1024,128]{2,1,0:T(8,128)(2,1)S(1)}, bf16[2,1024,128]{2,1,0:T(8,128)(2,1)S(1)}, u32[]{:S(2)}, u32[]{:S(2)}) collective-permute-start(bf16[2,1024,128]{2,1,0:T(8,128)(2,1)S(1)} %pad_maximum_fusion.1), channel_id=1, source_target_pairs={{8,0},{16,8},{24,16},{32,24},{40,32},{48,40},{56,48},{64,56},{72,6... | collective-permute-start | bytes 1572872 | tf_op jit(solution)/shard_map/ppermute | solution.py:19
  103.3 8.3 %collective-permute-start.9 = (f32[128,2,2,32]{0,3,2,1:T(8,128)S(1)}, f32[128,2,2,32]{0,3,2,1:T(8,128)S(1)}, u32[]{:S(2)}, u32[]{:S(2)}) collective-permute-start(f32[128,2,2,32]{0,3,2,1:T(8,128)S(1)} %select_bitcast_fusion.2), channel_id=1, source_target_pairs={{0,32},{8,40},{16,48},{24,56},{32,0},{40,8},{48,16},{56,24},{64,96... | collective-permute-start | bytes 196616 | tf_op jit(solution)/shard_map/ppermute | solution.py:40
  108.9 11.6 %copy-start.11 = (f32[1024,1024]{0,1:T(8,128)S(1)}, f32[1024,1024]{0,1:T(8,128)}, u32[]{:S(2)}) copy-start(f32[1024,1024]{0,1:T(8,128)} %copy-done.10) | copy-start | bytes 12582916
  109.0 26.7 %collective-permute-start.11 = (bf16[2,1024,128]{2,1,0:T(8,128)(2,1)S(1)}, bf16[2,1024,128]{2,1,0:T(8,128)(2,1)S(1)}, u32[]{:S(2)}, u32[]{:S(2)}) collective-permute-start(bf16[2,1024,128]{2,1,0:T(8,128)(2,1)S(1)} %pad_maximum_fusion.2), channel_id=1, source_target_pairs={{16,0},{24,8},{32,16},{40,24},{48,32},{56,40},{64,48},{72,56},{80,... | collective-permute-start | bytes 1572872 | tf_op jit(solution)/shard_map/ppermute | solution.py:19
  111.6 20.9 %collective-permute-start.13 = (f32[128,2,32]{0,2,1:T(8,128)S(1)}, f32[128,2,32]{0,2,1:T(8,128)S(1)}, u32[]{:S(2)}, u32[]{:S(2)}) collective-permute-start(f32[128,2,32]{0,2,1:T(8,128)S(1)} %select_bitcast_fusion.3), channel_id=1, source_target_pairs={{0,16},{8,24},{16,0},{24,8},{32,48},{40,56},{48,32},{56,40},{64,80... | collective-permute-start | bytes 98312 | tf_op jit(solution)/shard_map/ppermute | solution.py:40
  124.2 18.9 %copy-start.15 = (f32[1,1024,128]{2,1,0:T(8,128)S(1)}, f32[1,1024,128]{2,1,0:T(8,128)}, u32[]{:S(2)}) copy-start(f32[1,1024,128]{2,1,0:T(8,128)} %convolution_bitcast_fusion) | copy-start | bytes 1572868
  124.3 18.8 %collective-permute-start.12 = (bf16[2,1024,128]{2,1,0:T(8,128)(2,1)S(1)}, bf16[2,1024,128]{2,1,0:T(8,128)(2,1)S(1)}, u32[]{:S(2)}, u32[]{:S(2)}) collective-permute-start(bf16[2,1024,128]{2,1,0:T(8,128)(2,1)S(1)} %pad_maximum_fusion.3), channel_id=1, source_target_pairs={{24,0},{32,8},{40,16},{48,24},{56,32},{64,40},{72,48},{80,56},{88,... | collective-permute-start | bytes 1572872 | tf_op jit(solution)/shard_map/ppermute | solution.py:19
  132.5 2.6 %collective-permute-start.14 = (f32[128,32]{0,1:T(8,128)S(1)}, f32[128,32]{0,1:T(8,128)S(1)}, u32[]{:S(2)}, u32[]{:S(2)}) collective-permute-start(f32[128,32]{0,1:T(8,128)S(1)} %select_bitcast_fusion.4), channel_id=1, source_target_pairs={{0,8},{8,0},{16,24},{24,16},{32,40},{40,32},{48,56},{56,48},{64,72... | collective-permute-start | bytes 49160 | tf_op jit(solution)/shard_map/ppermute | solution.py:40
  (20 other events, 123.5 us)

commit v10 on v9

--- a/solution.py
+++ b/solution.py
@@ -30,8 +30,10 @@
     count = lax.axis_size(axis)
     my_index = lax.axis_index(axis)
     levels = count.bit_length() - 1
-    bit = 1 << (levels - 1 - level)
-    axis_pos = 1
+    order = [0] + list(range(levels - 1, 0, -1))
+    bit = 1 << order[level]
+    remaining = sorted(order[level:], reverse=True)
+    axis_pos = 1 + remaining.index(order[level])
     mine = (my_index // bit) % 2
     low = lax.index_in_dim(current, 0, axis_pos, keepdims=False)
     high = lax.index_in_dim(current, 1, axis_pos, keepdims=False)
@@ -147,6 +149,8 @@
     done_levels = 0
     for window_index in range(4):
         if window_index > 0 and done_levels < halving_levels:
+            if done_levels == 1:
+                halving, grad_queries = lax.optimization_barrier((halving, grad_queries))
             halving = halving_step(halving, "seq", done_levels)
             done_levels += 1
             halving, grad_attended = lax.optimization_barrier((halving, grad_attended))

time: 145 us -> 147 us (1.014)
  waiting for transfers between devices: 35.6 us -> 37.6 us
    ppermute x5, waiting for transfers between devices: 6.06 us -> 8.96 us  [halving_step(): return keep + lax.ppermute(send, axis, [(i, i ^ bit) for i in range(count)])]
    ppermute x5, starting transfers between devices: 19.8 us -> 21.8 us  [halving_step(): return keep + lax.ppermute(send, axis, [(i, i ^ bit) for i in range(count)])]
    ppermute x6, starting transfers between devices: 17.9 us -> 16.4 us  [shifted(): return lax.ppermute(block, axis, route)]
  transfers between devices with their start and end apart: 15 -> 15, of which waited for: 5 -> 7; matrix products, arithmetic and copies ran while one was open for 35% -> 31% of each run, Pallas kernels for 0% -> 0%
where the time goes in v10:
time: 147 us
  matrix products  45.6 us (31%)
  starting transfers between devices  44.6 us (30%)
  waiting for transfers between devices  37.6 us (26%)
  local copies, waits for them, and re-layouts  8.5 us (6%)
  other arithmetic  8.08 us (5%)
  between operations  2.18 us (1%)
    ppermute x5, starting transfers between devices, halving_step(): return keep + lax.ppermute(send, axis, [(i, i ^ bit) for i in range(count)])  21.8 us
    ppermute x6, starting transfers between devices, shifted(): return lax.ppermute(block, axis, route)  16.4 us
    ppermute x1, waiting for transfers between devices, per_device(): lax.ppermute(grad_out, 'head', [(i, i ^ 1) for i in range(head_devices)])  16.3 us
    dot_general x4, matrix products, pair_scores(): jnp.einsum('ihd,jhd->hij', query_heads, k_heads, preferred_element_type=j...  14.2 us
    dot_general x4, matrix products, per_device(): jnp.einsum('ihd,jhd->hij', grad_attended, v_heads, preferred_element_type...  13.7 us
    ppermute x5, waiting for transfers between devices, halving_step(): return keep + lax.ppermute(send, axis, [(i, i ^ bit) for i in range(count)])  8.96 us
    ppermute x6, waiting for transfers between devices, shifted(): return lax.ppermute(block, axis, route)  6.44 us
    ppermute x3, waiting for transfers between devices, per_device(): lax.ppermute(pair_block, 'head', [(i, (i + 2 * k) % head_devices) for i i...  5.87 us
  transfers between devices with their start and end apart: 15, of which 7 were waited for; matrix products, arithmetic and copies ran while one was open for 31% of the time, Pallas kernels for 0%

profile of v10, /device:TPU:1, one launch (start us, length us, event | category | flops | bytes accessed | tf_op | source)
XLA Modules:
  0.0 146.5 jit_solution(12211417540794445612)
XLA Ops:
  2.5 5.0 %collective-permute-start.2 = (bf16[2056,128]{1,0:T(8,128)(2,1)S(1)}, bf16[2056,128]{1,0:T(8,128)(2,1)S(1)}, u32[]{:S(2)}, u32[]{:S(2)}) collective-permute-start(bf16[2056,128]{1,0:T(8,128)(2,1)S(1)} %pad_maximum_fusion), channel_id=1, source_target_pairs={{0,24},{8,32},{16,40},{24,48},{32,56},{40,64},{48,72},{56,80},{64,... | collective-permute-start | bytes 1579016 | tf_op jit(solution)/shard_map/ppermute | solution.py:19
  7.5 3.2 %collective-permute-start.1 = (bf16[2056,128]{1,0:T(8,128)(2,1)S(1)}, bf16[2056,128]{1,0:T(8,128)(2,1)S(1)}, u32[]{:S(2)}, u32[]{:S(2)}) collective-permute-start(bf16[2056,128]{1,0:T(8,128)(2,1)S(1)} %pad_maximum_fusion), channel_id=1, source_target_pairs={{0,16},{8,24},{16,32},{24,40},{32,48},{40,56},{48,64},{56,72},{64,... | collective-permute-start | bytes 1579016 | tf_op jit(solution)/shard_map/ppermute | solution.py:19
  10.7 3.1 %collective-permute-start = (bf16[2056,128]{1,0:T(8,128)(2,1)S(1)}, bf16[2056,128]{1,0:T(8,128)(2,1)S(1)}, u32[]{:S(2)}, u32[]{:S(2)}) collective-permute-start(bf16[2056,128]{1,0:T(8,128)(2,1)S(1)} %pad_maximum_fusion), channel_id=1, source_target_pairs={{0,8},{8,16},{16,24},{24,32},{32,40},{40,48},{48,56},{56,64},{64,7... | collective-permute-start | bytes 1579016 | tf_op jit(solution)/shard_map/ppermute | solution.py:19
  13.7 2.7 %collective-permute-start.3 = (bf16[1024,128]{1,0:T(8,128)(2,1)}, bf16[1024,128]{1,0:T(8,128)(2,1)}, u32[]{:S(2)}, u32[]{:S(2)}) collective-permute-start(bf16[1024,128]{1,0:T(8,128)(2,1)} %param.14), channel_id=1, source_target_pairs={{0,1},{1,0},{2,3},{3,2},{4,5},{5,4},{6,7},{7,6},{8,9},{9,8},{10,11... | collective-permute-start | bytes 786440 | tf_op jit(solution)/shard_map/ppermute | solution.py:96
  16.5 3.7 %fusion.105 = f32[1024,1024]{1,0:T(8,128)} fusion(bf16[1024,128]{1,0:T(8,128)(2,1)S(1)} %copy-done, bf16[1024,128]{1,0:T(8,128)(2,1)} %param.9), kind=kOutput, calls=%fused_computation.208 | convolution fusion | flops 268435456 | bytes 4718592 | tf_op jit(solution)/shard_map/ihd,jhd->hij/dot_general | solution.py:79
  22.6 16.3 %collective-permute-done.3 = bf16[1024,128]{1,0:T(8,128)(2,1)} collective-permute-done((bf16[1024,128]{1,0:T(8,128)(2,1)}, bf16[1024,128]{1,0:T(8,128)(2,1)}, u32[]{:S(2)}, u32[]{:S(2)}) %collective-permute-start.3) | collective-permute-done | bytes 262176 | tf_op jit(solution)/shard_map/ppermute | solution.py:96
  40.4 2.6 %collective-permute-start.6 = (bf16[1024,256]{1,0:T(8,128)(2,1)S(1)}, bf16[1024,256]{1,0:T(8,128)(2,1)S(1)}, u32[]{:S(2)}, u32[]{:S(2)}) collective-permute-start(bf16[1024,256]{1,0:T(8,128)(2,1)S(1)} %maximum_select_fusion), channel_id=1, source_target_pairs={{0,6},{1,7},{2,0},{3,1},{4,2},{5,3},{6,4},{7,5},{8,14},{9,15},{10,... | collective-permute-start | bytes 1572872 | tf_op jit(solution)/shard_map/ppermute | solution.py:106
  45.6 2.0 %copy-done.9 = f32[1024,1024]{1,0:T(8,128)S(1)} copy-done((f32[1024,1024]{1,0:T(8,128)S(1)}, f32[1024,1024]{1,0:T(8,128)}, u32[]{:S(2)}) %copy-start.9) | copy-done | bytes 4194328
  47.5 9.1 %fusion.26 = (bf16[1024,1024]{1,0:T(8,128)(2,1)S(1)}, bf16[1024,1024]{1,0:T(8,128)(2,1)S(1)}, bf16[1024,1024]{1,0:T(8,128)(2,1)S(1)}, bf16[1024,1024]{1,0:T(8,128)(2,1)S(1)}, f32[1024,1024]{0,1:T(8,128)}) fusion(s32[1024]{0:T(1024)S(1)} %fusion.94, f32[]{:T(128)} %bitcast.369, pred[]{:T(512)S(6)} %ge.27, s32[1024]{0:T(1024)S(1)} %copy-done.27, ...), kind=kOutput, calls=%fused_computation.37 | convolution fusion | flops 312475648 | bytes 25711620 | tf_op jit(solution)/shard_map/ihd,jhd->hij/dot_general | solution.py:79
  60.9 2.6 %collective-permute-done.6 = bf16[1024,256]{1,0:T(8,128)(2,1)S(1)} collective-permute-done((bf16[1024,256]{1,0:T(8,128)(2,1)S(1)}, bf16[1024,256]{1,0:T(8,128)(2,1)S(1)}, u32[]{:S(2)}, u32[]{:S(2)}) %collective-permute-start.6) | collective-permute-done | bytes 524320 | tf_op jit(solution)/shard_map/ppermute | solution.py:106
  64.2 3.3 %collective-permute-done.4 = bf16[1024,256]{1,0:T(8,128)(2,1)S(1)} collective-permute-done((bf16[1024,256]{1,0:T(8,128)(2,1)S(1)}, bf16[1024,256]{1,0:T(8,128)(2,1)S(1)}, u32[]{:S(2)}, u32[]{:S(2)}) %collective-permute-start.4) | collective-permute-done | bytes 524320 | tf_op jit(solution)/shard_map/ppermute | solution.py:106
  72.3 5.1 %select_convert_fusion = bf16[1024,1024]{1,0:T(8,128)(2,1)S(1)} fusion(f32[1024,1024]{1,0:T(8,128)} %fusion.105, bf16[1024,128]{1,0:T(8,128)(2,1)S(1)} %copy-done.22, f32[]{:T(128)} %bitcast.368, s32[1024]{0:T(1024)S(1)} %copy-done.27, pred[]{:T(512)S(6)} %ge.26, bf16[1024,1,128]{0,2,1:T(8,128)(2,1)S(1)} %get-tuple-element.19), kind=kOutput, calls=%fused_computation.44 | convolution fusion | flops 286261248 | bytes 6819845 | tf_op jit(solution)/shard_map/ihd,jhd->hij/dot_general | solution.py:164
  78.9 1.8 %convolution_bitcast_fusion.2 = f32[1,1024,128]{2,1,0:T(8,128)} fusion(bf16[1024,1024]{1,0:T(8,128)(2,1)S(1)} %copy-done.8, bf16[1024,1,128]{0,2,1:T(8,128)(2,1)S(1)} %get-tuple-element.19), kind=kOutput, calls=%fused_computation.58 | convolution fusion | flops 268435456 | bytes 2883584 | tf_op jit(solution)/shard_map/hij,ihd->jhd/dot_general | solution.py:161
  80.7 2.0 %copy.79 = f32[1024,128]{1,0:T(8,128)} copy(f32[1024,128]{0,1:T(8,128)} %get-tuple-element.36) | data formatting | bytes 1048576
  85.1 2.9 %fusion.32 = bf16[1024,1024]{1,0:T(8,128)(2,1)S(1)} fusion(f32[1024,1024]{0,1:T(8,128)S(1)} %copy-done.28, s32[1024]{0:T(1024)S(1)} %fusion.94, f32[]{:T(128)} %bitcast.367, pred[]{:T(512)S(6)} %ge.27, s32[1024]{0:T(1024)S(1)} %copy-done.27, bf16[1024,1,128]{0,2,1:T(8,128)(2,1)S(1)} %get-tuple-element.19, bf16[2056,128]{1,0:T(8,128)(2,1)S(1)} %copy-done.24), kind=kOutput, calls=%fused_computation.43 | convolution fusion | flops 284164096 | bytes 6823941 | tf_op jit(solution)/shard_map/ihd,jhd->hij/dot_general | solution.py:164
  89.8 7.9 %collective-permute-start.8 = (f32[128,2,2,2,32]{0,4,3,2,1:T(8,128)S(1)}, f32[128,2,2,2,32]{0,4,3,2,1:T(8,128)S(1)}, u32[]{:S(2)}, u32[]{:S(2)}) collective-permute-start(f32[128,2,2,2,32]{0,4,3,2,1:T(8,128)S(1)} %select_bitcast_fusion.1), channel_id=1, source_target_pairs={{0,128},{8,136},{16,144},{24,152},{32,160},{40,168},{48,176},{56,1... | collective-permute-start | bytes 393224 | tf_op jit(solution)/shard_map/ppermute | solution.py:42
  98.7 2.3 %collective-permute-start.10 = (bf16[2,1024,128]{2,1,0:T(8,128)(2,1)S(1)}, bf16[2,1024,128]{2,1,0:T(8,128)(2,1)S(1)}, u32[]{:S(2)}, u32[]{:S(2)}) collective-permute-start(bf16[2,1024,128]{2,1,0:T(8,128)(2,1)S(1)} %pad_maximum_fusion.1), channel_id=1, source_target_pairs={{8,0},{16,8},{24,16},{32,24},{40,32},{48,40},{56,48},{64,56},{72,6... | collective-permute-start | bytes 1572872 | tf_op jit(solution)/shard_map/ppermute | solution.py:19
  101.5 4.3 %collective-permute-start.9 = (f32[128,2,2,32]{0,3,2,1:T(8,128)S(1)}, f32[128,2,2,32]{0,3,2,1:T(8,128)S(1)}, u32[]{:S(2)}, u32[]{:S(2)}) collective-permute-start(f32[128,2,2,32]{0,3,2,1:T(8,128)S(1)} %select_bitcast_fusion.2), channel_id=1, source_target_pairs={{0,64},{8,72},{16,80},{24,88},{32,96},{40,104},{48,112},{56,120},{... | collective-permute-start | bytes 196616 | tf_op jit(solution)/shard_map/ppermute | solution.py:42
  106.8 2.9 %fusion.21 = bf16[1024,1024]{1,0:T(8,128)(2,1)S(1)} fusion(f32[1024,1024]{0,1:T(8,128)S(1)} %copy-done.13, s32[1024]{0:T(1024)S(1)} %fusion.93, f32[]{:T(128)} %bitcast.371, pred[]{:T(512)S(6)} %ge.28, s32[1024]{0:T(1024)S(1)} %copy-done.27, bf16[1024,1,128]{0,2,1:T(8,128)(2,1)S(1)} %get-tuple-element.19, bf16[2056,128]{1,0:T(8,128)(2,1)S(1)} %copy-done.18), kind=kOutput, calls=%fused_computation.29 | convolution fusion | flops 284164096 | bytes 6823941 | tf_op jit(solution)/shard_map/ihd,jhd->hij/dot_general | solution.py:164
  112.9 9.1 %collective-permute-start.13 = (f32[128,2,32]{0,2,1:T(8,128)S(1)}, f32[128,2,32]{0,2,1:T(8,128)S(1)}, u32[]{:S(2)}, u32[]{:S(2)}) collective-permute-start(f32[128,2,32]{0,2,1:T(8,128)S(1)} %select_bitcast_fusion.3), channel_id=1, source_target_pairs={{0,32},{8,40},{16,48},{24,56},{32,0},{40,8},{48,16},{56,24},{64,96... | collective-permute-start | bytes 98312 | tf_op jit(solution)/shard_map/ppermute | solution.py:42
  123.0 2.9 %fusion.10 = bf16[1024,1024]{1,0:T(8,128)(2,1)S(1)} fusion(f32[1024,1024]{0,1:T(8,128)S(1)} %copy-done.11, s32[1024]{0:T(1024)S(1)} %fusion.92, f32[]{:T(128)} %bitcast.370, pred[]{:T(512)S(6)} %ge.29, s32[1024]{0:T(1024)S(1)} %copy-done.27, bf16[1024,1,128]{0,2,1:T(8,128)(2,1)S(1)} %get-tuple-element.19, bf16[2056,128]{1,0:T(8,128)(2,1)S(1)} %copy-done.20), kind=kOutput, calls=%fused_computation.15 | convolution fusion | flops 284164096 | bytes 6823941 | tf_op jit(solution)/shard_map/ihd,jhd->hij/dot_general | solution.py:164
  128.1 5.0 %collective-permute-done.13 = f32[128,2,32]{0,2,1:T(8,128)S(1)} collective-permute-done((f32[128,2,32]{0,2,1:T(8,128)S(1)}, f32[128,2,32]{0,2,1:T(8,128)S(1)}, u32[]{:S(2)}, u32[]{:S(2)}) %collective-permute-start.13) | collective-permute-done | bytes 32800 | tf_op jit(solution)/shard_map/ppermute | solution.py:42
  134.7 3.5 %collective-permute-done.14 = f32[128,32]{0,1:T(8,128)S(1)} collective-permute-done((f32[128,32]{0,1:T(8,128)S(1)}, f32[128,32]{0,1:T(8,128)S(1)}, u32[]{:S(2)}, u32[]{:S(2)}) %collective-permute-start.14) | collective-permute-done | bytes 16416 | tf_op jit(solution)/shard_map/ppermute | solution.py:42
  138.9 6.4 %collective-permute-done.12 = bf16[2,1024,128]{2,1,0:T(8,128)(2,1)S(1)} collective-permute-done((bf16[2,1024,128]{2,1,0:T(8,128)(2,1)S(1)}, bf16[2,1024,128]{2,1,0:T(8,128)(2,1)S(1)}, u32[]{:S(2)}, u32[]{:S(2)}) %collective-permute-start.12) | collective-permute-done | bytes 524320 | tf_op jit(solution)/shard_map/ppermute | solution.py:19
  (139 shorter events, 34.9 us)
Async XLA Ops:
  0.6 15.9 %copy-start = (bf16[1024,128]{1,0:T(8,128)(2,1)S(1)}, bf16[1024,128]{1,0:T(8,128)(2,1)}, u32[]{:S(2)}) copy-start(bf16[1024,128]{1,0:T(8,128)(2,1)} %param.8) | copy-start | bytes 786436
  0.6 20.4 %copy-start.25 = (bf16[128,1024]{1,0:T(8,128)(2,1)S(1)}, bf16[128,1024]{1,0:T(8,128)(2,1)}, u32[]{:S(2)}) copy-start(bf16[128,1024]{1,0:T(8,128)(2,1)} %param.15) | copy-start | bytes 786436
  0.7 21.5 %copy-start.26 = (bf16[1024,128]{1,0:T(8,128)(2,1)S(1)}, bf16[1024,128]{1,0:T(8,128)(2,1)}, u32[]{:S(2)}) copy-start(bf16[1024,128]{1,0:T(8,128)(2,1)} %param.11) | copy-start | bytes 786436
  2.5 41.0 %collective-permute-start.2 = (bf16[2056,128]{1,0:T(8,128)(2,1)S(1)}, bf16[2056,128]{1,0:T(8,128)(2,1)S(1)}, u32[]{:S(2)}, u32[]{:S(2)}) collective-permute-start(bf16[2056,128]{1,0:T(8,128)(2,1)S(1)} %pad_maximum_fusion), channel_id=1, source_target_pairs={{0,24},{8,32},{16,40},{24,48},{32,56},{40,64},{48,72},{56,80},{64,... | collective-permute-start | bytes 1579016 | tf_op jit(solution)/shard_map/ppermute | solution.py:19
  7.5 37.3 %collective-permute-start.1 = (bf16[2056,128]{1,0:T(8,128)(2,1)S(1)}, bf16[2056,128]{1,0:T(8,128)(2,1)S(1)}, u32[]{:S(2)}, u32[]{:S(2)}) collective-permute-start(bf16[2056,128]{1,0:T(8,128)(2,1)S(1)} %pad_maximum_fusion), channel_id=1, source_target_pairs={{0,16},{8,24},{16,32},{24,40},{32,48},{40,56},{48,64},{56,72},{64,... | collective-permute-start | bytes 1579016 | tf_op jit(solution)/shard_map/ppermute | solution.py:19
  10.7 34.9 %collective-permute-start = (bf16[2056,128]{1,0:T(8,128)(2,1)S(1)}, bf16[2056,128]{1,0:T(8,128)(2,1)S(1)}, u32[]{:S(2)}, u32[]{:S(2)}) collective-permute-start(bf16[2056,128]{1,0:T(8,128)(2,1)S(1)} %pad_maximum_fusion), channel_id=1, source_target_pairs={{0,8},{8,16},{16,24},{24,32},{32,40},{40,48},{48,56},{56,64},{64,7... | collective-permute-start | bytes 1579016 | tf_op jit(solution)/shard_map/ppermute | solution.py:19
  13.7 25.2 %collective-permute-start.3 = (bf16[1024,128]{1,0:T(8,128)(2,1)}, bf16[1024,128]{1,0:T(8,128)(2,1)}, u32[]{:S(2)}, u32[]{:S(2)}) collective-permute-start(bf16[1024,128]{1,0:T(8,128)(2,1)} %param.14), channel_id=1, source_target_pairs={{0,1},{1,0},{2,3},{3,2},{4,5},{5,4},{6,7},{7,6},{8,9},{9,8},{10,11... | collective-permute-start | bytes 786440 | tf_op jit(solution)/shard_map/ppermute | solution.py:96
  40.4 23.1 %collective-permute-start.6 = (bf16[1024,256]{1,0:T(8,128)(2,1)S(1)}, bf16[1024,256]{1,0:T(8,128)(2,1)S(1)}, u32[]{:S(2)}, u32[]{:S(2)}) collective-permute-start(bf16[1024,256]{1,0:T(8,128)(2,1)S(1)} %maximum_select_fusion), channel_id=1, source_target_pairs={{0,6},{1,7},{2,0},{3,1},{4,2},{5,3},{6,4},{7,5},{8,14},{9,15},{10,... | collective-permute-start | bytes 1572872 | tf_op jit(solution)/shard_map/ppermute | solution.py:106
  42.9 20.9 %collective-permute-start.5 = (bf16[1024,256]{1,0:T(8,128)(2,1)S(1)}, bf16[1024,256]{1,0:T(8,128)(2,1)S(1)}, u32[]{:S(2)}, u32[]{:S(2)}) collective-permute-start(bf16[1024,256]{1,0:T(8,128)(2,1)S(1)} %maximum_select_fusion), channel_id=1, source_target_pairs={{0,4},{1,5},{2,6},{3,7},{4,0},{5,1},{6,2},{7,3},{8,12},{9,13},{10,... | collective-permute-start | bytes 1572872 | tf_op jit(solution)/shard_map/ppermute | solution.py:106
  43.5 14.9 %copy-start.19 = (bf16[2056,128]{1,0:T(8,128)(2,1)}, bf16[2056,128]{1,0:T(8,128)(2,1)S(1)}, u32[]{:S(2)}) copy-start(bf16[2056,128]{1,0:T(8,128)(2,1)S(1)} %collective-permute-done.2) | copy-start | bytes 1579012
  43.5 23.9 %collective-permute-start.4 = (bf16[1024,256]{1,0:T(8,128)(2,1)S(1)}, bf16[1024,256]{1,0:T(8,128)(2,1)S(1)}, u32[]{:S(2)}, u32[]{:S(2)}) collective-permute-start(bf16[1024,256]{1,0:T(8,128)(2,1)S(1)} %maximum_select_fusion), channel_id=1, source_target_pairs={{0,2},{1,3},{2,4},{3,5},{4,6},{5,7},{6,0},{7,1},{8,10},{9,11},{10,... | collective-permute-start | bytes 1572872 | tf_op jit(solution)/shard_map/ppermute | solution.py:106
  45.6 13.7 %copy-start.23 = (bf16[2056,128]{1,0:T(8,128)(2,1)}, bf16[2056,128]{1,0:T(8,128)(2,1)S(1)}, u32[]{:S(2)}) copy-start(bf16[2056,128]{1,0:T(8,128)(2,1)S(1)} %collective-permute-done) | copy-start | bytes 1579012
  71.9 11.6 %collective-permute-start.7 = (f32[128,2,2,2,2,32]{0,5,4,3,2,1:T(8,128)}, f32[128,2,2,2,2,32]{0,5,4,3,2,1:T(8,128)}, u32[]{:S(2)}, u32[]{:S(2)}) collective-permute-start(f32[128,2,2,2,2,32]{0,5,4,3,2,1:T(8,128)} %select_bitcast_fusion), channel_id=1, source_target_pairs={{0,8},{8,0},{16,24},{24,16},{32,40},{40,32},{48,56},{56,48},{64,72... | collective-permute-start | bytes 786440 | tf_op jit(solution)/shard_map/ppermute | solution.py:42
  89.0 16.8 %copy-start.6 = (bf16[1024,1024]{1,0:T(8,128)(2,1)S(1)}, bf16[1024,1024]{1,0:T(8,128)(2,1)}, u32[]{:S(2)}) copy-start(bf16[1024,1024]{1,0:T(8,128)(2,1)} %copy-done.5) | copy-start | bytes 6291460
  89.8 17.1 %copy-start.13 = (f32[1024,1024]{0,1:T(8,128)S(1)}, f32[1024,1024]{0,1:T(8,128)}, u32[]{:S(2)}) copy-start(f32[1024,1024]{0,1:T(8,128)} %copy-done.12) | copy-start | bytes 12582916
  89.8 17.1 %copy-start.18 = (bf16[2056,128]{1,0:T(8,128)(2,1)S(1)}, bf16[2056,128]{1,0:T(8,128)(2,1)}, u32[]{:S(2)}) copy-start(bf16[2056,128]{1,0:T(8,128)(2,1)} %copy-done.17) | copy-start | bytes 1579012
  89.8 11.7 %collective-permute-start.8 = (f32[128,2,2,2,32]{0,4,3,2,1:T(8,128)S(1)}, f32[128,2,2,2,32]{0,4,3,2,1:T(8,128)S(1)}, u32[]{:S(2)}, u32[]{:S(2)}) collective-permute-start(f32[128,2,2,2,32]{0,4,3,2,1:T(8,128)S(1)} %select_bitcast_fusion.1), channel_id=1, source_target_pairs={{0,128},{8,136},{16,144},{24,152},{32,160},{40,168},{48,176},{56,1... | collective-permute-start | bytes 393224 | tf_op jit(solution)/shard_map/ppermute | solution.py:42
  98.7 40.1 %collective-permute-start.10 = (bf16[2,1024,128]{2,1,0:T(8,128)(2,1)S(1)}, bf16[2,1024,128]{2,1,0:T(8,128)(2,1)S(1)}, u32[]{:S(2)}, u32[]{:S(2)}) collective-permute-start(bf16[2,1024,128]{2,1,0:T(8,128)(2,1)S(1)} %pad_maximum_fusion.1), channel_id=1, source_target_pairs={{8,0},{16,8},{24,16},{32,24},{40,32},{48,40},{56,48},{64,56},{72,6... | collective-permute-start | bytes 1572872 | tf_op jit(solution)/shard_map/ppermute | solution.py:19
  101.5 11.4 %collective-permute-start.9 = (f32[128,2,2,32]{0,3,2,1:T(8,128)S(1)}, f32[128,2,2,32]{0,3,2,1:T(8,128)S(1)}, u32[]{:S(2)}, u32[]{:S(2)}) collective-permute-start(f32[128,2,2,32]{0,3,2,1:T(8,128)S(1)} %select_bitcast_fusion.2), channel_id=1, source_target_pairs={{0,64},{8,72},{16,80},{24,88},{32,96},{40,104},{48,112},{56,120},{... | collective-permute-start | bytes 196616 | tf_op jit(solution)/shard_map/ppermute | solution.py:42
  110.6 28.2 %collective-permute-start.11 = (bf16[2,1024,128]{2,1,0:T(8,128)(2,1)S(1)}, bf16[2,1024,128]{2,1,0:T(8,128)(2,1)S(1)}, u32[]{:S(2)}, u32[]{:S(2)}) collective-permute-start(bf16[2,1024,128]{2,1,0:T(8,128)(2,1)S(1)} %pad_maximum_fusion.2), channel_id=1, source_target_pairs={{16,0},{24,8},{32,16},{40,24},{48,32},{56,40},{64,48},{72,56},{80,... | collective-permute-start | bytes 1572872 | tf_op jit(solution)/shard_map/ppermute | solution.py:19
  112.9 20.1 %collective-permute-start.13 = (f32[128,2,32]{0,2,1:T(8,128)S(1)}, f32[128,2,32]{0,2,1:T(8,128)S(1)}, u32[]{:S(2)}, u32[]{:S(2)}) collective-permute-start(f32[128,2,32]{0,2,1:T(8,128)S(1)} %select_bitcast_fusion.3), channel_id=1, source_target_pairs={{0,32},{8,40},{16,48},{24,56},{32,0},{40,8},{48,16},{56,24},{64,96... | collective-permute-start | bytes 98312 | tf_op jit(solution)/shard_map/ppermute | solution.py:42
  125.9 19.4 %copy-start.15 = (f32[1,1024,128]{2,1,0:T(8,128)S(1)}, f32[1,1024,128]{2,1,0:T(8,128)}, u32[]{:S(2)}) copy-start(f32[1,1024,128]{2,1,0:T(8,128)} %convolution_bitcast_fusion.2) | copy-start | bytes 1572868
  126.8 18.5 %collective-permute-start.12 = (bf16[2,1024,128]{2,1,0:T(8,128)(2,1)S(1)}, bf16[2,1024,128]{2,1,0:T(8,128)(2,1)S(1)}, u32[]{:S(2)}, u32[]{:S(2)}) collective-permute-start(bf16[2,1024,128]{2,1,0:T(8,128)(2,1)S(1)} %pad_maximum_fusion.3), channel_id=1, source_target_pairs={{24,0},{32,8},{40,16},{48,24},{56,32},{64,40},{72,48},{80,56},{88,... | collective-permute-start | bytes 1572872 | tf_op jit(solution)/shard_map/ppermute | solution.py:19
  133.1 5.1 %collective-permute-start.14 = (f32[128,32]{0,1:T(8,128)S(1)}, f32[128,32]{0,1:T(8,128)S(1)}, u32[]{:S(2)}, u32[]{:S(2)}) collective-permute-start(f32[128,32]{0,1:T(8,128)S(1)} %select_bitcast_fusion.4), channel_id=1, source_target_pairs={{0,16},{8,24},{16,0},{24,8},{32,48},{40,56},{48,32},{56,40},{64,80... | collective-permute-start | bytes 49160 | tf_op jit(solution)/shard_map/ppermute | solution.py:42
  (20 other events, 130.1 us)
